TPU v7x, 256 devices: a whole 4x4x8 slice. The times are simulated.
256 devices in a mesh: win: 32 (over y, z), grp: 8 (over x, core).
Axes of the slice: x: 4, y: 4, z: 8, core: 2. Of those that a mesh axis runs over, the one named last changes fastest.
Arguments:
- points: bfloat16 [32, 8, 512, 512], P('win', 'grp'), may hold values from -6 to 6
- rank: int32 [32, 8, 512], P('win', 'grp'), may hold values from 0 to 16383, as said below
- counts: int32 [8, 32, 8], replicated, may hold values from 1 to 128, 512 in all within a row
- w_qkv_one: bfloat16 [512, 1536], replicated
- w_out_one: bfloat16 [512, 512], replicated, may hold values from -0.25 to 0.25
- w_up: bfloat16 [512, 2048], replicated, may hold values from -0.25 to 0.25
- w_down: bfloat16 [2048, 512], replicated, may hold values from -0.125 to 0.125
- w_qkv_two: bfloat16 [512, 1536], replicated
- w_out_two: bfloat16 [512, 512], replicated, may hold values from -0.25 to 0.25
Outputs:
- encoded: bfloat16 [32, 8, 512, 512], P('win', 'grp')
Inputs may be any that keep to these rules, and one draw needn't show every extreme that they name: Within each of the 8 grp columns, rank over all 32 devices of win is a permutation of 0 to 16383. Each device holds at most 32 points whose rank // 512 is any one owner, and exactly 32 for some owner; each owner receives exactly 32 from some device. For each grp column and owner the 8 counts sum to 512, and the largest is 128.
All inputs are finite; a program needn't handle non-finite values.
Results may differ from a plain program's by a relative error of at most 0.03.
The roundings to bfloat16 on the way count: a program that leaves them out, or rounds other values in their place, can miss the bound.
Values may be sent and summed in bfloat16 or wider, within the bound.
No kernel may reach another device: no remote copies, remote signals or barrier semaphores. Data moves between devices by JAX's collectives and lax.ppermute only.
A program may use at most 128 MiB of HBM per device.

v0:
```python
import jax
import jax.numpy as jnp
from jax import lax
from jax.sharding import PartitionSpec as P

HEAD_DIM = 32
WINDOW_SLOTS = 128


EPSILON = 1e-05
MASKED = -1e30


def normalize(row_data):
    values = row_data.astype(jnp.float32)
    center = values - jnp.mean(values, axis=-1, keepdims=True)
    spread = jnp.mean(center * center, axis=-1, keepdims=True)
    return (center * lax.rsqrt(spread + EPSILON)).astype(jnp.bfloat16)


def project(row_data, weight):
    return jnp.dot(normalize(row_data), weight, preferred_element_type=jnp.float32).astype(
        jnp.bfloat16
    )


def attention_core(packed, valid):
    block_count, width_len, triple = packed.shape
    model_dim = triple // 3
    heads_count = model_dim // HEAD_DIM
    split_heads = packed.reshape(block_count, width_len, 3, heads_count, HEAD_DIM)
    scores = jnp.einsum(
        "bqhe,bkhe->bhqk",
        split_heads[:, :, 0],
        split_heads[:, :, 1],
        preferred_element_type=jnp.float32,
    ) * HEAD_DIM ** (-0.5)
    scores = jnp.where(valid[:, None, None, :], scores, MASKED)
    row_max = jnp.max(scores, axis=-1, keepdims=True)
    weights = jnp.exp(scores - row_max)
    weights = (weights / jnp.sum(weights, axis=-1, keepdims=True)).astype(jnp.bfloat16)
    context = jnp.einsum(
        "bhqk,bkhe->bqhe", weights, split_heads[:, :, 2], preferred_element_type=jnp.float32
    )
    return context.astype(jnp.bfloat16).reshape(block_count * width_len, model_dim)


def residual_add(row_data, context, weight):
    return (
        row_data.astype(jnp.float32) + jnp.dot(context, weight, preferred_element_type=jnp.float32)
    ).astype(jnp.bfloat16)


def feed_forward(row_data, w_up, w_down):
    hidden = jax.nn.gelu(
        jnp.dot(normalize(row_data), w_up, preferred_element_type=jnp.float32), approximate=True
    ).astype(jnp.bfloat16)
    return (
        row_data.astype(jnp.float32) + jnp.dot(hidden, w_down, preferred_element_type=jnp.float32)
    ).astype(jnp.bfloat16)


def on_device(points, rank, counts, w_qkv_one, w_out_one, w_up, w_down, w_qkv_two, w_out_two):
    owner_count = lax.axis_size("win")
    group_count = lax.axis_size("grp")
    win_index = lax.axis_index("win")
    grp_index = lax.axis_index("grp")
    local_points = points.shape[2]
    model_dim = points.shape[3]
    blocks = counts.shape[2]
    slots_all = blocks * WINDOW_SLOTS
    capacity = 2 * local_points // owner_count
    dilation_stride = WINDOW_SLOTS // group_count
    rows_x = points.reshape(local_points, model_dim)
    point_rank = rank.reshape(local_points)
    block_ids = jnp.arange(blocks, dtype=jnp.int32)
    column_counts = lax.dynamic_index_in_dim(counts, grp_index, 0, keepdims=False)
    window_ends = jnp.cumsum(column_counts, axis=1)
    starts = window_ends - column_counts
    owner_dev = point_rank // local_points
    offset = point_rank % local_points
    choose = (owner_dev[:, None] == jnp.arange(owner_count, dtype=jnp.int32)[None, :]).astype(
        jnp.int32
    )
    owner_ends = jnp.sum(choose[:, :, None] * window_ends[None], axis=1)
    owner_starts = jnp.sum(choose[:, :, None] * starts[None], axis=1)
    window = jnp.sum((owner_ends <= offset[:, None]).astype(jnp.int32), axis=1)
    block_pick = (window[:, None] == block_ids[None, :]).astype(jnp.int32)
    dest_slot = window * WINDOW_SLOTS + offset - jnp.sum(block_pick * owner_starts, axis=1)
    peer_order = jnp.sum(choose * (jnp.cumsum(choose, axis=0) - 1), axis=1)
    send_place = owner_dev * capacity + peer_order
    outgoing = (
        jnp.zeros((owner_count * capacity, model_dim), jnp.bfloat16).at[send_place].set(rows_x)
    )
    outgoing_slot = (
        jnp.full((owner_count * capacity,), slots_all, jnp.int32).at[send_place].set(dest_slot)
    )
    arrived, arrived_slot = (
        lax.all_to_all(outgoing, "win", split_axis=0, concat_axis=0, tiled=True),
        lax.all_to_all(outgoing_slot, "win", split_axis=0, concat_axis=0, tiled=True),
    )
    own_counts = lax.dynamic_index_in_dim(column_counts, win_index, 0, keepdims=False)
    column = jnp.arange(WINDOW_SLOTS, dtype=jnp.int32)
    usable_mask = column[None, :] < own_counts[:, None]
    padded_x = (
        jnp.zeros((slots_all, model_dim), jnp.bfloat16).at[arrived_slot].set(arrived, mode="drop")
    )
    packed = project(padded_x, w_qkv_one).reshape(blocks, WINDOW_SLOTS, 3 * model_dim)
    context = attention_core(packed, usable_mask)
    first_pad = feed_forward(residual_add(padded_x, context, w_out_one), w_up, w_down)
    mask_send = usable_mask.astype(jnp.bfloat16).reshape(blocks, dilation_stride, group_count)
    dilated_rows = lax.all_to_all(
        first_pad.reshape(blocks, dilation_stride, group_count, model_dim),
        "grp",
        split_axis=2,
        concat_axis=1,
        tiled=True,
    )
    valid_marks = lax.all_to_all(mask_send, "grp", split_axis=2, concat_axis=1, tiled=True)
    block_count = dilated_rows.shape[0]
    flat_rows = dilated_rows.reshape(block_count * WINDOW_SLOTS, model_dim)
    packed_two = project(flat_rows, w_qkv_two).reshape(block_count, WINDOW_SLOTS, 3 * model_dim)
    head_context = attention_core(packed_two, valid_marks.reshape(block_count, WINDOW_SLOTS) > 0.5)
    mixed_rows = residual_add(flat_rows, head_context, w_out_two).reshape(
        block_count, WINDOW_SLOTS, 1, model_dim
    )
    second_pad = lax.all_to_all(mixed_rows, "grp", split_axis=1, concat_axis=2, tiled=True).reshape(
        slots_all, model_dim
    )
    returning = jnp.take(second_pad, arrived_slot, axis=0, mode="fill", fill_value=0)
    returned = lax.all_to_all(returning, "win", split_axis=0, concat_axis=0, tiled=True)
    encoded = jnp.take(returned, send_place, axis=0)
    return encoded.reshape(1, 1, local_points, model_dim)


def solution(mesh):
    return jax.shard_map(
        on_device,
        mesh=mesh,
        in_specs=(
            P("win", "grp", None, None),
            P("win", "grp", None),
            P(),
            P(),
            P(),
            P(),
            P(),
            P(),
            P(),
        ),
        out_specs=P("win", "grp", None, None),
        check_vma=False,
    )
```

profile of v0, /device:TPU:32, one launch (start us, length us, event | category | flops | bytes accessed | tf_op | source)
XLA Modules:
  0.0 210.3 jit_solution(3294899480315234753)
XLA Ops:
  6.2 2.4 %scatter_custom_fusion = s32[1024]{0:T(1024)S(1)} fusion(s32[512]{0:T(512)S(1)} %bitcast.161, s32[512]{0:T(512)S(1)} %add_subtract_fusion, s32[]{:T(128)} %constant.120.clone.1), kind=kCustom, calls=%fused_computation.140 | custom fusion | bytes 4100 | tf_op jit(solution)/shard_map/scatter | solution.py:96
  9.4 11.4 %all-to-all-start = ((s32[32,32,1]{1,2,0:T(1,128)}), s32[32,32,1]{1,2,0:T(1,128)S(1)}, u32[]{:S(2)}, u32[]{:S(2)}) async-start(s32[32,32,1]{1,2,0:T(1,128)} %all_to_all.49), calls=%async_computation | async-start | bytes 32768 | tf_op jit(solution)/shard_map/all_to_all | solution.py:100
  20.7 4.0 %scatter_custom_fusion.1 = bf16[1024,512]{1,0:T(8,128)(2,1)} fusion(s32[512]{0:T(512)S(1)} %bitcast.162, bf16[1,1,512,512]{3,2,1,0:T(8,128)(2,1)} %param.9, bf16[]{:T(256)} %constant.126.clone.1), kind=kCustom, calls=%fused_computation.82 | custom fusion | bytes 1572866 | tf_op jit(solution)/shard_map/scatter | solution.py:93
  24.7 4.6 %all-to-all-done = s32[32,32,1]{1,2,0:T(1,128)S(1)} async-done(((s32[32,32,1]{1,2,0:T(1,128)}), s32[32,32,1]{1,2,0:T(1,128)S(1)}, u32[]{:S(2)}, u32[]{:S(2)}) %all-to-all-start) | async-done | bytes 4128 | tf_op jit(solution)/shard_map/all_to_all | solution.py:100
  29.3 5.2 %all-to-all-start.1 = ((bf16[32,32,512]{2,1,0:T(8,128)(2,1)}), bf16[32,32,512]{2,1,0:T(8,128)(2,1)S(1)}, u32[]{:S(2)}, u32[]{:S(2)}) async-start(bf16[32,32,512]{2,1,0:T(8,128)(2,1)} %bitcast.12), calls=%async_computation.1 | async-start | bytes 2097152 | tf_op jit(solution)/shard_map/all_to_all | solution.py:99
  37.6 24.9 %all-to-all-done.1 = bf16[32,32,512]{2,1,0:T(8,128)(2,1)S(1)} async-done(((bf16[32,32,512]{2,1,0:T(8,128)(2,1)}), bf16[32,32,512]{2,1,0:T(8,128)(2,1)S(1)}, u32[]{:S(2)}, u32[]{:S(2)}) %all-to-all-start.1) | async-done | bytes 1048608 | tf_op jit(solution)/shard_map/all_to_all | solution.py:99
  62.5 4.3 %all-to-all-start.3 = ((bf16[8,16,8]{1,0,2:T(8,128)(2,1)}), bf16[8,16,8]{1,0,2:T(8,128)(2,1)S(1)}, u32[]{:S(2)}, u32[]{:S(2)}) async-start(bf16[8,16,8]{1,0,2:T(8,128)(2,1)} %compare_convert_fusion), calls=%async_computation.3 | async-start | bytes 32768 | tf_op jit(solution)/shard_map/all_to_all | solution.py:119
  66.8 5.8 %scatter_custom_fusion.2 = bf16[1024,512]{1,0:T(8,128)(2,1)S(1)} fusion(s32[1024]{0:T(1024)S(1)} %bitcast.159, bf16[1024,512]{1,0:T(8,128)(2,1)} %bitcast.151, bf16[]{:T(256)} %constant.126.clone.1), kind=kCustom, calls=%fused_computation.84 | custom fusion | bytes 1049088 | tf_op jit(solution)/shard_map/scatter | solution.py:106
  73.4 4.9 %convolution_convert_fusion.1 = bf16[1024,1536]{1,0:T(8,128)(2,1)} fusion(bf16[512,1536]{1,0:T(8,128)(2,1)} %param.12, bf16[1024,512]{1,0:T(8,128)(2,1)S(1)} %scatter_custom_fusion.2, f32[1024]{0:T(1024)S(1)} %add_rsqrt_fusion.1, f32[1024]{0:T(1024)S(1)} %broadcast_multiply_fusion.1), kind=kOutput, calls=%fused_computation.34 | convolution fusion | flops 1614282752 | bytes 5775360 | tf_op jit(solution)/shard_map/dot_general | solution.py:22
  78.3 4.7 %copy.120 = bf16[1024,1536]{0,1:T(8,128)(2,1)} copy(bf16[1024,1536]{1,0:T(8,128)(2,1)} %convolution_convert_fusion.1) | data formatting | bytes 6291456 | tf_op jit(solution)/shard_map/convert_element_type | solution.py:22
  83.0 2.7 %copy.155 = bf16[192,8,8,128]{3,2,1,0:T(8,128)(2,1)S(1)} copy(bf16[192,8,8,128]{3,1,2,0:T(8,128)(2,1)} %bitcast.145) | data formatting | bytes 6291456
  86.1 1.3 fusion.52
  87.4 3.5 %fusion.86 = (f32[8,16,128]{2,1,0:T(8,128)S(1)}, f32[8,16,128,128]{2,3,1,0:T(8,128)S(1)}) fusion(f32[8,16,128,128]{2,3,1,0:T(8,128)S(1)} %fusion.52, pred[8,128]{1,0:T(8,128)(4,1)S(1)} %iota_compare_fusion.3), kind=kOutput, calls=%fused_computation.158 | output fusion | flops 12583039 | bytes 16843776 | tf_op jit(solution)/shard_map/sub | solution.py:40
  90.9 1.2 fusion.41
  95.1 7.0 %fusion.31 = bf16[1024,512]{1,0:T(8,128)(2,1)S(1)} fusion(bf16[1024,512]{1,0:T(8,128)(2,1)} %copy-done.3, bf16[2048,512]{1,0:T(8,128)(2,1)S(1)} %copy-done, bf16[512,2048]{1,0:T(8,128)(2,1)} %param.14, f32[1024]{0:T(1024)S(1)} %add_rsqrt_fusion, f32[1024]{0:T(1024)S(1)} %broadcast_multiply_fusion), kind=kOutput, calls=%fused_computation.50 | convolution fusion | flops 4317511680 | bytes 6299648 | tf_op jit(solution)/shard_map/dot_general | solution.py:59
  102.2 1.3 copy.126
  103.5 4.8 %all-to-all-start.2 = ((bf16[8,16,8,512]{3,1,0,2:T(8,128)(2,1)}), bf16[8,16,8,512]{3,1,0,2:T(8,128)(2,1)S(1)}, u32[]{:S(2)}, u32[]{:S(2)}) async-start(bf16[8,16,8,512]{3,1,0,2:T(8,128)(2,1)} %copy.126), calls=%async_computation.2 | async-start | bytes 2097152 | tf_op jit(solution)/shard_map/all_to_all | solution.py:112
  108.4 15.8 %all-to-all-done.2 = bf16[8,16,8,512]{3,1,0,2:T(8,128)(2,1)S(1)} async-done(((bf16[8,16,8,512]{3,1,0,2:T(8,128)(2,1)}), bf16[8,16,8,512]{3,1,0,2:T(8,128)(2,1)S(1)}, u32[]{:S(2)}, u32[]{:S(2)}) %all-to-all-start.2) | async-done | bytes 1048608 | tf_op jit(solution)/shard_map/all_to_all | solution.py:112
  126.9 3.5 %convolution_convert_fusion = bf16[1024,1536]{1,0:T(8,128)(2,1)} fusion(bf16[1024,512]{1,0:T(8,128)(2,1)S(1)} %fusion.33, bf16[512,1536]{1,0:T(8,128)(2,1)S(1)} %copy-done.5), kind=kOutput, calls=%fused_computation.33 | convolution fusion | flops 1612185600 | bytes 5767168 | tf_op jit(solution)/shard_map/dot_general | solution.py:22
  130.3 4.7 %copy.133 = bf16[1024,1536]{0,1:T(8,128)(2,1)} copy(bf16[1024,1536]{1,0:T(8,128)(2,1)} %convolution_convert_fusion) | data formatting | bytes 6291456 | tf_op jit(solution)/shard_map/convert_element_type | solution.py:22
  135.0 2.7 %copy.157 = bf16[192,8,8,128]{3,2,1,0:T(8,128)(2,1)S(1)} copy(bf16[192,8,8,128]{3,1,2,0:T(8,128)(2,1)} %bitcast.146) | data formatting | bytes 6291456
  138.1 1.3 fusion.51
  139.4 3.5 %fusion.87 = (f32[8,16,128]{2,1,0:T(8,128)S(1)}, f32[8,16,128,128]{2,3,1,0:T(8,128)S(1)}) fusion(f32[8,16,128,128]{2,3,1,0:T(8,128)S(1)} %fusion.51, pred[8,128]{1,0:T(8,128)(4,1)S(1)} %gt.23), kind=kOutput, calls=%fused_computation.159 | output fusion | flops 12583039 | bytes 16843776 | tf_op jit(solution)/shard_map/sub | solution.py:40
  142.9 1.2 fusion.42
  145.5 1.6 copy.140
  147.1 3.6 %all-to-all-start.4 = ((bf16[8,128,1,512]{3,0,2,1:T(8,128)(2,1)}), bf16[8,128,1,512]{3,0,2,1:T(8,128)(2,1)S(1)}, u32[]{:S(2)}, u32[]{:S(2)}) async-start(bf16[8,128,1,512]{3,0,2,1:T(8,128)(2,1)} %copy.140), calls=%async_computation.4 | async-start | bytes 2097152 | tf_op jit(solution)/shard_map/all_to_all | solution.py:127
  150.7 15.8 %all-to-all-done.4 = bf16[8,128,1,512]{3,0,2,1:T(8,128)(2,1)S(1)} async-done(((bf16[8,128,1,512]{3,0,2,1:T(8,128)(2,1)}), bf16[8,128,1,512]{3,0,2,1:T(8,128)(2,1)S(1)}, u32[]{:S(2)}, u32[]{:S(2)}) %all-to-all-start.4) | async-done | bytes 1048608 | tf_op jit(solution)/shard_map/all_to_all | solution.py:127
  167.1 4.0 %gather_fusion = bf16[1024,512]{1,0:T(8,128)(2,1)S(1)} fusion(bf16[1024,512]{1,0:T(8,128)(2,1)S(1)} %bitcast.141, s32[1024]{0:T(1024)S(1)} %broadcast_clamp_fusion), kind=kCustom, calls=%fused_computation | custom fusion | bytes 2101248 | tf_op jit(solution)/shard_map/jit(_take)/gather | solution.py:130
  172.3 5.2 %all-to-all-start.5 = ((bf16[32,32,512]{2,1,0:T(8,128)(2,1)}), bf16[32,32,512]{2,1,0:T(8,128)(2,1)S(1)}, u32[]{:S(2)}, u32[]{:S(2)}) async-start(bf16[32,32,512]{2,1,0:T(8,128)(2,1)} %broadcast_select_fusion), calls=%async_computation.5 | async-start | bytes 2097152 | tf_op jit(solution)/shard_map/all_to_all | solution.py:131
  177.5 28.2 %all-to-all-done.5 = bf16[32,32,512]{2,1,0:T(8,128)(2,1)S(1)} async-done(((bf16[32,32,512]{2,1,0:T(8,128)(2,1)}), bf16[32,32,512]{2,1,0:T(8,128)(2,1)S(1)}, u32[]{:S(2)}, u32[]{:S(2)}) %all-to-all-start.5) | async-done | bytes 1048608 | tf_op jit(solution)/shard_map/all_to_all | solution.py:131
  205.7 2.6 %gather_fusion.1 = bf16[512,512]{1,0:T(8,128)(2,1)} fusion(bf16[1024,512]{1,0:T(8,128)(2,1)S(1)} %bitcast.142, s32[1024]{0:T(1024)S(1)} %pad_clamp_fusion), kind=kCustom, calls=%fused_computation.1 | custom fusion | bytes 1050624 | tf_op jit(solution)/shard_map/jit(_take)/gather | solution.py:132
  208.3 2.0 bitcast_select_fusion
  (75 shorter events, 20.4 us)
Async XLA Ops:
  0.0 95.1 %copy-start = (bf16[2048,512]{1,0:T(8,128)(2,1)S(1)}, bf16[2048,512]{1,0:T(8,128)(2,1)}, u32[]{:S(2)}) copy-start(bf16[2048,512]{1,0:T(8,128)(2,1)} %param.15) | copy-start | bytes 6291460
  9.4 19.9 %all-to-all-start = ((s32[32,32,1]{1,2,0:T(1,128)}), s32[32,32,1]{1,2,0:T(1,128)S(1)}, u32[]{:S(2)}, u32[]{:S(2)}) async-start(s32[32,32,1]{1,2,0:T(1,128)} %all_to_all.49), calls=%async_computation | async-start | bytes 32768 | tf_op jit(solution)/shard_map/all_to_all | solution.py:100
  29.3 33.2 %all-to-all-start.1 = ((bf16[32,32,512]{2,1,0:T(8,128)(2,1)}), bf16[32,32,512]{2,1,0:T(8,128)(2,1)S(1)}, u32[]{:S(2)}, u32[]{:S(2)}) async-start(bf16[32,32,512]{2,1,0:T(8,128)(2,1)} %bitcast.12), calls=%async_computation.1 | async-start | bytes 2097152 | tf_op jit(solution)/shard_map/all_to_all | solution.py:99
  62.5 4.3 %copy-start.2 = (bf16[32,32,512]{2,1,0:T(8,128)(2,1)}, bf16[32,32,512]{2,1,0:T(8,128)(2,1)S(1)}, u32[]{:S(2)}) copy-start(bf16[32,32,512]{2,1,0:T(8,128)(2,1)S(1)} %all-to-all-done.1) | copy-start | bytes 3145732
  62.5 41.0 %all-to-all-start.3 = ((bf16[8,16,8]{1,0,2:T(8,128)(2,1)}), bf16[8,16,8]{1,0,2:T(8,128)(2,1)S(1)}, u32[]{:S(2)}, u32[]{:S(2)}) async-start(bf16[8,16,8]{1,0,2:T(8,128)(2,1)} %compare_convert_fusion), calls=%async_computation.3 | async-start | bytes 32768 | tf_op jit(solution)/shard_map/all_to_all | solution.py:119
  90.8 1.9 copy-start.6
  93.6 1.0 copy-start.3
  103.5 20.7 %all-to-all-start.2 = ((bf16[8,16,8,512]{3,1,0,2:T(8,128)(2,1)}), bf16[8,16,8,512]{3,1,0,2:T(8,128)(2,1)S(1)}, u32[]{:S(2)}, u32[]{:S(2)}) async-start(bf16[8,16,8,512]{3,1,0,2:T(8,128)(2,1)} %copy.126), calls=%async_computation.2 | async-start | bytes 2097152 | tf_op jit(solution)/shard_map/all_to_all | solution.py:112
  125.5 1.4 copy-start.5
  142.9 1.9 copy-start.4
  147.1 19.4 %all-to-all-start.4 = ((bf16[8,128,1,512]{3,0,2,1:T(8,128)(2,1)}), bf16[8,128,1,512]{3,0,2,1:T(8,128)(2,1)S(1)}, u32[]{:S(2)}, u32[]{:S(2)}) async-start(bf16[8,128,1,512]{3,0,2,1:T(8,128)(2,1)} %copy.140), calls=%async_computation.4 | async-start | bytes 2097152 | tf_op jit(solution)/shard_map/all_to_all | solution.py:127
  172.3 33.4 %all-to-all-start.5 = ((bf16[32,32,512]{2,1,0:T(8,128)(2,1)}), bf16[32,32,512]{2,1,0:T(8,128)(2,1)S(1)}, u32[]{:S(2)}, u32[]{:S(2)}) async-start(bf16[32,32,512]{2,1,0:T(8,128)(2,1)} %broadcast_select_fusion), calls=%async_computation.5 | async-start | bytes 2097152 | tf_op jit(solution)/shard_map/all_to_all | solution.py:131
  177.5 32.8 %copy-start.1 = (bf16[2048,512]{1,0:T(8,128)(2,1)S(1)}, bf16[2048,512]{1,0:T(8,128)(2,1)}, u32[]{:S(2)}) copy-start(bf16[2048,512]{1,0:T(8,128)(2,1)} %param.15) | copy-start | bytes 6291460
where the time goes:
time: 211 us; the launch traced here: 210 us
  waiting for transfers between devices  89.3 us (42%)
  local copies, waits for them, and re-layouts  44.9 us (21%)
  starting transfers between devices  34.4 us (16%)
  matrix products  22 us (10%)
  other arithmetic  19.3 us (9%)
    all_to_all x1, waiting for transfers between devices, on_device(): lax.all_to_all(returning, 'win', split_axis=0, concat_axis=0, tiled=True)  28.2 us
    all_to_all x1, waiting for transfers between devices, on_device(): lax.all_to_all(outgoing, 'win', split_axis=0, concat_axis=0, tiled=True)  24.9 us
    all_to_all x1, waiting for transfers between devices, on_device(): lax.all_to_all(mixed_rows, 'grp', split_axis=1, concat_axis=2, tiled=True)  15.8 us
    all_to_all x1, waiting for transfers between devices, on_device(): lax.all_to_all(first_pad.reshape(blocks, dilation_stride, group_count, mo...  15.8 us
    all_to_all x1, starting transfers between devices, on_device(): lax.all_to_all(outgoing_slot, 'win', split_axis=0, concat_axis=0, tiled=T...  11.4 us
    convert_element_type x2, local copies, waits for them, and re-layouts, project(): jnp.dot(normalize(row_data), weight, preferred_element_type=jnp.float32)  9.38 us
    dot_general x2, matrix products, project(): jnp.dot(normalize(row_data), weight, preferred_element_type=jnp.float32)  8.39 us
    unnamed x16, local copies, waits for them, and re-layouts  7.21 us
  transfers between devices with their start and end apart: 6, of which 5 were waited for; matrix products, arithmetic and copies ran while one was open for 20% of the time, Pallas kernels for 0%

commit v1 on v0

--- a/solution.py
+++ b/solution.py
@@ -60,6 +60,16 @@
     ).astype(jnp.bfloat16)
 
 
+def place(onehot, rows):
+    return jnp.dot(onehot, rows, preferred_element_type=jnp.float32).astype(jnp.bfloat16)
+
+
+def place_back(onehot, rows):
+    return lax.dot_general(
+        onehot, rows, (((0,), (0,)), ((), ())), preferred_element_type=jnp.float32
+    ).astype(jnp.bfloat16)
+
+
 def on_device(points, rank, counts, w_qkv_one, w_out_one, w_up, w_down, w_qkv_two, w_out_two):
     owner_count = lax.axis_size("win")
     group_count = lax.axis_size("grp")
@@ -70,45 +80,49 @@
     blocks = counts.shape[2]
     slots_all = blocks * WINDOW_SLOTS
     capacity = 2 * local_points // owner_count
+    buffer_rows = owner_count * capacity
     dilation_stride = WINDOW_SLOTS // group_count
     rows_x = points.reshape(local_points, model_dim)
     point_rank = rank.reshape(local_points)
-    block_ids = jnp.arange(blocks, dtype=jnp.int32)
+    all_rank = lax.all_gather(point_rank, "win", axis=0, tiled=False)
     column_counts = lax.dynamic_index_in_dim(counts, grp_index, 0, keepdims=False)
-    window_ends = jnp.cumsum(column_counts, axis=1)
-    starts = window_ends - column_counts
+
     owner_dev = point_rank // local_points
-    offset = point_rank % local_points
-    choose = (owner_dev[:, None] == jnp.arange(owner_count, dtype=jnp.int32)[None, :]).astype(
-        jnp.int32
-    )
-    owner_ends = jnp.sum(choose[:, :, None] * window_ends[None], axis=1)
-    owner_starts = jnp.sum(choose[:, :, None] * starts[None], axis=1)
-    window = jnp.sum((owner_ends <= offset[:, None]).astype(jnp.int32), axis=1)
-    block_pick = (window[:, None] == block_ids[None, :]).astype(jnp.int32)
-    dest_slot = window * WINDOW_SLOTS + offset - jnp.sum(block_pick * owner_starts, axis=1)
+    owner_ids = jnp.arange(owner_count, dtype=jnp.int32)
+    choose = (owner_dev[:, None] == owner_ids[None, :]).astype(jnp.int32)
     peer_order = jnp.sum(choose * (jnp.cumsum(choose, axis=0) - 1), axis=1)
     send_place = owner_dev * capacity + peer_order
-    outgoing = (
-        jnp.zeros((owner_count * capacity, model_dim), jnp.bfloat16).at[send_place].set(rows_x)
+    buffer_ids = jnp.arange(buffer_rows, dtype=jnp.int32)
+    send_hot = (buffer_ids[:, None] == send_place[None, :]).astype(jnp.bfloat16)
+    outgoing = place(send_hot, rows_x)
+    arrived = lax.all_to_all(outgoing, "win", split_axis=0, concat_axis=0, tiled=True)
+
+    own_counts = lax.dynamic_index_in_dim(column_counts, win_index, 0, keepdims=False)
+    own_ends = jnp.cumsum(own_counts)
+    own_starts = own_ends - own_counts
+    mine = (all_rank // local_points) == win_index
+    mine_i = mine.astype(jnp.int32)
+    order = jnp.cumsum(mine_i, axis=1) - 1
+    offset = all_rank % local_points
+    window = jnp.sum((own_ends[None, None, :] <= offset[:, :, None]).astype(jnp.int32), axis=2)
+    block_ids = jnp.arange(blocks, dtype=jnp.int32)
+    start_of = jnp.sum(
+        (window[:, :, None] == block_ids[None, None, :]).astype(jnp.int32) * own_starts[None, None, :],
+        axis=2,
     )
-    outgoing_slot = (
-        jnp.full((owner_count * capacity,), slots_all, jnp.int32).at[send_place].set(dest_slot)
-    )
-    arrived, arrived_slot = (
-        lax.all_to_all(outgoing, "win", split_axis=0, concat_axis=0, tiled=True),
-        lax.all_to_all(outgoing_slot, "win", split_axis=0, concat_axis=0, tiled=True),
-    )
-    own_counts = lax.dynamic_index_in_dim(column_counts, win_index, 0, keepdims=False)
+    slot = window * WINDOW_SLOTS + offset - start_of
+    cap_ids = jnp.arange(capacity, dtype=jnp.int32)
+    pick = (order[:, :, None] == cap_ids[None, None, :]) & mine[:, :, None]
+    arrived_slot = jnp.sum(pick.astype(jnp.int32) * (slot[:, :, None] + 1), axis=1) - 1
+    slot_ids = jnp.arange(slots_all, dtype=jnp.int32)
+    recv_hot = (slot_ids[:, None] == arrived_slot.reshape(1, buffer_rows)).astype(jnp.bfloat16)
+    padded_x = place(recv_hot, arrived)
+
     column = jnp.arange(WINDOW_SLOTS, dtype=jnp.int32)
     usable_mask = column[None, :] < own_counts[:, None]
-    padded_x = (
-        jnp.zeros((slots_all, model_dim), jnp.bfloat16).at[arrived_slot].set(arrived, mode="drop")
-    )
     packed = project(padded_x, w_qkv_one).reshape(blocks, WINDOW_SLOTS, 3 * model_dim)
     context = attention_core(packed, usable_mask)
     first_pad = feed_forward(residual_add(padded_x, context, w_out_one), w_up, w_down)
-    mask_send = usable_mask.astype(jnp.bfloat16).reshape(blocks, dilation_stride, group_count)
     dilated_rows = lax.all_to_all(
         first_pad.reshape(blocks, dilation_stride, group_count, model_dim),
         "grp",
@@ -116,20 +130,24 @@
         concat_axis=1,
         tiled=True,
     )
-    valid_marks = lax.all_to_all(mask_send, "grp", split_axis=2, concat_axis=1, tiled=True)
+    owner_counts = lax.dynamic_index_in_dim(counts, win_index, 1, keepdims=False)
+    k_ids = jnp.arange(dilation_stride, dtype=jnp.int32)
+    valid_marks = (k_ids[None, None, :] * group_count + grp_index) < jnp.transpose(owner_counts)[
+        :, :, None
+    ]
     block_count = dilated_rows.shape[0]
     flat_rows = dilated_rows.reshape(block_count * WINDOW_SLOTS, model_dim)
     packed_two = project(flat_rows, w_qkv_two).reshape(block_count, WINDOW_SLOTS, 3 * model_dim)
-    head_context = attention_core(packed_two, valid_marks.reshape(block_count, WINDOW_SLOTS) > 0.5)
+    head_context = attention_core(packed_two, valid_marks.reshape(block_count, WINDOW_SLOTS))
     mixed_rows = residual_add(flat_rows, head_context, w_out_two).reshape(
         block_count, WINDOW_SLOTS, 1, model_dim
     )
     second_pad = lax.all_to_all(mixed_rows, "grp", split_axis=1, concat_axis=2, tiled=True).reshape(
         slots_all, model_dim
     )
-    returning = jnp.take(second_pad, arrived_slot, axis=0, mode="fill", fill_value=0)
+    returning = place_back(recv_hot, second_pad)
     returned = lax.all_to_all(returning, "win", split_axis=0, concat_axis=0, tiled=True)
-    encoded = jnp.take(returned, send_place, axis=0)
+    encoded = place_back(send_hot, returned)
     return encoded.reshape(1, 1, local_points, model_dim)
 
 

time: 211 us -> 221 us (1.047)
  blocking collectives: 0 us -> 121 us
  waiting for transfers between devices: 89.3 us -> 15.5 us
  local copies, waits for them, and re-layouts: 44.9 us -> 23.8 us
  starting transfers between devices: 34.4 us -> 15.7 us
  matrix products: 22 us -> 27.9 us
  other arithmetic: 19.3 us -> 15.9 us
    all_gather x0 -> x1, blocking collectives: none -> 66.7 us  [on_device(): all_rank = lax.all_gather(point_rank, 'win', axis=0, tiled=False)]
    all_to_all x0 -> x2, blocking collectives: none -> 54.3 us  [the longest x1 35.9 us: on_device(): lax.all_to_all(returning, 'win', split_axis=0, concat_axis=0, tiled=True)]
    all_to_all x4 -> x0, waiting for transfers between devices: 48.6 us -> none  [the longest x1 28.2 us: on_device(): lax.all_to_all(returning, 'win', split_axis=0, concat_axis=0, tiled=True)]
    all_to_all x1, waiting for transfers between devices: 24.9 us -> 0.01 us  [on_device(): lax.all_to_all(outgoing, 'win', split_axis=0, concat_axis=0, tiled=True)]
    all_to_all x4 -> x0, starting transfers between devices: 24.4 us -> none  [the longest x1 11.4 us: on_device(): lax.all_to_all(outgoing_slot, 'win', split_axis=0, concat_axis=0, tiled=T...]
    scatter x3 -> x0, local copies, waits for them, and re-layouts: 12.3 us -> none  [the longest x1 5.84 us: on_device(): jnp.zeros((slots_all, model_dim), jnp.bfloat16).at[arrived_slot]]
    dot_general x0 -> x4, matrix products: none -> 6.93 us  [the longest x2 4.08 us: place(): jnp.dot(onehot, rows, preferred_element_type=jnp.float32)]
    gather x2 -> x0, local copies, waits for them, and re-layouts: 6.58 us -> none  [the longest x1 3.97 us: on_device(): jnp.take(second_pad, arrived_slot, axis=0, mode='fill', fill_value=0)]
  transfers between devices with their start and end apart: 6 -> 2, of which waited for: 5 -> 1; matrix products, arithmetic and copies ran while one was open for 20% -> 2% of each run, Pallas kernels for 0% -> 0%
where the time goes in v1:
time: 221 us; the launch traced here: 220 us
  blocking collectives  121 us (55%)
  matrix products  27.9 us (13%)
  local copies, waits for them, and re-layouts  23.8 us (11%)
  other arithmetic  15.9 us (7%)
  starting transfers between devices  15.7 us (7%)
  waiting for transfers between devices  15.5 us (7%)
    all_gather x1, blocking collectives, on_device(): all_rank = lax.all_gather(point_rank, 'win', axis=0, tiled=False)  66.7 us
    all_to_all x1, blocking collectives, on_device(): lax.all_to_all(returning, 'win', split_axis=0, concat_axis=0, tiled=True)  35.9 us
    all_to_all x1, blocking collectives, on_device(): lax.all_to_all(mixed_rows, 'grp', split_axis=1, concat_axis=2, tiled=True)  18.4 us
    all_to_all x1, waiting for transfers between devices, on_device(): lax.all_to_all(first_pad.reshape(blocks, dilation_stride, group_count, mo...  15.5 us
    all_to_all x1, starting transfers between devices, on_device(): lax.all_to_all(outgoing, 'win', split_axis=0, concat_axis=0, tiled=True)  11.4 us
    convert_element_type x2, local copies, waits for them, and re-layouts, project(): jnp.dot(normalize(row_data), weight, preferred_element_type=jnp.float32)  9.38 us
    dot_general x1, matrix products, feed_forward(): jnp.dot(hidden, w_down, preferred_element_type=jnp.float32)  7.4 us
    sub x2, other arithmetic, attention_core(): weights = jnp.exp(scores - row_max)  7.09 us
  transfers between devices with their start and end apart: 2, of which 1 were waited for; matrix products, arithmetic and copies ran while one was open for 2% of the time, Pallas kernels for 0%

profile of v1, /device:TPU:32, one launch (start us, length us, event | category | flops | bytes accessed | tf_op | source)
XLA Modules:
  0.0 220.1 jit_solution(18286271890335403194)
XLA Ops:
  0.0 0.8 add_select_fusion.2
  1.6 1.2 reduce-window.16
  3.1 0.7 multiply_add_fusion
  3.8 2.8 %fusion.44 = bf16[1024,512]{1,0:T(8,128)(2,1)} fusion(s32[512]{0:T(512)S(1)} %multiply_add_fusion, bf16[1,1,512,512]{3,2,1,0:T(8,128)(2,1)} %param.9), kind=kOutput, calls=%fused_computation.65 | convolution fusion | flops 537919488 | bytes 1574912 | tf_op jit(solution)/shard_map/dot_general | solution.py:64
  6.5 11.4 %all-to-all-start = ((bf16[32,32,512]{2,1,0:T(8,128)(2,1)}), bf16[32,32,512]{2,1,0:T(8,128)(2,1)S(1)}, u32[]{:S(2)}, u32[]{:S(2)}) async-start(bf16[32,32,512]{2,1,0:T(8,128)(2,1)} %bitcast.170), calls=%async_computation | async-start | bytes 2097152 | tf_op jit(solution)/shard_map/all_to_all | solution.py:98
  17.9 66.7 %all-gather = s32[32,1,512]{2,1,0:T(1,128)S(1)} all-gather(s32[1,1,512]{2,1,0:T(1,128)S(1)} %copy-done.6), channel_id=2, replica_groups=mesh['win'=32,'grp'=8] {'win'}, dimensions={0}, use_global_device_ids=true | all-gather | bytes 67584 | tf_op jit(solution)/shard_map/all_gather | solution.py:87
  85.0 1.2 reduce-window.20
  87.9 1.3 convert_reduce_fusion.1
  90.3 3.5 %convolution_convert_fusion.1 = bf16[1024,1536]{1,0:T(8,128)(2,1)} fusion(bf16[512,1536]{1,0:T(8,128)(2,1)S(1)} %copy-done.7, bf16[1024,512]{1,0:T(8,128)(2,1)S(1)} %get-tuple-element.14, f32[1024]{0:T(1024)S(1)} %add_rsqrt_fusion.1, f32[1024]{0:T(1024)S(1)} %broadcast_multiply_fusion.1), kind=kOutput, calls=%fused_computation.32 | convolution fusion | flops 1614282752 | bytes 5775360 | tf_op jit(solution)/shard_map/dot_general | solution.py:22
  93.8 4.7 %copy.124 = bf16[1024,1536]{0,1:T(8,128)(2,1)} copy(bf16[1024,1536]{1,0:T(8,128)(2,1)} %convolution_convert_fusion.1) | data formatting | bytes 6291456 | tf_op jit(solution)/shard_map/convert_element_type | solution.py:22
  98.5 2.7 %copy.167 = bf16[192,8,8,128]{3,2,1,0:T(8,128)(2,1)S(1)} copy(bf16[192,8,8,128]{3,1,2,0:T(8,128)(2,1)} %bitcast.164) | data formatting | bytes 6291456
  101.6 1.3 fusion.64
  102.9 3.6 %fusion.99 = (f32[8,16,128]{2,1,0:T(8,128)S(1)}, f32[8,16,128,128]{2,3,1,0:T(8,128)S(1)}) fusion(f32[8,16,128,128]{2,3,1,0:T(8,128)S(1)} %fusion.64, pred[8,128]{1,0:T(8,128)(4,1)S(1)} %iota_compare_fusion.20), kind=kOutput, calls=%fused_computation.163 | output fusion | flops 12583039 | bytes 16843776 | tf_op jit(solution)/shard_map/sub | solution.py:40
  106.5 1.2 fusion.51
  108.5 0.8 convert_reduce_fusion
  109.9 7.4 %fusion.33 = bf16[1024,512]{1,0:T(8,128)(2,1)} fusion(bf16[1024,512]{1,0:T(8,128)(2,1)S(1)} %get-tuple-element.18, bf16[2048,512]{1,0:T(8,128)(2,1)S(1)} %copy-done, bf16[512,2048]{1,0:T(8,128)(2,1)} %param.14, f32[1024]{0:T(1024)S(1)} %add_rsqrt_fusion, f32[1024]{0:T(1024)S(1)} %broadcast_multiply_fusion), kind=kOutput, calls=%fused_computation.48 | convolution fusion | flops 4317511680 | bytes 6299648 | tf_op jit(solution)/shard_map/dot_general | solution.py:59
  117.3 2.6 %copy.130 = bf16[8,16,8,512]{3,1,0,2:T(8,128)(2,1)} copy(bf16[8,16,8,512]{3,2,1,0:T(8,128)(2,1)} %bitcast.172) | data formatting | bytes 2097152 | tf_op jit(solution)/shard_map/reshape | solution.py:127
  119.8 4.3 %all-to-all-start.1 = ((bf16[8,16,8,512]{3,1,0,2:T(8,128)(2,1)}), bf16[8,16,8,512]{3,1,0,2:T(8,128)(2,1)S(1)}, u32[]{:S(2)}, u32[]{:S(2)}) async-start(bf16[8,16,8,512]{3,1,0,2:T(8,128)(2,1)} %copy.130), calls=%async_computation.1 | async-start | bytes 2097152 | tf_op jit(solution)/shard_map/all_to_all | solution.py:126
  124.6 15.5 %all-to-all-done.1 = bf16[8,16,8,512]{3,1,0,2:T(8,128)(2,1)S(1)} async-done(((bf16[8,16,8,512]{3,1,0,2:T(8,128)(2,1)}), bf16[8,16,8,512]{3,1,0,2:T(8,128)(2,1)S(1)}, u32[]{:S(2)}, u32[]{:S(2)}) %all-to-all-start.1) | async-done | bytes 1048608 | tf_op jit(solution)/shard_map/all_to_all | solution.py:126
  141.9 0.8 copy-done.8
  142.7 3.5 %convolution_convert_fusion = bf16[1024,1536]{1,0:T(8,128)(2,1)} fusion(bf16[1024,512]{1,0:T(8,128)(2,1)S(1)} %fusion.35, bf16[512,1536]{1,0:T(8,128)(2,1)S(1)} %copy-done.8), kind=kOutput, calls=%fused_computation.31 | convolution fusion | flops 1612185600 | bytes 5767168 | tf_op jit(solution)/shard_map/dot_general | solution.py:22
  146.2 4.7 %copy.137 = bf16[1024,1536]{0,1:T(8,128)(2,1)} copy(bf16[1024,1536]{1,0:T(8,128)(2,1)} %convolution_convert_fusion) | data formatting | bytes 6291456 | tf_op jit(solution)/shard_map/convert_element_type | solution.py:22
  150.9 2.7 %copy.169 = bf16[192,8,8,128]{3,2,1,0:T(8,128)(2,1)S(1)} copy(bf16[192,8,8,128]{3,1,2,0:T(8,128)(2,1)} %bitcast.165) | data formatting | bytes 6291456
  153.9 1.3 fusion.63
  155.3 3.5 %fusion.100 = (f32[8,16,128]{2,1,0:T(8,128)S(1)}, f32[8,16,128,128]{2,3,1,0:T(8,128)S(1)}) fusion(f32[8,16,128,128]{2,3,1,0:T(8,128)S(1)} %fusion.63, pred[8,128]{1,0:T(8,128)(4,1)S(1)} %broadcast_compare_fusion), kind=kOutput, calls=%fused_computation.164 | output fusion | flops 12583039 | bytes 16843776 | tf_op jit(solution)/shard_map/sub | solution.py:40
  158.7 1.2 fusion.52
  159.9 0.7 copy.144
  160.7 0.7 fusion.36
  162.0 18.4 %all_to_all.48 = bf16[8,128,1,512]{3,0,2,1:T(8,128)(2,1)S(1)} all-to-all(bf16[8,128,1,512]{3,0,2,1:T(8,128)(2,1)S(1)} %copy.145), channel_id=1, replica_groups=mesh['win'=32,'grp'=8] {'grp'}, dimensions={1} | all-to-all | bytes 2097152 | tf_op jit(solution)/shard_map/all_to_all | solution.py:145
  181.3 1.3 fusion.46
  182.6 35.9 %all_to_all.49 = bf16[32,32,512]{2,1,0:T(8,128)(2,1)S(1)} all-to-all(bf16[32,32,512]{2,1,0:T(8,128)(2,1)S(1)} %bitcast.174), channel_id=1, replica_groups=mesh['win'=32,'grp'=8] {'win'}, dimensions={0} | all-to-all | bytes 2097152 | tf_op jit(solution)/shard_map/all_to_all | solution.py:149
  218.5 1.6 fusion.54
  (74 shorter events, 9.9 us)
Async XLA Ops:
  0.0 109.8 %copy-start = (bf16[2048,512]{1,0:T(8,128)(2,1)S(1)}, bf16[2048,512]{1,0:T(8,128)(2,1)}, u32[]{:S(2)}) copy-start(bf16[2048,512]{1,0:T(8,128)(2,1)} %param.15) | copy-start | bytes 6291460
  0.0 17.9 %copy-start.6 = (s32[1,1,512]{2,1,0:T(1,128)S(1)}, s32[1,1,512]{2,1,0:T(1,128)}, u32[]{:S(2)}) copy-start(s32[1,1,512]{2,1,0:T(1,128)} %param.10) | copy-start | bytes 6148
  0.0 84.6 %copy-start.5 = (s32[8,32,8]{1,2,0:T(8,128)S(1)}, s32[8,32,8]{1,2,0:T(8,128)}, u32[]{:S(2)}) copy-start(s32[8,32,8]{1,2,0:T(8,128)} %param.11) | copy-start | bytes 24580
  6.5 81.4 %all-to-all-start = ((bf16[32,32,512]{2,1,0:T(8,128)(2,1)}), bf16[32,32,512]{2,1,0:T(8,128)(2,1)S(1)}, u32[]{:S(2)}, u32[]{:S(2)}) async-start(bf16[32,32,512]{2,1,0:T(8,128)(2,1)} %bitcast.170), calls=%async_computation | async-start | bytes 2097152 | tf_op jit(solution)/shard_map/all_to_all | solution.py:98
  87.9 2.3 %copy-start.7 = (bf16[512,1536]{1,0:T(8,128)(2,1)S(1)}, bf16[512,1536]{1,0:T(8,128)(2,1)}, u32[]{:S(2)}) copy-start(bf16[512,1536]{1,0:T(8,128)(2,1)} %param.12) | copy-start | bytes 4718596
  89.3 1.0 copy-start.2
  106.5 1.9 copy-start.3
  106.5 1.9 copy-start.9
  119.8 20.2 %all-to-all-start.1 = ((bf16[8,16,8,512]{3,1,0,2:T(8,128)(2,1)}), bf16[8,16,8,512]{3,1,0,2:T(8,128)(2,1)S(1)}, u32[]{:S(2)}, u32[]{:S(2)}) async-start(bf16[8,16,8,512]{3,1,0,2:T(8,128)(2,1)} %copy.130), calls=%async_computation.1 | async-start | bytes 2097152 | tf_op jit(solution)/shard_map/all_to_all | solution.py:126
  141.3 1.4 copy-start.8
  158.7 1.9 copy-start.4
  181.3 38.7 %copy-start.1 = (bf16[2048,512]{1,0:T(8,128)(2,1)S(1)}, bf16[2048,512]{1,0:T(8,128)(2,1)}, u32[]{:S(2)}) copy-start(bf16[2048,512]{1,0:T(8,128)(2,1)} %param.15) | copy-start | bytes 6291460

commit v2 on v1

--- a/solution.py
+++ b/solution.py
@@ -84,7 +84,6 @@
     dilation_stride = WINDOW_SLOTS // group_count
     rows_x = points.reshape(local_points, model_dim)
     point_rank = rank.reshape(local_points)
-    all_rank = lax.all_gather(point_rank, "win", axis=0, tiled=False)
     column_counts = lax.dynamic_index_in_dim(counts, grp_index, 0, keepdims=False)
 
     owner_dev = point_rank // local_points
@@ -97,23 +96,20 @@
     outgoing = place(send_hot, rows_x)
     arrived = lax.all_to_all(outgoing, "win", split_axis=0, concat_axis=0, tiled=True)
 
+    window_ends = jnp.cumsum(column_counts, axis=1)
+    starts = window_ends - column_counts
+    offset = point_rank % local_points
+    owner_ends = jnp.sum(choose[:, :, None] * window_ends[None], axis=1)
+    owner_starts = jnp.sum(choose[:, :, None] * starts[None], axis=1)
+    window = jnp.sum((owner_ends <= offset[:, None]).astype(jnp.int32), axis=1)
+    block_ids = jnp.arange(blocks, dtype=jnp.int32)
+    block_pick = (window[:, None] == block_ids[None, :]).astype(jnp.int32)
+    dest_slot = window * WINDOW_SLOTS + offset - jnp.sum(block_pick * owner_starts, axis=1)
+    outgoing_slot = jnp.sum(send_hot.astype(jnp.int32) * (dest_slot[None, :] + 1), axis=1) - 1
+    arrived_slot = lax.all_to_all(
+        outgoing_slot.reshape(owner_count, capacity), "win", split_axis=0, concat_axis=0, tiled=True
+    )
     own_counts = lax.dynamic_index_in_dim(column_counts, win_index, 0, keepdims=False)
-    own_ends = jnp.cumsum(own_counts)
-    own_starts = own_ends - own_counts
-    mine = (all_rank // local_points) == win_index
-    mine_i = mine.astype(jnp.int32)
-    order = jnp.cumsum(mine_i, axis=1) - 1
-    offset = all_rank % local_points
-    window = jnp.sum((own_ends[None, None, :] <= offset[:, :, None]).astype(jnp.int32), axis=2)
-    block_ids = jnp.arange(blocks, dtype=jnp.int32)
-    start_of = jnp.sum(
-        (window[:, :, None] == block_ids[None, None, :]).astype(jnp.int32) * own_starts[None, None, :],
-        axis=2,
-    )
-    slot = window * WINDOW_SLOTS + offset - start_of
-    cap_ids = jnp.arange(capacity, dtype=jnp.int32)
-    pick = (order[:, :, None] == cap_ids[None, None, :]) & mine[:, :, None]
-    arrived_slot = jnp.sum(pick.astype(jnp.int32) * (slot[:, :, None] + 1), axis=1) - 1
     slot_ids = jnp.arange(slots_all, dtype=jnp.int32)
     recv_hot = (slot_ids[:, None] == arrived_slot.reshape(1, buffer_rows)).astype(jnp.bfloat16)
     padded_x = place(recv_hot, arrived)

time: 221 us -> 189 us (0.86)
  blocking collectives: 121 us -> 51.5 us
  waiting for transfers between devices: 15.5 us -> 47.3 us
  starting transfers between devices: 15.7 us -> 20.6 us
    all_gather x1 -> x0, blocking collectives: 66.7 us -> none  [on_device(): all_rank = lax.all_gather(point_rank, 'win', axis=0, tiled=False)]
    all_to_all x1, waiting for transfers between devices: 0.01 us -> 26 us  [on_device(): lax.all_to_all(outgoing, 'win', split_axis=0, concat_axis=0, tiled=True)]
    all_to_all x0 -> x1, starting transfers between devices: none -> 11.4 us  [on_device(): lax.all_to_all(outgoing_slot.reshape(owner_count, capacity), 'win', split...]
    all_to_all x1, starting transfers between devices: 11.4 us -> 4.99 us  [on_device(): lax.all_to_all(outgoing, 'win', split_axis=0, concat_axis=0, tiled=True)]
    all_to_all x0 -> x1, waiting for transfers between devices: none -> 5.82 us  [on_device(): lax.all_to_all(outgoing_slot.reshape(owner_count, capacity), 'win', split...]
    all_to_all x1, blocking collectives: 35.9 us -> 33.1 us  [on_device(): lax.all_to_all(returning, 'win', split_axis=0, concat_axis=0, tiled=True)]
    unnamed x23 -> x20, local copies, waits for them, and re-layouts: 6.77 us -> 6.69 us
  transfers between devices with their start and end apart: 2 -> 3, of which waited for: 1 -> 3; matrix products, arithmetic and copies ran while one was open for 2% -> 3% of each run, Pallas kernels for 0% -> 0%
where the time goes in v2:
time: 189 us
  blocking collectives  51.5 us (27%)
  waiting for transfers between devices  47.3 us (25%)
  matrix products  27.9 us (15%)
  local copies, waits for them, and re-layouts  25.8 us (14%)
  starting transfers between devices  20.6 us (11%)
  other arithmetic  15.1 us (8%)
    all_to_all x1, blocking collectives, on_device(): lax.all_to_all(returning, 'win', split_axis=0, concat_axis=0, tiled=True)  33.1 us
    all_to_all x1, waiting for transfers between devices, on_device(): lax.all_to_all(outgoing, 'win', split_axis=0, concat_axis=0, tiled=True)  26 us
    all_to_all x1, blocking collectives, on_device(): lax.all_to_all(mixed_rows, 'grp', split_axis=1, concat_axis=2, tiled=True)  18.4 us
    all_to_all x1, waiting for transfers between devices, on_device(): lax.all_to_all(first_pad.reshape(blocks, dilation_stride, group_count, mo...  15.5 us
    all_to_all x1, starting transfers between devices, on_device(): lax.all_to_all(outgoing_slot.reshape(owner_count, capacity), 'win', split...  11.4 us
    convert_element_type x2, local copies, waits for them, and re-layouts, project(): jnp.dot(normalize(row_data), weight, preferred_element_type=jnp.float32)  9.38 us
    dot_general x1, matrix products, feed_forward(): jnp.dot(hidden, w_down, preferred_element_type=jnp.float32)  7.42 us
    sub x2, other arithmetic, attention_core(): weights = jnp.exp(scores - row_max)  7.09 us
  transfers between devices with their start and end apart: 3, of which 3 were waited for; matrix products, arithmetic and copies ran while one was open for 3% of the time, Pallas kernels for 0%

profile of v2, /device:TPU:32, one launch (start us, length us, event | category | flops | bytes accessed | tf_op | source)
XLA Modules:
  0.0 188.6 jit_solution(14707029718772299494)
XLA Ops:
  0.0 0.8 dynamic-slice_bitcast_fusion
  3.1 1.2 reduce-window.6
  6.7 11.4 %all-to-all-start = ((s32[32,1,32]{2,1,0:T(1,128)}), s32[32,1,32]{2,1,0:T(1,128)S(1)}, u32[]{:S(2)}, u32[]{:S(2)}) async-start(s32[32,1,32]{2,1,0:T(1,128)} %sub.86), calls=%async_computation | async-start | bytes 32768 | tf_op jit(solution)/shard_map/all_to_all | solution.py:109
  18.1 2.8 %fusion.44 = bf16[1024,512]{1,0:T(8,128)(2,1)} fusion(s32[512]{0:T(512)S(1)} %get-tuple-element.24, bf16[1,1,512,512]{3,2,1,0:T(8,128)(2,1)} %param.9), kind=kOutput, calls=%fused_computation.64 | convolution fusion | flops 537919488 | bytes 1574912 | tf_op jit(solution)/shard_map/dot_general | solution.py:64
  20.9 5.8 %all-to-all-done = s32[32,1,32]{2,1,0:T(1,128)S(1)} async-done(((s32[32,1,32]{2,1,0:T(1,128)}), s32[32,1,32]{2,1,0:T(1,128)S(1)}, u32[]{:S(2)}, u32[]{:S(2)}) %all-to-all-start) | async-done | bytes 4128 | tf_op jit(solution)/shard_map/all_to_all | solution.py:109
  26.7 5.0 %all-to-all-start.1 = ((bf16[32,32,512]{2,1,0:T(8,128)(2,1)}), bf16[32,32,512]{2,1,0:T(8,128)(2,1)S(1)}, u32[]{:S(2)}, u32[]{:S(2)}) async-start(bf16[32,32,512]{2,1,0:T(8,128)(2,1)} %bitcast.130), calls=%async_computation.1 | async-start | bytes 2097152 | tf_op jit(solution)/shard_map/all_to_all | solution.py:97
  33.2 26.0 %all-to-all-done.1 = bf16[32,32,512]{2,1,0:T(8,128)(2,1)S(1)} async-done(((bf16[32,32,512]{2,1,0:T(8,128)(2,1)}), bf16[32,32,512]{2,1,0:T(8,128)(2,1)S(1)}, u32[]{:S(2)}, u32[]{:S(2)}) %all-to-all-start.1) | async-done | bytes 1048608 | tf_op jit(solution)/shard_map/all_to_all | solution.py:97
  59.2 1.3 convert_reduce_fusion.1
  61.6 3.5 %convolution_convert_fusion.1 = bf16[1024,1536]{1,0:T(8,128)(2,1)} fusion(bf16[512,1536]{1,0:T(8,128)(2,1)S(1)} %copy-done.6, bf16[1024,512]{1,0:T(8,128)(2,1)S(1)} %get-tuple-element.16, f32[1024]{0:T(1024)S(1)} %add_rsqrt_fusion.1, f32[1024]{0:T(1024)S(1)} %broadcast_multiply_fusion.1), kind=kOutput, calls=%fused_computation.32 | convolution fusion | flops 1614282752 | bytes 5775360 | tf_op jit(solution)/shard_map/dot_general | solution.py:22
  65.1 4.7 %copy.122 = bf16[1024,1536]{0,1:T(8,128)(2,1)} copy(bf16[1024,1536]{1,0:T(8,128)(2,1)} %convolution_convert_fusion.1) | data formatting | bytes 6291456 | tf_op jit(solution)/shard_map/convert_element_type | solution.py:22
  69.8 2.7 %copy.161 = bf16[192,8,8,128]{3,2,1,0:T(8,128)(2,1)S(1)} copy(bf16[192,8,8,128]{3,1,2,0:T(8,128)(2,1)} %bitcast.124) | data formatting | bytes 6291456
  72.8 1.3 fusion.64
  74.2 3.6 %fusion.94 = (f32[8,16,128]{2,1,0:T(8,128)S(1)}, f32[8,16,128,128]{2,3,1,0:T(8,128)S(1)}) fusion(f32[8,16,128,128]{2,3,1,0:T(8,128)S(1)} %fusion.64, pred[8,128]{1,0:T(8,128)(4,1)S(1)} %iota_compare_fusion.19), kind=kOutput, calls=%fused_computation.151 | output fusion | flops 12583039 | bytes 16843776 | tf_op jit(solution)/shard_map/sub | solution.py:40
  77.8 1.2 fusion.51
  79.0 0.7 copy.127
  79.8 0.8 convert_reduce_fusion
  81.1 7.4 %fusion.33 = bf16[1024,512]{1,0:T(8,128)(2,1)} fusion(bf16[1024,512]{1,0:T(8,128)(2,1)S(1)} %get-tuple-element.20, bf16[2048,512]{1,0:T(8,128)(2,1)S(1)} %copy-done, bf16[512,2048]{1,0:T(8,128)(2,1)} %param.14, f32[1024]{0:T(1024)S(1)} %add_rsqrt_fusion, f32[1024]{0:T(1024)S(1)} %broadcast_multiply_fusion), kind=kOutput, calls=%fused_computation.48 | convolution fusion | flops 4317511680 | bytes 6299648 | tf_op jit(solution)/shard_map/dot_general | solution.py:59
  88.6 2.6 %copy.128 = bf16[8,16,8,512]{3,1,0,2:T(8,128)(2,1)} copy(bf16[8,16,8,512]{3,2,1,0:T(8,128)(2,1)} %bitcast.132) | data formatting | bytes 2097152 | tf_op jit(solution)/shard_map/reshape | solution.py:123
  91.1 4.3 %all-to-all-start.2 = ((bf16[8,16,8,512]{3,1,0,2:T(8,128)(2,1)}), bf16[8,16,8,512]{3,1,0,2:T(8,128)(2,1)S(1)}, u32[]{:S(2)}, u32[]{:S(2)}) async-start(bf16[8,16,8,512]{3,1,0,2:T(8,128)(2,1)} %copy.128), calls=%async_computation.2 | async-start | bytes 2097152 | tf_op jit(solution)/shard_map/all_to_all | solution.py:122
  95.9 15.5 %all-to-all-done.2 = bf16[8,16,8,512]{3,1,0,2:T(8,128)(2,1)S(1)} async-done(((bf16[8,16,8,512]{3,1,0,2:T(8,128)(2,1)}), bf16[8,16,8,512]{3,1,0,2:T(8,128)(2,1)S(1)}, u32[]{:S(2)}, u32[]{:S(2)}) %all-to-all-start.2) | async-done | bytes 1048608 | tf_op jit(solution)/shard_map/all_to_all | solution.py:122
  113.2 0.8 copy-done.7
  114.0 3.5 %convolution_convert_fusion = bf16[1024,1536]{1,0:T(8,128)(2,1)} fusion(bf16[1024,512]{1,0:T(8,128)(2,1)S(1)} %fusion.35, bf16[512,1536]{1,0:T(8,128)(2,1)S(1)} %copy-done.7), kind=kOutput, calls=%fused_computation.31 | convolution fusion | flops 1612185600 | bytes 5767168 | tf_op jit(solution)/shard_map/dot_general | solution.py:22
  117.5 4.7 %copy.135 = bf16[1024,1536]{0,1:T(8,128)(2,1)} copy(bf16[1024,1536]{1,0:T(8,128)(2,1)} %convolution_convert_fusion) | data formatting | bytes 6291456 | tf_op jit(solution)/shard_map/convert_element_type | solution.py:22
  122.2 2.7 %copy.163 = bf16[192,8,8,128]{3,2,1,0:T(8,128)(2,1)S(1)} copy(bf16[192,8,8,128]{3,1,2,0:T(8,128)(2,1)} %bitcast.125) | data formatting | bytes 6291456
  125.2 1.3 fusion.63
  126.5 3.5 %fusion.95 = (f32[8,16,128]{2,1,0:T(8,128)S(1)}, f32[8,16,128,128]{2,3,1,0:T(8,128)S(1)}) fusion(f32[8,16,128,128]{2,3,1,0:T(8,128)S(1)} %fusion.63, pred[8,128]{1,0:T(8,128)(4,1)S(1)} %broadcast_compare_fusion), kind=kOutput, calls=%fused_computation.152 | output fusion | flops 12583039 | bytes 16843776 | tf_op jit(solution)/shard_map/sub | solution.py:40
  130.0 1.2 fusion.52
  131.9 0.7 fusion.36
  133.3 18.4 %all_to_all.54 = bf16[8,128,1,512]{3,0,2,1:T(8,128)(2,1)S(1)} all-to-all(bf16[8,128,1,512]{3,0,2,1:T(8,128)(2,1)S(1)} %copy.143), channel_id=1, replica_groups=mesh['win'=32,'grp'=8] {'grp'}, dimensions={1} | all-to-all | bytes 2097152 | tf_op jit(solution)/shard_map/all_to_all | solution.py:141
  152.6 1.3 fusion.46
  153.9 33.1 %all_to_all.55 = bf16[32,32,512]{2,1,0:T(8,128)(2,1)S(1)} all-to-all(bf16[32,32,512]{2,1,0:T(8,128)(2,1)S(1)} %bitcast.134), channel_id=1, replica_groups=mesh['win'=32,'grp'=8] {'win'}, dimensions={0} | all-to-all | bytes 2097152 | tf_op jit(solution)/shard_map/all_to_all | solution.py:145
  187.0 1.6 fusion.54
  (71 shorter events, 12.9 us)
Async XLA Ops:
  0.0 81.1 %copy-start = (bf16[2048,512]{1,0:T(8,128)(2,1)S(1)}, bf16[2048,512]{1,0:T(8,128)(2,1)}, u32[]{:S(2)}) copy-start(bf16[2048,512]{1,0:T(8,128)(2,1)} %param.15) | copy-start | bytes 6291460
  0.0 31.7 %copy-start.5 = (s32[8,32,8]{1,2,0:T(8,128)S(1)}, s32[8,32,8]{1,2,0:T(8,128)}, u32[]{:S(2)}) copy-start(s32[8,32,8]{1,2,0:T(8,128)} %param.11) | copy-start | bytes 24580
  6.7 19.9 %all-to-all-start = ((s32[32,1,32]{2,1,0:T(1,128)}), s32[32,1,32]{2,1,0:T(1,128)S(1)}, u32[]{:S(2)}, u32[]{:S(2)}) async-start(s32[32,1,32]{2,1,0:T(1,128)} %sub.86), calls=%async_computation | async-start | bytes 32768 | tf_op jit(solution)/shard_map/all_to_all | solution.py:109
  26.7 32.5 %all-to-all-start.1 = ((bf16[32,32,512]{2,1,0:T(8,128)(2,1)}), bf16[32,32,512]{2,1,0:T(8,128)(2,1)S(1)}, u32[]{:S(2)}, u32[]{:S(2)}) async-start(bf16[32,32,512]{2,1,0:T(8,128)(2,1)} %bitcast.130), calls=%async_computation.1 | async-start | bytes 2097152 | tf_op jit(solution)/shard_map/all_to_all | solution.py:97
  59.2 2.3 %copy-start.6 = (bf16[512,1536]{1,0:T(8,128)(2,1)S(1)}, bf16[512,1536]{1,0:T(8,128)(2,1)}, u32[]{:S(2)}) copy-start(bf16[512,1536]{1,0:T(8,128)(2,1)} %param.12) | copy-start | bytes 4718596
  60.6 1.0 copy-start.2
  77.8 1.9 %copy-start.3 = (bf16[1024,512]{1,0:T(8,128)(2,1)S(1)}, bf16[1024,512]{1,0:T(8,128)(2,1)}, u32[]{:S(2)}) copy-start(bf16[1024,512]{1,0:T(8,128)(2,1)} %copy-done.2) | copy-start | bytes 3145732
  77.8 1.9 %copy-start.8 = (bf16[512,512]{1,0:T(8,128)(2,1)S(1)}, bf16[512,512]{1,0:T(8,128)(2,1)}, u32[]{:S(2)}) copy-start(bf16[512,512]{1,0:T(8,128)(2,1)} %param.13) | copy-start | bytes 1572868
  91.1 20.2 %all-to-all-start.2 = ((bf16[8,16,8,512]{3,1,0,2:T(8,128)(2,1)}), bf16[8,16,8,512]{3,1,0,2:T(8,128)(2,1)S(1)}, u32[]{:S(2)}, u32[]{:S(2)}) async-start(bf16[8,16,8,512]{3,1,0,2:T(8,128)(2,1)} %copy.128), calls=%async_computation.2 | async-start | bytes 2097152 | tf_op jit(solution)/shard_map/all_to_all | solution.py:122
  112.6 1.4 copy-start.7
  130.0 1.9 %copy-start.4 = (bf16[512,512]{1,0:T(8,128)(2,1)S(1)}, bf16[512,512]{1,0:T(8,128)(2,1)}, u32[]{:S(2)}) copy-start(bf16[512,512]{1,0:T(8,128)(2,1)} %param.17) | copy-start | bytes 1572868
  152.6 36.0 %copy-start.1 = (bf16[2048,512]{1,0:T(8,128)(2,1)S(1)}, bf16[2048,512]{1,0:T(8,128)(2,1)}, u32[]{:S(2)}) copy-start(bf16[2048,512]{1,0:T(8,128)(2,1)} %param.15) | copy-start | bytes 6291460

commit v3 on v2

--- a/solution.py
+++ b/solution.py
@@ -9,6 +9,7 @@
 
 EPSILON = 1e-05
 MASKED = -1e30
+CHUNKS = 2
 
 
 def normalize(row_data):
@@ -116,31 +117,36 @@
 
     column = jnp.arange(WINDOW_SLOTS, dtype=jnp.int32)
     usable_mask = column[None, :] < own_counts[:, None]
-    packed = project(padded_x, w_qkv_one).reshape(blocks, WINDOW_SLOTS, 3 * model_dim)
-    context = attention_core(packed, usable_mask)
-    first_pad = feed_forward(residual_add(padded_x, context, w_out_one), w_up, w_down)
-    dilated_rows = lax.all_to_all(
-        first_pad.reshape(blocks, dilation_stride, group_count, model_dim),
-        "grp",
-        split_axis=2,
-        concat_axis=1,
-        tiled=True,
-    )
     owner_counts = lax.dynamic_index_in_dim(counts, win_index, 1, keepdims=False)
     k_ids = jnp.arange(dilation_stride, dtype=jnp.int32)
     valid_marks = (k_ids[None, None, :] * group_count + grp_index) < jnp.transpose(owner_counts)[
         :, :, None
     ]
-    block_count = dilated_rows.shape[0]
-    flat_rows = dilated_rows.reshape(block_count * WINDOW_SLOTS, model_dim)
-    packed_two = project(flat_rows, w_qkv_two).reshape(block_count, WINDOW_SLOTS, 3 * model_dim)
-    head_context = attention_core(packed_two, valid_marks.reshape(block_count, WINDOW_SLOTS))
-    mixed_rows = residual_add(flat_rows, head_context, w_out_two).reshape(
-        block_count, WINDOW_SLOTS, 1, model_dim
-    )
-    second_pad = lax.all_to_all(mixed_rows, "grp", split_axis=1, concat_axis=2, tiled=True).reshape(
-        slots_all, model_dim
-    )
+    valid_marks = valid_marks.reshape(blocks, WINDOW_SLOTS)
+    padded_blocks = padded_x.reshape(blocks, WINDOW_SLOTS, model_dim)
+    per = blocks // CHUNKS
+    pieces = []
+    for chunk in range(CHUNKS):
+        low, high = chunk * per, (chunk + 1) * per
+        chunk_x = padded_blocks[low:high].reshape(per * WINDOW_SLOTS, model_dim)
+        packed = project(chunk_x, w_qkv_one).reshape(per, WINDOW_SLOTS, 3 * model_dim)
+        context = attention_core(packed, usable_mask[low:high])
+        first_pad = feed_forward(residual_add(chunk_x, context, w_out_one), w_up, w_down)
+        dilated_rows = lax.all_to_all(
+            first_pad.reshape(per, dilation_stride, group_count, model_dim),
+            "grp",
+            split_axis=2,
+            concat_axis=1,
+            tiled=True,
+        )
+        flat_rows = dilated_rows.reshape(per * WINDOW_SLOTS, model_dim)
+        packed_two = project(flat_rows, w_qkv_two).reshape(per, WINDOW_SLOTS, 3 * model_dim)
+        head_context = attention_core(packed_two, valid_marks[low:high])
+        mixed_rows = residual_add(flat_rows, head_context, w_out_two).reshape(
+            per, WINDOW_SLOTS, 1, model_dim
+        )
+        pieces.append(lax.all_to_all(mixed_rows, "grp", split_axis=1, concat_axis=2, tiled=True))
+    second_pad = jnp.concatenate(pieces, axis=0).reshape(slots_all, model_dim)
     returning = place_back(recv_hot, second_pad)
     returned = lax.all_to_all(returning, "win", split_axis=0, concat_axis=0, tiled=True)
     encoded = place_back(send_hot, returned)

time: 189 us -> 221 us (1.17)
  local copies, waits for them, and re-layouts: 25.8 us -> 46.6 us
  blocking collectives: 51.5 us -> 33.1 us
  starting transfers between devices: 20.6 us -> 33.7 us
  matrix products: 27.9 us -> 38.5 us
  waiting for transfers between devices: 47.3 us -> 51.6 us
    all_to_all x1 -> x0, blocking collectives: 18.4 us -> none  [on_device(): lax.all_to_all(mixed_rows, 'grp', split_axis=1, concat_axis=2, tiled=True)]
    another operation x1 -> x5, local copies, waits for them, and re-layouts: 0.01 us -> 14 us  [the longest x4 14 us: attention_core(): packed.reshape(block_count, width_len, 3, heads_count, HEAD_DIM)]
    all_to_all x1 -> x4, starting transfers between devices: 4.3 us -> 17.3 us  [the longest x2 9.12 us: on_device(): lax.all_to_all(first_pad.reshape(per, dilation_stride, group_count, model...]
    slice x2 -> x4, local copies, waits for them, and re-layouts: 0.69 us -> 8.62 us  [attention_core(): split_heads[:, :, 2]]
    dot_general x2 -> x4, matrix products: 6.99 us -> 13 us  [project(): jnp.dot(normalize(row_data), weight, preferred_element_type=jnp.float32)]
    all_to_all x1 -> x4, waiting for transfers between devices: 15.5 us -> 20.1 us  [the longest x2 10.2 us: on_device(): lax.all_to_all(mixed_rows, 'grp', split_axis=1, concat_axis=2, tiled=True)]
    unnamed x20 -> x22, local copies, waits for them, and re-layouts: 6.69 us -> 2.06 us
    dot_general x1 -> x2, matrix products: 7.42 us -> 9.54 us  [feed_forward(): jnp.dot(hidden, w_down, preferred_element_type=jnp.float32)]
  transfers between devices with their start and end apart: 3 -> 6, of which waited for: 3 -> 4; matrix products, arithmetic and copies ran while one was open for 3% -> 21% of each run, Pallas kernels for 0% -> 0%
where the time goes in v3:
time: 221 us; the launch traced here: 220 us
  waiting for transfers between devices  51.6 us (23%)
  local copies, waits for them, and re-layouts  46.6 us (21%)
  matrix products  38.5 us (17%)
  starting transfers between devices  33.7 us (15%)
  blocking collectives  33.1 us (15%)
  other arithmetic  15.7 us (7%)
    all_to_all x1, blocking collectives, on_device(): lax.all_to_all(returning, 'win', split_axis=0, concat_axis=0, tiled=True)  33.1 us
    all_to_all x1, waiting for transfers between devices, on_device(): lax.all_to_all(outgoing, 'win', split_axis=0, concat_axis=0, tiled=True)  25.7 us
    another operation x4, local copies, waits for them, and re-layouts, attention_core(): packed.reshape(block_count, width_len, 3, heads_count, HEAD_DIM)  14 us
    dot_general x4, matrix products, project(): jnp.dot(normalize(row_data), weight, preferred_element_type=jnp.float32)  13 us
    all_to_all x1, starting transfers between devices, on_device(): lax.all_to_all(outgoing_slot.reshape(owner_count, capacity), 'win', split...  11.4 us
    convert_element_type x4, local copies, waits for them, and re-layouts, project(): jnp.dot(normalize(row_data), weight, preferred_element_type=jnp.float32)  10.4 us
    all_to_all x2, waiting for transfers between devices, on_device(): lax.all_to_all(mixed_rows, 'grp', split_axis=1, concat_axis=2, tiled=True)  10.2 us
    all_to_all x2, waiting for transfers between devices, on_device(): lax.all_to_all(first_pad.reshape(per, dilation_stride, group_count, model...  9.86 us
  transfers between devices with their start and end apart: 6, of which 4 were waited for; matrix products, arithmetic and copies ran while one was open for 21% of the time, Pallas kernels for 0%

profile of v3, /device:TPU:32, one launch (start us, length us, event | category | flops | bytes accessed | tf_op | source)
XLA Modules:
  0.0 219.7 jit_solution(3007014903606004657)
XLA Ops:
  6.7 11.4 %all-to-all-start = ((s32[32,1,32]{2,1,0:T(1,128)}), s32[32,1,32]{2,1,0:T(1,128)S(1)}, u32[]{:S(2)}, u32[]{:S(2)}) async-start(s32[32,1,32]{2,1,0:T(1,128)} %sub.131), calls=%async_computation | async-start | bytes 32768 | tf_op jit(solution)/shard_map/all_to_all | solution.py:110
  18.1 2.8 %fusion.51 = bf16[1024,512]{1,0:T(8,128)(2,1)} fusion(s32[512]{0:T(512)S(1)} %get-tuple-element.42, bf16[1,1,512,512]{3,2,1,0:T(8,128)(2,1)} %param.9), kind=kOutput, calls=%fused_computation.82 | convolution fusion | flops 537919488 | bytes 1574912 | tf_op jit(solution)/shard_map/dot_general | solution.py:65
  20.9 5.8 %all-to-all-done = s32[32,1,32]{2,1,0:T(1,128)S(1)} async-done(((s32[32,1,32]{2,1,0:T(1,128)}), s32[32,1,32]{2,1,0:T(1,128)S(1)}, u32[]{:S(2)}, u32[]{:S(2)}) %all-to-all-start) | async-done | bytes 4128 | tf_op jit(solution)/shard_map/all_to_all | solution.py:110
  26.7 5.0 %all-to-all-start.1 = ((bf16[32,32,512]{2,1,0:T(8,128)(2,1)}), bf16[32,32,512]{2,1,0:T(8,128)(2,1)S(1)}, u32[]{:S(2)}, u32[]{:S(2)}) async-start(bf16[32,32,512]{2,1,0:T(8,128)(2,1)} %bitcast.7), calls=%async_computation.1 | async-start | bytes 2097152 | tf_op jit(solution)/shard_map/all_to_all | solution.py:98
  33.6 25.7 %all-to-all-done.1 = bf16[32,32,512]{2,1,0:T(8,128)(2,1)S(1)} async-done(((bf16[32,32,512]{2,1,0:T(8,128)(2,1)}), bf16[32,32,512]{2,1,0:T(8,128)(2,1)S(1)}, u32[]{:S(2)}, u32[]{:S(2)}) %all-to-all-start.1) | async-done | bytes 1048608 | tf_op jit(solution)/shard_map/all_to_all | solution.py:98
  60.2 2.6 %fusion.52 = bf16[1024,512]{1,0:T(8,128)(2,1)S(1)} fusion(bf16[1024,512]{1,0:T(8,128)(2,1)} %bitcast.196, s32[1024]{0:T(1024)S(1)} %eq.81), kind=kOutput, calls=%fused_computation.83 | convolution fusion | flops 1075314688 | bytes 2101248 | tf_op jit(solution)/shard_map/dot_general | solution.py:65
  63.6 2.2 convolution_convert_fusion.3
  65.8 2.6 %copy.201 = bf16[512,1536]{0,1:T(8,128)(2,1)} copy(bf16[512,1536]{1,0:T(8,128)(2,1)} %convolution_convert_fusion.3) | data formatting | bytes 3145728 | tf_op jit(solution)/shard_map/convert_element_type | solution.py:23
  68.4 3.5 %reshape_reshape.12 = bf16[4,128,3,16,32]{1,0,4,3,2:T(4,128)(2,1)} reshape(bf16[512,1536]{0,1:T(8,128)(2,1)} %copy.201) | data formatting | bytes 3145728 | tf_op jit(solution)/shard_map/reshape;reshape | solution.py:32
  71.9 2.0 fusion.172
  79.2 4.5 %fusion.63 = bf16[512,512]{1,0:T(8,128)(2,1)S(1)} fusion(bf16[2048,512]{1,0:T(8,128)(2,1)S(1)} %copy-done, bf16[512,512]{1,0:T(8,128)(2,1)} %copy-done.6, bf16[512,2048]{1,0:T(8,128)(2,1)} %param.14, f32[512]{0:T(512)S(1)} %add_rsqrt_fusion.2, f32[512]{0:T(512)S(1)} %broadcast_multiply_fusion.2), kind=kOutput, calls=%fused_computation.92 | convolution fusion | flops 2158755840 | bytes 5246976 | tf_op jit(solution)/shard_map/dot_general | solution.py:60
  84.7 4.3 %all-to-all-start.2 = ((bf16[4,16,8,512]{3,1,0,2:T(8,128)(2,1)}), bf16[4,16,8,512]{3,1,0,2:T(8,128)(2,1)S(1)}, u32[]{:S(2)}, u32[]{:S(2)}) async-start(bf16[4,16,8,512]{3,1,0,2:T(8,128)(2,1)} %copy.207), calls=%async_computation.2 | async-start | bytes 1048576 | tf_op jit(solution)/shard_map/all_to_all | solution.py:135
  89.0 3.8 %convolution_convert_fusion.1 = bf16[512,1536]{1,0:T(8,128)(2,1)} fusion(bf16[512,1536]{1,0:T(8,128)(2,1)} %param.12, f32[512]{0:T(512)S(1)} %add_rsqrt_fusion.1, f32[512]{0:T(512)S(1)} %broadcast_multiply_fusion.1, bf16[1024,512]{1,0:T(8,128)(2,1)} %copy-done.2), kind=kOutput, calls=%fused_computation.42 | convolution fusion | flops 807141376 | bytes 3674112 | tf_op jit(solution)/shard_map/dot_general | solution.py:23
  92.8 2.6 %copy.224 = bf16[512,1536]{0,1:T(8,128)(2,1)} copy(bf16[512,1536]{1,0:T(8,128)(2,1)} %convolution_convert_fusion.1) | data formatting | bytes 3145728 | tf_op jit(solution)/shard_map/convert_element_type | solution.py:23
  95.4 3.5 %reshape_reshape.14 = bf16[4,128,3,16,32]{1,0,4,3,2:T(4,128)(2,1)} reshape(bf16[512,1536]{0,1:T(8,128)(2,1)} %copy.224) | data formatting | bytes 3145728 | tf_op jit(solution)/shard_map/reshape;reshape | solution.py:32
  98.9 2.0 fusion.174
  105.6 5.0 %fusion.66 = bf16[512,512]{1,0:T(8,128)(2,1)} fusion(bf16[2048,512]{1,0:T(8,128)(2,1)S(1)} %copy-done, bf16[512,512]{1,0:T(8,128)(2,1)S(1)} %get-tuple-element.36, bf16[512,2048]{1,0:T(8,128)(2,1)} %param.14, f32[512]{0:T(512)S(1)} %add_rsqrt_fusion, f32[512]{0:T(512)S(1)} %broadcast_multiply_fusion), kind=kOutput, calls=%fused_computation.93 | convolution fusion | flops 2158755840 | bytes 5246976 | tf_op jit(solution)/shard_map/dot_general | solution.py:60
  110.7 2.0 copy.230
  112.7 4.8 %all-to-all-start.4 = ((bf16[4,16,8,512]{3,1,0,2:T(8,128)(2,1)}), bf16[4,16,8,512]{3,1,0,2:T(8,128)(2,1)S(1)}, u32[]{:S(2)}, u32[]{:S(2)}) async-start(bf16[4,16,8,512]{3,1,0,2:T(8,128)(2,1)} %copy.230), calls=%async_computation.4 | async-start | bytes 1048576 | tf_op jit(solution)/shard_map/all_to_all | solution.py:135
  117.9 9.9 %all-to-all-done.4 = bf16[4,16,8,512]{3,1,0,2:T(8,128)(2,1)S(1)} async-done(((bf16[4,16,8,512]{3,1,0,2:T(8,128)(2,1)}), bf16[4,16,8,512]{3,1,0,2:T(8,128)(2,1)S(1)}, u32[]{:S(2)}, u32[]{:S(2)}) %all-to-all-start.4) | async-done | bytes 524320 | tf_op jit(solution)/shard_map/all_to_all | solution.py:135
  128.9 3.5 %convolution_convert_fusion.2 = bf16[512,1536]{1,0:T(8,128)(2,1)} fusion(bf16[512,512]{1,0:T(8,128)(2,1)S(1)} %fusion.97, bf16[512,1536]{1,0:T(8,128)(2,1)} %param.16), kind=kOutput, calls=%fused_computation.43 | convolution fusion | flops 806092800 | bytes 3670016 | tf_op jit(solution)/shard_map/dot_general | solution.py:23
  132.5 2.6 %copy.214 = bf16[512,1536]{0,1:T(8,128)(2,1)} copy(bf16[512,1536]{1,0:T(8,128)(2,1)} %convolution_convert_fusion.2) | data formatting | bytes 3145728 | tf_op jit(solution)/shard_map/convert_element_type | solution.py:23
  135.1 3.5 %reshape_reshape.13 = bf16[4,128,3,16,32]{1,0,4,3,2:T(4,128)(2,1)} reshape(bf16[512,1536]{0,1:T(8,128)(2,1)} %copy.214) | data formatting | bytes 3145728 | tf_op jit(solution)/shard_map/reshape;reshape | solution.py:32
  138.6 2.2 %fusion.171 = (bf16[4,128,1,16,32]{1,0,4,3,2:T(4,128)(2,1)S(1)}, bf16[4,128,1,16,32]{1,0,4,3,2:T(4,128)(2,1)S(1)}, bf16[4,128,1,16,32]{1,0,4,3,2:T(4,128)(2,1)S(1)}) fusion(bf16[4,128,3,16,32]{1,0,4,3,2:T(4,128)(2,1)} %reshape_reshape.13), kind=kLoop, calls=%fused_computation.243 | loop fusion | bytes 3145728 | tf_op jit(solution)/shard_map/slice | solution.py:44
  146.1 3.5 %all-to-all-start.3 = ((bf16[4,128,1,512]{3,0,2,1:T(4,128)(2,1)}), bf16[4,128,1,512]{3,0,2,1:T(4,128)(2,1)S(1)}, u32[]{:S(2)}, u32[]{:S(2)}) async-start(bf16[4,128,1,512]{3,0,2,1:T(4,128)(2,1)} %copy.222), calls=%async_computation.3 | async-start | bytes 1048576 | tf_op jit(solution)/shard_map/all_to_all | solution.py:148
  150.5 3.5 %convolution_convert_fusion = bf16[512,1536]{1,0:T(8,128)(2,1)} fusion(bf16[512,512]{1,0:T(8,128)(2,1)S(1)} %fusion.95, bf16[512,1536]{1,0:T(8,128)(2,1)} %param.16), kind=kOutput, calls=%fused_computation.41 | convolution fusion | flops 806092800 | bytes 3670016 | tf_op jit(solution)/shard_map/dot_general | solution.py:23
  154.0 2.6 %copy.237 = bf16[512,1536]{0,1:T(8,128)(2,1)} copy(bf16[512,1536]{1,0:T(8,128)(2,1)} %convolution_convert_fusion) | data formatting | bytes 3145728 | tf_op jit(solution)/shard_map/convert_element_type | solution.py:23
  156.6 3.5 %reshape_reshape.15 = bf16[4,128,3,16,32]{1,0,4,3,2:T(4,128)(2,1)} reshape(bf16[512,1536]{0,1:T(8,128)(2,1)} %copy.237) | data formatting | bytes 3145728 | tf_op jit(solution)/shard_map/reshape;reshape | solution.py:32
  160.2 2.4 %fusion.173 = (bf16[4,128,1,16,32]{1,0,4,3,2:T(4,128)(2,1)S(1)}, bf16[4,128,1,16,32]{1,0,4,3,2:T(4,128)(2,1)S(1)}, bf16[4,128,1,16,32]{1,0,4,3,2:T(4,128)(2,1)S(1)}) fusion(bf16[4,128,3,16,32]{1,0,4,3,2:T(4,128)(2,1)} %reshape_reshape.15), kind=kLoop, calls=%fused_computation.245 | loop fusion | bytes 3145728 | tf_op jit(solution)/shard_map/slice | solution.py:44
  167.9 4.7 %all-to-all-start.5 = ((bf16[4,128,1,512]{3,0,2,1:T(4,128)(2,1)}), bf16[4,128,1,512]{3,0,2,1:T(4,128)(2,1)S(1)}, u32[]{:S(2)}, u32[]{:S(2)}) async-start(bf16[4,128,1,512]{3,0,2,1:T(4,128)(2,1)} %copy.243), calls=%async_computation.5 | async-start | bytes 1048576 | tf_op jit(solution)/shard_map/all_to_all | solution.py:148
  172.7 10.2 %all-to-all-done.5 = bf16[4,128,1,512]{3,0,2,1:T(4,128)(2,1)S(1)} async-done(((bf16[4,128,1,512]{3,0,2,1:T(4,128)(2,1)}), bf16[4,128,1,512]{3,0,2,1:T(4,128)(2,1)S(1)}, u32[]{:S(2)}, u32[]{:S(2)}) %all-to-all-start.5) | async-done | bytes 524320 | tf_op jit(solution)/shard_map/all_to_all | solution.py:148
  185.0 33.1 %all_to_all.84 = bf16[32,32,512]{2,1,0:T(8,128)(2,1)S(1)} all-to-all(bf16[32,32,512]{2,1,0:T(8,128)(2,1)S(1)} %bitcast.198), channel_id=1, replica_groups=mesh['win'=32,'grp'=8] {'win'}, dimensions={0} | all-to-all | bytes 2097152 | tf_op jit(solution)/shard_map/all_to_all | solution.py:151
  (119 shorter events, 37.8 us)
Async XLA Ops:
  0.0 79.2 %copy-start = (bf16[2048,512]{1,0:T(8,128)(2,1)S(1)}, bf16[2048,512]{1,0:T(8,128)(2,1)}, u32[]{:S(2)}) copy-start(bf16[2048,512]{1,0:T(8,128)(2,1)} %param.15) | copy-start | bytes 6291460
  0.0 31.7 %copy-start.7 = (s32[8,32,8]{1,2,0:T(8,128)S(1)}, s32[8,32,8]{1,2,0:T(8,128)}, u32[]{:S(2)}) copy-start(s32[8,32,8]{1,2,0:T(8,128)} %param.11) | copy-start | bytes 24580
  6.7 19.9 %all-to-all-start = ((s32[32,1,32]{2,1,0:T(1,128)}), s32[32,1,32]{2,1,0:T(1,128)S(1)}, u32[]{:S(2)}, u32[]{:S(2)}) async-start(s32[32,1,32]{2,1,0:T(1,128)} %sub.131), calls=%async_computation | async-start | bytes 32768 | tf_op jit(solution)/shard_map/all_to_all | solution.py:110
  26.7 32.5 %all-to-all-start.1 = ((bf16[32,32,512]{2,1,0:T(8,128)(2,1)}), bf16[32,32,512]{2,1,0:T(8,128)(2,1)S(1)}, u32[]{:S(2)}, u32[]{:S(2)}) async-start(bf16[32,32,512]{2,1,0:T(8,128)(2,1)} %bitcast.7), calls=%async_computation.1 | async-start | bytes 2097152 | tf_op jit(solution)/shard_map/all_to_all | solution.py:98
  59.2 1.0 copy-start.5
  60.2 3.4 %copy-start.8 = (bf16[512,1536]{1,0:T(8,128)(2,1)S(1)}, bf16[512,1536]{1,0:T(8,128)(2,1)}, u32[]{:S(2)}) copy-start(bf16[512,1536]{1,0:T(8,128)(2,1)} %param.12) | copy-start | bytes 4718596
  62.8 14.7 %copy-start.2 = (bf16[1024,512]{1,0:T(8,128)(2,1)}, bf16[1024,512]{1,0:T(8,128)(2,1)S(1)}, u32[]{:S(2)}) copy-start(bf16[1024,512]{1,0:T(8,128)(2,1)S(1)} %fusion.52) | copy-start | bytes 3145732
  76.4 1.1 copy-start.9
  78.1 0.8 copy-start.6
  84.7 28.0 %all-to-all-start.2 = ((bf16[4,16,8,512]{3,1,0,2:T(8,128)(2,1)}), bf16[4,16,8,512]{3,1,0,2:T(8,128)(2,1)S(1)}, u32[]{:S(2)}, u32[]{:S(2)}) async-start(bf16[4,16,8,512]{3,1,0,2:T(8,128)(2,1)} %copy.207), calls=%async_computation.2 | async-start | bytes 1048576 | tf_op jit(solution)/shard_map/all_to_all | solution.py:135
  103.4 1.2 copy-start.3
  103.4 1.3 copy-start.10
  112.7 15.1 %all-to-all-start.4 = ((bf16[4,16,8,512]{3,1,0,2:T(8,128)(2,1)}), bf16[4,16,8,512]{3,1,0,2:T(8,128)(2,1)S(1)}, u32[]{:S(2)}, u32[]{:S(2)}) async-start(bf16[4,16,8,512]{3,1,0,2:T(8,128)(2,1)} %copy.230), calls=%async_computation.4 | async-start | bytes 1048576 | tf_op jit(solution)/shard_map/all_to_all | solution.py:135
  143.3 1.1 copy-start.4
  146.1 21.8 %all-to-all-start.3 = ((bf16[4,128,1,512]{3,0,2,1:T(4,128)(2,1)}), bf16[4,128,1,512]{3,0,2,1:T(4,128)(2,1)S(1)}, u32[]{:S(2)}, u32[]{:S(2)}) async-start(bf16[4,128,1,512]{3,0,2,1:T(4,128)(2,1)} %copy.222), calls=%async_computation.3 | async-start | bytes 1048576 | tf_op jit(solution)/shard_map/all_to_all | solution.py:148
  167.9 15.0 %all-to-all-start.5 = ((bf16[4,128,1,512]{3,0,2,1:T(4,128)(2,1)}), bf16[4,128,1,512]{3,0,2,1:T(4,128)(2,1)S(1)}, u32[]{:S(2)}, u32[]{:S(2)}) async-start(bf16[4,128,1,512]{3,0,2,1:T(4,128)(2,1)} %copy.243), calls=%async_computation.5 | async-start | bytes 1048576 | tf_op jit(solution)/shard_map/all_to_all | solution.py:148
  183.7 36.0 %copy-start.1 = (bf16[2048,512]{1,0:T(8,128)(2,1)S(1)}, bf16[2048,512]{1,0:T(8,128)(2,1)}, u32[]{:S(2)}) copy-start(bf16[2048,512]{1,0:T(8,128)(2,1)} %param.15) | copy-start | bytes 6291460

commit v4 on v2

--- a/solution.py
+++ b/solution.py
@@ -24,31 +24,34 @@
     )
 
 
-def attention_core(packed, valid):
-    block_count, width_len, triple = packed.shape
-    model_dim = triple // 3
+def attention_block(row_data, valid, w_qkv, w_out):
+    rows_count, model_dim = row_data.shape
     heads_count = model_dim // HEAD_DIM
-    split_heads = packed.reshape(block_count, width_len, 3, heads_count, HEAD_DIM)
+    block_count = rows_count // WINDOW_SLOTS
+    normed = normalize(row_data)
+    w_split = w_qkv.reshape(model_dim, 3, heads_count, HEAD_DIM)
+
+    def head_major(part):
+        out = jnp.einsum("nd,dhe->hne", normed, w_split[:, part], preferred_element_type=jnp.float32)
+        return out.astype(jnp.bfloat16).reshape(heads_count, block_count, WINDOW_SLOTS, HEAD_DIM)
+
+    query, key, value = head_major(0), head_major(1), head_major(2)
     scores = jnp.einsum(
-        "bqhe,bkhe->bhqk",
-        split_heads[:, :, 0],
-        split_heads[:, :, 1],
-        preferred_element_type=jnp.float32,
+        "hbqe,hbke->hbqk", query, key, preferred_element_type=jnp.float32
     ) * HEAD_DIM ** (-0.5)
-    scores = jnp.where(valid[:, None, None, :], scores, MASKED)
+    scores = jnp.where(valid[None, :, None, :], scores, MASKED)
     row_max = jnp.max(scores, axis=-1, keepdims=True)
     weights = jnp.exp(scores - row_max)
     weights = (weights / jnp.sum(weights, axis=-1, keepdims=True)).astype(jnp.bfloat16)
-    context = jnp.einsum(
-        "bhqk,bkhe->bqhe", weights, split_heads[:, :, 2], preferred_element_type=jnp.float32
+    context = jnp.einsum("hbqk,hbke->hbqe", weights, value, preferred_element_type=jnp.float32)
+    context = context.astype(jnp.bfloat16).reshape(heads_count, rows_count, HEAD_DIM)
+    mixed = jnp.einsum(
+        "hne,hed->nd",
+        context,
+        w_out.reshape(heads_count, HEAD_DIM, model_dim),
+        preferred_element_type=jnp.float32,
     )
-    return context.astype(jnp.bfloat16).reshape(block_count * width_len, model_dim)
-
-
-def residual_add(row_data, context, weight):
-    return (
-        row_data.astype(jnp.float32) + jnp.dot(context, weight, preferred_element_type=jnp.float32)
-    ).astype(jnp.bfloat16)
+    return (row_data.astype(jnp.float32) + mixed).astype(jnp.bfloat16)
 
 
 def feed_forward(row_data, w_up, w_down):
@@ -116,9 +119,7 @@
 
     column = jnp.arange(WINDOW_SLOTS, dtype=jnp.int32)
     usable_mask = column[None, :] < own_counts[:, None]
-    packed = project(padded_x, w_qkv_one).reshape(blocks, WINDOW_SLOTS, 3 * model_dim)
-    context = attention_core(packed, usable_mask)
-    first_pad = feed_forward(residual_add(padded_x, context, w_out_one), w_up, w_down)
+    first_pad = feed_forward(attention_block(padded_x, usable_mask, w_qkv_one, w_out_one), w_up, w_down)
     dilated_rows = lax.all_to_all(
         first_pad.reshape(blocks, dilation_stride, group_count, model_dim),
         "grp",
@@ -133,9 +134,9 @@
     ]
     block_count = dilated_rows.shape[0]
     flat_rows = dilated_rows.reshape(block_count * WINDOW_SLOTS, model_dim)
-    packed_two = project(flat_rows, w_qkv_two).reshape(block_count, WINDOW_SLOTS, 3 * model_dim)
-    head_context = attention_core(packed_two, valid_marks.reshape(block_count, WINDOW_SLOTS))
-    mixed_rows = residual_add(flat_rows, head_context, w_out_two).reshape(
+    mixed_rows = attention_block(
+        flat_rows, valid_marks.reshape(block_count, WINDOW_SLOTS), w_qkv_two, w_out_two
+    ).reshape(
         block_count, WINDOW_SLOTS, 1, model_dim
     )
     second_pad = lax.all_to_all(mixed_rows, "grp", split_axis=1, concat_axis=2, tiled=True).reshape(

time: 189 us -> 170 us (0.90)
  waiting for transfers between devices: 47.3 us -> 37.1 us
  local copies, waits for them, and re-layouts: 25.8 us -> 18.5 us
  matrix products: 27.9 us -> 25.9 us
    convert_element_type x5 -> x0, local copies, waits for them, and re-layouts: 11 us -> none  [the longest x2 9.38 us: project(): jnp.dot(normalize(row_data), weight, preferred_element_type=jnp.float32)]
    dot_general x8 -> x6, matrix products: 13.6 us -> 6.6 us  [the longest x2 2.61 us: attention_block(): jnp.einsum('hbqe,hbke->hbqk', query, key, preferred_element_type=jnp.floa...]
    all_to_all x1, waiting for transfers between devices: 26 us -> 20.7 us  [on_device(): lax.all_to_all(outgoing, 'win', split_axis=0, concat_axis=0, tiled=True)]
    unnamed x0 -> x6, matrix products: none -> 4.96 us
    all_to_all x1, waiting for transfers between devices: 15.5 us -> 10.5 us  [on_device(): lax.all_to_all(first_pad.reshape(blocks, dilation_stride, group_count, mo...]
    slice x3, local copies, waits for them, and re-layouts: 0.91 us -> 5.09 us  [the longest x2 4.87 us: head_major(): w_split[:, part]]
  transfers between devices with their start and end apart: 3 -> 3, of which waited for: 3 -> 3; matrix products, arithmetic and copies ran while one was open for 3% -> 9% of each run, Pallas kernels for 0% -> 0%
where the time goes in v4:
time: 170 us; the launch traced here: 169 us
  blocking collectives  51.6 us (30%)
  waiting for transfers between devices  37.1 us (22%)
  matrix products  25.9 us (15%)
  starting transfers between devices  20.7 us (12%)
  local copies, waits for them, and re-layouts  18.5 us (11%)
  other arithmetic  14.9 us (9%)
    all_to_all x1, blocking collectives, on_device(): lax.all_to_all(returning, 'win', split_axis=0, concat_axis=0, tiled=True)  33.2 us
    all_to_all x1, waiting for transfers between devices, on_device(): lax.all_to_all(outgoing, 'win', split_axis=0, concat_axis=0, tiled=True)  20.7 us
    all_to_all x1, blocking collectives, on_device(): lax.all_to_all(mixed_rows, 'grp', split_axis=1, concat_axis=2, tiled=True)  18.4 us
    all_to_all x1, starting transfers between devices, on_device(): lax.all_to_all(outgoing_slot.reshape(owner_count, capacity), 'win', split...  11.4 us
    all_to_all x1, waiting for transfers between devices, on_device(): lax.all_to_all(first_pad.reshape(blocks, dilation_stride, group_count, mo...  10.5 us
    dot_general x1, matrix products, feed_forward(): jnp.dot(hidden, w_down, preferred_element_type=jnp.float32)  7.4 us
    sub x2, other arithmetic, attention_block(): weights = jnp.exp(scores - row_max)  7.11 us
    unnamed x20, local copies, waits for them, and re-layouts  6.35 us
  transfers between devices with their start and end apart: 3, of which 3 were waited for; matrix products, arithmetic and copies ran while one was open for 9% of the time, Pallas kernels for 0%

profile of v4, /device:TPU:32, one launch (start us, length us, event | category | flops | bytes accessed | tf_op | source)
XLA Modules:
  0.0 169.0 jit_solution(17998953685495266342)
XLA Ops:
  0.0 0.8 dynamic-slice_bitcast_fusion
  3.1 1.2 reduce-window.6
  6.7 11.4 %all-to-all-start = ((s32[32,1,32]{2,1,0:T(1,128)}), s32[32,1,32]{2,1,0:T(1,128)S(1)}, u32[]{:S(2)}, u32[]{:S(2)}) async-start(s32[32,1,32]{2,1,0:T(1,128)} %sub.85), calls=%async_computation | async-start | bytes 32768 | tf_op jit(solution)/shard_map/all_to_all | solution.py:112
  18.1 2.7 %fusion.46 = bf16[1024,512]{1,0:T(8,128)(2,1)} fusion(s32[512]{0:T(512)S(1)} %get-tuple-element.24, bf16[1,1,512,512]{3,2,1,0:T(8,128)(2,1)} %param.9), kind=kOutput, calls=%fused_computation.63 | convolution fusion | flops 537919488 | bytes 1574912 | tf_op jit(solution)/shard_map/dot_general | solution.py:67
  20.8 5.8 %all-to-all-done = s32[32,1,32]{2,1,0:T(1,128)S(1)} async-done(((s32[32,1,32]{2,1,0:T(1,128)}), s32[32,1,32]{2,1,0:T(1,128)S(1)}, u32[]{:S(2)}, u32[]{:S(2)}) %all-to-all-start) | async-done | bytes 4128 | tf_op jit(solution)/shard_map/all_to_all | solution.py:112
  26.7 5.0 %all-to-all-start.1 = ((bf16[32,32,512]{2,1,0:T(8,128)(2,1)}), bf16[32,32,512]{2,1,0:T(8,128)(2,1)S(1)}, u32[]{:S(2)}, u32[]{:S(2)}) async-start(bf16[32,32,512]{2,1,0:T(8,128)(2,1)} %bitcast.191), calls=%async_computation.1 | async-start | bytes 2097152 | tf_op jit(solution)/shard_map/all_to_all | solution.py:100
  31.7 2.6 %copy.116 = bf16[512,1536]{0,1:T(8,128)(2,1)} copy(bf16[512,1536]{1,0:T(8,128)(2,1)} %param.12) | data formatting | bytes 3145728 | tf_op args[3]
  34.6 2.5 %fusion.107 = (bf16[512,1,16,32]{0,3,2,1:T(8,128)(2,1)}, bf16[512,1,16,32]{0,3,2,1:T(8,128)(2,1)}, bf16[512,1,16,32]{0,3,2,1:T(8,128)(2,1)}) fusion(bf16[512,3,16,32]{0,3,2,1:T(8,128)(2,1)} %bitcast.181), kind=kLoop, calls=%fused_computation.160 | loop fusion | bytes 3145728 | tf_op jit(solution)/shard_map/slice | solution.py:35
  38.5 20.7 %all-to-all-done.1 = bf16[32,32,512]{2,1,0:T(8,128)(2,1)S(1)} async-done(((bf16[32,32,512]{2,1,0:T(8,128)(2,1)}), bf16[32,32,512]{2,1,0:T(8,128)(2,1)S(1)}, u32[]{:S(2)}, u32[]{:S(2)}) %all-to-all-start.1) | async-done | bytes 1048608 | tf_op jit(solution)/shard_map/all_to_all | solution.py:100
  59.2 1.3 convert_reduce_fusion.1
  61.1 0.9 fusion.102
  62.1 0.9 fusion.104
  63.1 0.9 fusion.100
  64.0 1.3 fusion.70
  65.4 3.6 %fusion.108 = (f32[16,8,128]{2,1,0:T(8,128)S(1)}, f32[16,8,128,128]{2,3,1,0:T(8,128)S(1)}) fusion(f32[16,8,128,128]{2,3,1,0:T(8,128)S(1)} %fusion.70, pred[8,128]{1,0:T(8,128)(4,1)S(1)} %iota_compare_fusion.19), kind=kOutput, calls=%fused_computation.161 | output fusion | flops 12583039 | bytes 16843776 | tf_op jit(solution)/shard_map/sub | solution.py:44
  69.0 1.2 fusion.53
  70.2 0.8 convert_reduce_fusion
  71.6 7.4 %fusion.33 = bf16[1024,512]{1,0:T(8,128)(2,1)} fusion(bf16[1024,512]{1,0:T(8,128)(2,1)S(1)} %get-tuple-element.20, bf16[2048,512]{1,0:T(8,128)(2,1)S(1)} %copy-done, bf16[512,2048]{1,0:T(8,128)(2,1)} %param.14, f32[1024]{0:T(1024)S(1)} %add_rsqrt_fusion.1, f32[1024]{0:T(1024)S(1)} %broadcast_multiply_fusion.1), kind=kOutput, calls=%fused_computation.46 | convolution fusion | flops 4317511680 | bytes 6299648 | tf_op jit(solution)/shard_map/dot_general | solution.py:62
  79.0 2.5 %copy.122 = bf16[8,16,8,512]{3,1,0,2:T(8,128)(2,1)} copy(bf16[8,16,8,512]{3,2,1,0:T(8,128)(2,1)} %bitcast.192) | data formatting | bytes 2097152 | tf_op jit(solution)/shard_map/reshape | solution.py:124
  81.5 4.3 %all-to-all-start.2 = ((bf16[8,16,8,512]{3,1,0,2:T(8,128)(2,1)}), bf16[8,16,8,512]{3,1,0,2:T(8,128)(2,1)S(1)}, u32[]{:S(2)}, u32[]{:S(2)}) async-start(bf16[8,16,8,512]{3,1,0,2:T(8,128)(2,1)} %copy.122), calls=%async_computation.2 | async-start | bytes 2097152 | tf_op jit(solution)/shard_map/all_to_all | solution.py:123
  85.8 2.6 %copy.126 = bf16[512,1536]{0,1:T(8,128)(2,1)} copy(bf16[512,1536]{1,0:T(8,128)(2,1)} %param.16) | data formatting | bytes 3145728 | tf_op args[7]
  88.9 2.3 %fusion.106 = (bf16[512,1,16,32]{0,3,2,1:T(8,128)(2,1)S(1)}, bf16[512,1,16,32]{0,3,2,1:T(8,128)(2,1)S(1)}, bf16[512,1,16,32]{0,3,2,1:T(8,128)(2,1)}) fusion(bf16[512,3,16,32]{0,3,2,1:T(8,128)(2,1)} %bitcast.182), kind=kLoop, calls=%fused_computation.159 | loop fusion | bytes 3145728 | tf_op jit(solution)/shard_map/slice | solution.py:35
  91.3 10.5 %all-to-all-done.2 = bf16[8,16,8,512]{3,1,0,2:T(8,128)(2,1)S(1)} async-done(((bf16[8,16,8,512]{3,1,0,2:T(8,128)(2,1)}), bf16[8,16,8,512]{3,1,0,2:T(8,128)(2,1)S(1)}, u32[]{:S(2)}, u32[]{:S(2)}) %all-to-all-start.2) | async-done | bytes 1048608 | tf_op jit(solution)/shard_map/all_to_all | solution.py:123
  103.7 0.7 fusion.111
  105.2 1.3 fusion.63
  106.5 3.5 %fusion.109 = (f32[16,8,128]{2,1,0:T(8,128)S(1)}, f32[16,8,128,128]{2,3,1,0:T(8,128)S(1)}) fusion(f32[16,8,128,128]{2,3,1,0:T(8,128)S(1)} %fusion.63, pred[8,128]{1,0:T(8,128)(4,1)S(1)} %broadcast_compare_fusion), kind=kOutput, calls=%fused_computation.162 | output fusion | flops 12583039 | bytes 16843776 | tf_op jit(solution)/shard_map/sub | solution.py:44
  110.0 1.2 fusion.54
  111.3 0.9 copy-done.8
  113.6 18.4 %all_to_all.54 = bf16[8,128,1,512]{3,0,2,1:T(8,128)(2,1)S(1)} all-to-all(bf16[8,128,1,512]{3,0,2,1:T(8,128)(2,1)S(1)} %copy.132), channel_id=1, replica_groups=mesh['win'=32,'grp'=8] {'grp'}, dimensions={1} | all-to-all | bytes 2097152 | tf_op jit(solution)/shard_map/all_to_all | solution.py:142
  132.9 1.3 fusion.48
  134.2 33.2 %all_to_all.55 = bf16[32,32,512]{2,1,0:T(8,128)(2,1)S(1)} all-to-all(bf16[32,32,512]{2,1,0:T(8,128)(2,1)S(1)} %bitcast.196), channel_id=1, replica_groups=mesh['win'=32,'grp'=8] {'win'}, dimensions={0} | all-to-all | bytes 2097152 | tf_op jit(solution)/shard_map/all_to_all | solution.py:146
  167.4 1.6 fusion.56
  (67 shorter events, 13.0 us)
Async XLA Ops:
  0.0 71.6 %copy-start = (bf16[2048,512]{1,0:T(8,128)(2,1)S(1)}, bf16[2048,512]{1,0:T(8,128)(2,1)}, u32[]{:S(2)}) copy-start(bf16[2048,512]{1,0:T(8,128)(2,1)} %param.15) | copy-start | bytes 6291460
  6.7 19.9 %all-to-all-start = ((s32[32,1,32]{2,1,0:T(1,128)}), s32[32,1,32]{2,1,0:T(1,128)S(1)}, u32[]{:S(2)}, u32[]{:S(2)}) async-start(s32[32,1,32]{2,1,0:T(1,128)} %sub.85), calls=%async_computation | async-start | bytes 32768 | tf_op jit(solution)/shard_map/all_to_all | solution.py:112
  26.7 32.5 %all-to-all-start.1 = ((bf16[32,32,512]{2,1,0:T(8,128)(2,1)}), bf16[32,32,512]{2,1,0:T(8,128)(2,1)S(1)}, u32[]{:S(2)}, u32[]{:S(2)}) async-start(bf16[32,32,512]{2,1,0:T(8,128)(2,1)} %bitcast.191), calls=%async_computation.1 | async-start | bytes 2097152 | tf_op jit(solution)/shard_map/all_to_all | solution.py:100
  31.7 2.6 %copy-start.6 = (s32[8,32,8]{1,2,0:T(8,128)S(1)}, s32[8,32,8]{1,2,0:T(8,128)}, u32[]{:S(2)}) copy-start(s32[8,32,8]{1,2,0:T(8,128)} %param.11) | copy-start | bytes 24580
  59.2 1.9 %copy-start.5 = (bf16[512,1,16,32]{0,3,2,1:T(8,128)(2,1)S(1)}, bf16[512,1,16,32]{0,3,2,1:T(8,128)(2,1)}, u32[]{:S(2)}) copy-start(bf16[512,1,16,32]{0,3,2,1:T(8,128)(2,1)} %get-tuple-element.11) | copy-start | bytes 1572868
  61.1 1.0 copy-start.4
  62.1 1.1 copy-start.3
  69.0 1.2 copy-start.7
  81.5 20.2 %all-to-all-start.2 = ((bf16[8,16,8,512]{3,1,0,2:T(8,128)(2,1)}), bf16[8,16,8,512]{3,1,0,2:T(8,128)(2,1)S(1)}, u32[]{:S(2)}, u32[]{:S(2)}) async-start(bf16[8,16,8,512]{3,1,0,2:T(8,128)(2,1)} %copy.122), calls=%async_computation.2 | async-start | bytes 2097152 | tf_op jit(solution)/shard_map/all_to_all | solution.py:123
  101.8 1.2 copy-start.2
  111.2 1.1 copy-start.8
  134.2 34.8 %copy-start.1 = (bf16[2048,512]{1,0:T(8,128)(2,1)S(1)}, bf16[2048,512]{1,0:T(8,128)(2,1)}, u32[]{:S(2)}) copy-start(bf16[2048,512]{1,0:T(8,128)(2,1)} %param.15) | copy-start | bytes 6291460

commit v5 on v4

--- a/solution.py
+++ b/solution.py
@@ -9,6 +9,8 @@
 
 EPSILON = 1e-05
 MASKED = -1e30
+SLOT_BASE = 32
+TAIL = 128
 
 
 def normalize(row_data):
@@ -97,7 +99,6 @@
     buffer_ids = jnp.arange(buffer_rows, dtype=jnp.int32)
     send_hot = (buffer_ids[:, None] == send_place[None, :]).astype(jnp.bfloat16)
     outgoing = place(send_hot, rows_x)
-    arrived = lax.all_to_all(outgoing, "win", split_axis=0, concat_axis=0, tiled=True)
 
     window_ends = jnp.cumsum(column_counts, axis=1)
     starts = window_ends - column_counts
@@ -108,10 +109,19 @@
     block_ids = jnp.arange(blocks, dtype=jnp.int32)
     block_pick = (window[:, None] == block_ids[None, :]).astype(jnp.int32)
     dest_slot = window * WINDOW_SLOTS + offset - jnp.sum(block_pick * owner_starts, axis=1)
-    outgoing_slot = jnp.sum(send_hot.astype(jnp.int32) * (dest_slot[None, :] + 1), axis=1) - 1
-    arrived_slot = lax.all_to_all(
-        outgoing_slot.reshape(owner_count, capacity), "win", split_axis=0, concat_axis=0, tiled=True
+    slot_code = jnp.sum(send_hot.astype(jnp.int32) * (dest_slot[None, :] + 1), axis=1)
+    slot_code = slot_code.reshape(owner_count, capacity)
+    code_tail = jnp.concatenate(
+        [slot_code // SLOT_BASE, slot_code % SLOT_BASE], axis=1
+    ).astype(jnp.bfloat16)
+    code_tail = jnp.pad(code_tail, ((0, 0), (0, TAIL - 2 * capacity)))
+    sending = jnp.concatenate(
+        [outgoing.reshape(owner_count, capacity * model_dim), code_tail], axis=1
     )
+    receiving = lax.all_to_all(sending, "win", split_axis=0, concat_axis=0, tiled=True)
+    arrived = receiving[:, : capacity * model_dim].reshape(buffer_rows, model_dim)
+    code_back = receiving[:, capacity * model_dim :].astype(jnp.int32)
+    arrived_slot = code_back[:, :capacity] * SLOT_BASE + code_back[:, capacity : 2 * capacity] - 1
     own_counts = lax.dynamic_index_in_dim(column_counts, win_index, 0, keepdims=False)
     slot_ids = jnp.arange(slots_all, dtype=jnp.int32)
     recv_hot = (slot_ids[:, None] == arrived_slot.reshape(1, buffer_rows)).astype(jnp.bfloat16)

time: 170 us -> 175 us (1.029)
  local copies, waits for them, and re-layouts: 18.5 us -> 28.5 us
  starting transfers between devices: 20.7 us -> 15.7 us
  waiting for transfers between devices: 37.1 us -> 34 us
  other arithmetic: 14.9 us -> 17.8 us
    unnamed x20 -> x23, local copies, waits for them, and re-layouts: 6.35 us -> 14.3 us
    all_to_all x2 -> x1, starting transfers between devices: 16.3 us -> 11.3 us  [on_device(): lax.all_to_all(sending, 'win', split_axis=0, concat_axis=0, tiled=True)]
    all_to_all x2 -> x1, waiting for transfers between devices: 26.6 us -> 23.4 us  [on_device(): lax.all_to_all(sending, 'win', split_axis=0, concat_axis=0, tiled=True)]
    reshape x0 -> x3, local copies, waits for them, and re-layouts: none -> 2.72 us  [the longest x1 1.33 us: on_device(): outgoing.reshape(owner_count, capacity * model_dim)]
    all_to_all x1 -> x2, other arithmetic: 0.73 us -> 3.4 us  [on_device(): lax.all_to_all(sending, 'win', split_axis=0, concat_axis=0, tiled=True)]
  transfers between devices with their start and end apart: 3 -> 2, of which waited for: 3 -> 2; matrix products, arithmetic and copies ran while one was open for 9% -> 6% of each run, Pallas kernels for 0% -> 0%
where the time goes in v5:
time: 175 us; the launch traced here: 174 us
  blocking collectives  51.7 us (30%)
  waiting for transfers between devices  34 us (19%)
  local copies, waits for them, and re-layouts  28.5 us (16%)
  matrix products  26.2 us (15%)
  other arithmetic  17.8 us (10%)
  starting transfers between devices  15.7 us (9%)
    all_to_all x1, blocking collectives, on_device(): lax.all_to_all(returning, 'win', split_axis=0, concat_axis=0, tiled=True)  33.3 us
    all_to_all x1, waiting for transfers between devices, on_device(): lax.all_to_all(sending, 'win', split_axis=0, concat_axis=0, tiled=True)  23.4 us
    all_to_all x1, blocking collectives, on_device(): lax.all_to_all(mixed_rows, 'grp', split_axis=1, concat_axis=2, tiled=True)  18.4 us
    unnamed x23, local copies, waits for them, and re-layouts  14.3 us
    all_to_all x1, starting transfers between devices, on_device(): lax.all_to_all(sending, 'win', split_axis=0, concat_axis=0, tiled=True)  11.3 us
    all_to_all x1, waiting for transfers between devices, on_device(): lax.all_to_all(first_pad.reshape(blocks, dilation_stride, group_count, mo...  10.6 us
    dot_general x1, matrix products, feed_forward(): jnp.dot(hidden, w_down, preferred_element_type=jnp.float32)  7.4 us
    sub x2, other arithmetic, attention_block(): weights = jnp.exp(scores - row_max)  7.12 us
  transfers between devices with their start and end apart: 2, of which 2 were waited for; matrix products, arithmetic and copies ran while one was open for 6% of the time, Pallas kernels for 0%

profile of v5, /device:TPU:32, one launch (start us, length us, event | category | flops | bytes accessed | tf_op | source)
XLA Modules:
  0.0 174.1 jit_solution(4036967064676253309)
XLA Ops:
  3.1 1.2 reduce-window.6
  6.1 1.8 %fusion.46 = bf16[1024,512]{1,0:T(8,128)(2,1)S(1)} fusion(s32[512]{0:T(512)S(1)} %get-tuple-element.26, bf16[1,1,512,512]{3,2,1,0:T(8,128)(2,1)} %param.9), kind=kOutput, calls=%fused_computation.63 | convolution fusion | flops 537919488 | bytes 1574912 | tf_op jit(solution)/shard_map/dot_general | solution.py:69
  7.9 1.3 reshape.387
  9.3 1.3 maximum_bitcast_fusion
  11.1 2.1 %reduce.6 = bf16[32,16512]{1,0:T(8,128)(2,1)} reduce(bf16[32,1,16512]{2,0,1:T(8,128)(2,1)S(1)} %maximum_bitcast_fusion, bf16[]{:T(256)} %broadcast.377), dimensions={1}, to_apply=%copy.117.reduce_sub_computation | reduce | bytes 2113538 | tf_op jit(solution)/shard_map/all_to_all | solution.py:121
  13.2 2.6 %reshape.425 = bf16[32,2,8256]{2,1,0:T(2,128)(2,1)} reshape(bf16[32,16512]{1,0:T(8,128)(2,1)} %reduce.6) | data formatting | bytes 2113536
  15.9 11.3 %all-to-all-start = ((bf16[32,2,8256]{2,1,0:T(2,128)(2,1)}), bf16[32,2,8256]{2,1,0:T(2,128)(2,1)S(1)}, u32[]{:S(2)}, u32[]{:S(2)}) async-start(bf16[32,2,8256]{2,1,0:T(2,128)(2,1)} %reshape.425), calls=%async_computation | async-start | bytes 2129920 | tf_op jit(solution)/shard_map/all_to_all | solution.py:121
  27.2 2.6 %copy.118 = bf16[512,1536]{0,1:T(8,128)(2,1)} copy(bf16[512,1536]{1,0:T(8,128)(2,1)} %param.12) | data formatting | bytes 3145728 | tf_op args[3]
  30.1 2.5 %fusion.115 = (bf16[512,1,16,32]{0,3,2,1:T(8,128)(2,1)}, bf16[512,1,16,32]{0,3,2,1:T(8,128)(2,1)}, bf16[512,1,16,32]{0,3,2,1:T(8,128)(2,1)}) fusion(bf16[512,3,16,32]{0,3,2,1:T(8,128)(2,1)} %bitcast.184), kind=kLoop, calls=%fused_computation.179 | loop fusion | bytes 3145728 | tf_op jit(solution)/shard_map/slice | solution.py:37
  32.7 23.4 %all-to-all-done = bf16[32,2,8256]{2,1,0:T(2,128)(2,1)S(1)} async-done(((bf16[32,2,8256]{2,1,0:T(2,128)(2,1)}), bf16[32,2,8256]{2,1,0:T(2,128)(2,1)S(1)}, u32[]{:S(2)}, u32[]{:S(2)}) %all-to-all-start) | async-done | bytes 1056800 | tf_op jit(solution)/shard_map/all_to_all | solution.py:121
  56.1 3.6 %reshape.426 = bf16[32,1,16512]{2,1,0:T(2,128)(2,1)} reshape(bf16[32,2,8256]{2,1,0:T(2,128)(2,1)S(1)} %all-to-all-done) | data formatting | bytes 2113536
  59.7 1.7 copy.191
  61.5 1.3 reshape.389
  63.0 2.6 %convert_reduce_fusion.1 = (f32[1024]{0:T(1024)S(1)}, bf16[1024,512]{1,0:T(8,128)(2,1)S(1)}) fusion(bf16[1024,512]{1,0:T(8,128)(2,1)} %reshape.389, s32[1024]{0:T(1024)S(1)} %eq.83), kind=kOutput, calls=%fused_computation.36 | convolution fusion | flops 1076362240 | bytes 2105344 | tf_op jit(solution)/shard_map/dot_general | solution.py:69
  66.2 0.9 fusion.112
  69.1 1.3 fusion.70
  70.4 3.6 %fusion.116 = (f32[16,8,128]{2,1,0:T(8,128)S(1)}, f32[16,8,128,128]{2,3,1,0:T(8,128)S(1)}) fusion(f32[16,8,128,128]{2,3,1,0:T(8,128)S(1)} %fusion.70, pred[8,128]{1,0:T(8,128)(4,1)S(1)} %iota_compare_fusion.20), kind=kOutput, calls=%fused_computation.180 | output fusion | flops 12583039 | bytes 16843776 | tf_op jit(solution)/shard_map/sub | solution.py:46
  74.1 1.2 fusion.53
  76.7 7.4 %fusion.33 = bf16[1024,512]{1,0:T(8,128)(2,1)} fusion(bf16[1024,512]{1,0:T(8,128)(2,1)S(1)} %get-tuple-element.22, bf16[2048,512]{1,0:T(8,128)(2,1)S(1)} %copy-done, bf16[512,2048]{1,0:T(8,128)(2,1)} %param.14, f32[1024]{0:T(1024)S(1)} %add_rsqrt_fusion.1, f32[1024]{0:T(1024)S(1)} %broadcast_multiply_fusion.1), kind=kOutput, calls=%fused_computation.46 | convolution fusion | flops 4317511680 | bytes 6299648 | tf_op jit(solution)/shard_map/dot_general | solution.py:64
  84.1 2.5 %copy.124 = bf16[8,16,8,512]{3,1,0,2:T(8,128)(2,1)} copy(bf16[8,16,8,512]{3,2,1,0:T(8,128)(2,1)} %bitcast.195) | data formatting | bytes 2097152 | tf_op jit(solution)/shard_map/reshape | solution.py:134
  86.6 4.3 %all-to-all-start.1 = ((bf16[8,16,8,512]{3,1,0,2:T(8,128)(2,1)}), bf16[8,16,8,512]{3,1,0,2:T(8,128)(2,1)S(1)}, u32[]{:S(2)}, u32[]{:S(2)}) async-start(bf16[8,16,8,512]{3,1,0,2:T(8,128)(2,1)} %copy.124), calls=%async_computation.1 | async-start | bytes 2097152 | tf_op jit(solution)/shard_map/all_to_all | solution.py:133
  90.9 2.6 %copy.128 = bf16[512,1536]{0,1:T(8,128)(2,1)} copy(bf16[512,1536]{1,0:T(8,128)(2,1)} %param.16) | data formatting | bytes 3145728 | tf_op args[7]
  94.0 2.3 %fusion.114 = (bf16[512,1,16,32]{0,3,2,1:T(8,128)(2,1)S(1)}, bf16[512,1,16,32]{0,3,2,1:T(8,128)(2,1)S(1)}, bf16[512,1,16,32]{0,3,2,1:T(8,128)(2,1)}) fusion(bf16[512,3,16,32]{0,3,2,1:T(8,128)(2,1)} %bitcast.185), kind=kLoop, calls=%fused_computation.178 | loop fusion | bytes 3145728 | tf_op jit(solution)/shard_map/slice | solution.py:37
  96.2 10.6 %all-to-all-done.1 = bf16[8,16,8,512]{3,1,0,2:T(8,128)(2,1)S(1)} async-done(((bf16[8,16,8,512]{3,1,0,2:T(8,128)(2,1)}), bf16[8,16,8,512]{3,1,0,2:T(8,128)(2,1)S(1)}, u32[]{:S(2)}, u32[]{:S(2)}) %all-to-all-start.1) | async-done | bytes 1048608 | tf_op jit(solution)/shard_map/all_to_all | solution.py:133
  110.2 1.3 fusion.63
  111.5 3.5 %fusion.117 = (f32[16,8,128]{2,1,0:T(8,128)S(1)}, f32[16,8,128,128]{2,3,1,0:T(8,128)S(1)}) fusion(f32[16,8,128,128]{2,3,1,0:T(8,128)S(1)} %fusion.63, pred[8,128]{1,0:T(8,128)(4,1)S(1)} %broadcast_compare_fusion), kind=kOutput, calls=%fused_computation.181 | output fusion | flops 12583039 | bytes 16843776 | tf_op jit(solution)/shard_map/sub | solution.py:46
  115.0 1.2 fusion.54
  116.3 0.9 copy-done.8
  118.6 18.4 %all_to_all.48 = bf16[8,128,1,512]{3,0,2,1:T(8,128)(2,1)S(1)} all-to-all(bf16[8,128,1,512]{3,0,2,1:T(8,128)(2,1)S(1)} %copy.134), channel_id=1, replica_groups=mesh['win'=32,'grp'=8] {'grp'}, dimensions={1} | all-to-all | bytes 2097152 | tf_op jit(solution)/shard_map/all_to_all | solution.py:152
  137.9 1.3 fusion.48
  139.2 33.3 %all_to_all.49 = bf16[32,32,512]{2,1,0:T(8,128)(2,1)S(1)} all-to-all(bf16[32,32,512]{2,1,0:T(8,128)(2,1)S(1)} %bitcast.199), channel_id=1, replica_groups=mesh['win'=32,'grp'=8] {'win'}, dimensions={0} | all-to-all | bytes 2097152 | tf_op jit(solution)/shard_map/all_to_all | solution.py:156
  172.5 1.6 fusion.56
  (75 shorter events, 16.1 us)
Async XLA Ops:
  0.0 76.7 %copy-start = (bf16[2048,512]{1,0:T(8,128)(2,1)S(1)}, bf16[2048,512]{1,0:T(8,128)(2,1)}, u32[]{:S(2)}) copy-start(bf16[2048,512]{1,0:T(8,128)(2,1)} %param.15) | copy-start | bytes 6291460
  15.9 40.2 %all-to-all-start = ((bf16[32,2,8256]{2,1,0:T(2,128)(2,1)}), bf16[32,2,8256]{2,1,0:T(2,128)(2,1)S(1)}, u32[]{:S(2)}, u32[]{:S(2)}) async-start(bf16[32,2,8256]{2,1,0:T(2,128)(2,1)} %reshape.425), calls=%async_computation | async-start | bytes 2129920 | tf_op jit(solution)/shard_map/all_to_all | solution.py:121
  27.2 2.6 %copy-start.6 = (s32[8,32,8]{1,2,0:T(8,128)S(1)}, s32[8,32,8]{1,2,0:T(8,128)}, u32[]{:S(2)}) copy-start(s32[8,32,8]{1,2,0:T(8,128)} %param.11) | copy-start | bytes 24580
  63.0 3.2 %copy-start.5 = (bf16[512,1,16,32]{0,3,2,1:T(8,128)(2,1)S(1)}, bf16[512,1,16,32]{0,3,2,1:T(8,128)(2,1)}, u32[]{:S(2)}) copy-start(bf16[512,1,16,32]{0,3,2,1:T(8,128)(2,1)} %get-tuple-element.12) | copy-start | bytes 1572868
  66.1 1.0 copy-start.4
  67.1 1.1 copy-start.3
  74.1 1.2 copy-start.7
  86.6 20.2 %all-to-all-start.1 = ((bf16[8,16,8,512]{3,1,0,2:T(8,128)(2,1)}), bf16[8,16,8,512]{3,1,0,2:T(8,128)(2,1)S(1)}, u32[]{:S(2)}, u32[]{:S(2)}) async-start(bf16[8,16,8,512]{3,1,0,2:T(8,128)(2,1)} %copy.124), calls=%async_computation.1 | async-start | bytes 2097152 | tf_op jit(solution)/shard_map/all_to_all | solution.py:133
  106.8 1.2 copy-start.2
  116.2 1.1 copy-start.8
  139.2 34.9 %copy-start.1 = (bf16[2048,512]{1,0:T(8,128)(2,1)S(1)}, bf16[2048,512]{1,0:T(8,128)(2,1)}, u32[]{:S(2)}) copy-start(bf16[2048,512]{1,0:T(8,128)(2,1)} %param.15) | copy-start | bytes 6291460

commit v6 on v4

--- a/solution.py
+++ b/solution.py
@@ -9,6 +9,8 @@
 
 EPSILON = 1e-05
 MASKED = -1e30
+SLOT_BASE = 32
+TAIL = 128
 
 
 def normalize(row_data):
@@ -96,8 +98,6 @@
     send_place = owner_dev * capacity + peer_order
     buffer_ids = jnp.arange(buffer_rows, dtype=jnp.int32)
     send_hot = (buffer_ids[:, None] == send_place[None, :]).astype(jnp.bfloat16)
-    outgoing = place(send_hot, rows_x)
-    arrived = lax.all_to_all(outgoing, "win", split_axis=0, concat_axis=0, tiled=True)
 
     window_ends = jnp.cumsum(column_counts, axis=1)
     starts = window_ends - column_counts
@@ -108,10 +108,24 @@
     block_ids = jnp.arange(blocks, dtype=jnp.int32)
     block_pick = (window[:, None] == block_ids[None, :]).astype(jnp.int32)
     dest_slot = window * WINDOW_SLOTS + offset - jnp.sum(block_pick * owner_starts, axis=1)
-    outgoing_slot = jnp.sum(send_hot.astype(jnp.int32) * (dest_slot[None, :] + 1), axis=1) - 1
-    arrived_slot = lax.all_to_all(
-        outgoing_slot.reshape(owner_count, capacity), "win", split_axis=0, concat_axis=0, tiled=True
-    )
+    slot_code = dest_slot + 1
+    tail_ids = jnp.arange(TAIL, dtype=jnp.int32)
+    code_cols = jnp.where(
+        tail_ids[None, :] == 0,
+        (slot_code // SLOT_BASE)[:, None],
+        jnp.where(tail_ids[None, :] == 1, (slot_code % SLOT_BASE)[:, None], 0),
+    ).astype(jnp.bfloat16)
+    outgoing = place(send_hot, jnp.concatenate([rows_x, code_cols], axis=1))
+    receiving = lax.all_to_all(
+        outgoing.reshape(owner_count, capacity, model_dim + TAIL),
+        "win",
+        split_axis=0,
+        concat_axis=0,
+        tiled=True,
+    ).reshape(buffer_rows, model_dim + TAIL)
+    arrived = receiving[:, :model_dim]
+    code_back = receiving[:, model_dim:].astype(jnp.int32)
+    arrived_slot = code_back[:, 0] * SLOT_BASE + code_back[:, 1] - 1
     own_counts = lax.dynamic_index_in_dim(column_counts, win_index, 0, keepdims=False)
     slot_ids = jnp.arange(slots_all, dtype=jnp.int32)
     recv_hot = (slot_ids[:, None] == arrived_slot.reshape(1, buffer_rows)).astype(jnp.bfloat16)

time: 170 us -> 165 us (0.971)
  starting transfers between devices: 20.7 us -> 15.7 us
  waiting for transfers between devices: 37.1 us -> 39 us
    all_to_all x2 -> x1, starting transfers between devices: 16.3 us -> 11.4 us  [on_device(): lax.all_to_all(outgoing.reshape(owner_count, capacity, model_dim + TAIL),...]
    all_to_all x2 -> x1, waiting for transfers between devices: 26.6 us -> 28.5 us  [on_device(): lax.all_to_all(outgoing.reshape(owner_count, capacity, model_dim + TAIL),...]
  transfers between devices with their start and end apart: 3 -> 2, of which waited for: 3 -> 2; matrix products, arithmetic and copies ran while one was open for 9% -> 7% of each run, Pallas kernels for 0% -> 0%
where the time goes in v6:
time: 165 us
  blocking collectives  51.9 us (31%)
  waiting for transfers between devices  39 us (24%)
  matrix products  26.3 us (16%)
  local copies, waits for them, and re-layouts  17.2 us (10%)
  starting transfers between devices  15.7 us (10%)
  other arithmetic  14.3 us (9%)
    all_to_all x1, blocking collectives, on_device(): lax.all_to_all(returning, 'win', split_axis=0, concat_axis=0, tiled=True)  33.5 us
    all_to_all x1, waiting for transfers between devices, on_device(): lax.all_to_all(outgoing.reshape(owner_count, capacity, model_dim + TAIL),...  28.5 us
    all_to_all x1, blocking collectives, on_device(): lax.all_to_all(mixed_rows, 'grp', split_axis=1, concat_axis=2, tiled=True)  18.4 us
    all_to_all x1, starting transfers between devices, on_device(): lax.all_to_all(outgoing.reshape(owner_count, capacity, model_dim + TAIL),...  11.4 us
    all_to_all x1, waiting for transfers between devices, on_device(): lax.all_to_all(first_pad.reshape(blocks, dilation_stride, group_count, mo...  10.5 us
    dot_general x1, matrix products, feed_forward(): jnp.dot(hidden, w_down, preferred_element_type=jnp.float32)  7.41 us
    sub x2, other arithmetic, attention_block(): weights = jnp.exp(scores - row_max)  7.12 us
    unnamed x20, local copies, waits for them, and re-layouts  6.35 us
  transfers between devices with their start and end apart: 2, of which 2 were waited for; matrix products, arithmetic and copies ran while one was open for 7% of the time, Pallas kernels for 0%

profile of v6, /device:TPU:32, one launch (start us, length us, event | category | flops | bytes accessed | tf_op | source)
XLA Modules:
  0.0 164.7 jit_solution(1477481710247207009)
XLA Ops:
  0.0 0.8 dynamic-slice_bitcast_fusion
  4.0 1.2 reduce-window.6
  5.8 3.1 %fusion.45 = bf16[1024,640]{1,0:T(8,128)(2,1)} fusion(s32[512]{0:T(512)S(1)} %multiply_add_fusion, bf16[512,128]{1,0:T(8,128)(2,1)S(1)} %select_convert_fusion, bf16[512,512]{1,0:T(8,128)(2,1)} %bitcast.203), kind=kOutput, calls=%fused_computation.61 | convolution fusion | flops 673579008 | bytes 1968128 | tf_op jit(solution)/shard_map/dot_general | solution.py:69
  8.9 11.4 %all-to-all-start = ((bf16[32,32,640]{2,1,0:T(8,128)(2,1)}), bf16[32,32,640]{2,1,0:T(8,128)(2,1)S(1)}, u32[]{:S(2)}, u32[]{:S(2)}) async-start(bf16[32,32,640]{2,1,0:T(8,128)(2,1)} %bitcast.189), calls=%async_computation | async-start | bytes 2621440 | tf_op jit(solution)/shard_map/all_to_all | solution.py:119
  20.3 2.6 %copy.117 = bf16[512,1536]{0,1:T(8,128)(2,1)} copy(bf16[512,1536]{1,0:T(8,128)(2,1)} %param.12) | data formatting | bytes 3145728 | tf_op args[3]
  23.2 2.6 %fusion.113 = (bf16[512,1,16,32]{0,3,2,1:T(8,128)(2,1)}, bf16[512,1,16,32]{0,3,2,1:T(8,128)(2,1)}, bf16[512,1,16,32]{0,3,2,1:T(8,128)(2,1)}) fusion(bf16[512,3,16,32]{0,3,2,1:T(8,128)(2,1)} %bitcast.178), kind=kLoop, calls=%fused_computation.177 | loop fusion | bytes 3145728 | tf_op jit(solution)/shard_map/slice | solution.py:37
  25.7 28.5 %all-to-all-done = bf16[32,32,640]{2,1,0:T(8,128)(2,1)S(1)} async-done(((bf16[32,32,640]{2,1,0:T(8,128)(2,1)}), bf16[32,32,640]{2,1,0:T(8,128)(2,1)S(1)}, u32[]{:S(2)}, u32[]{:S(2)}) %all-to-all-start) | async-done | bytes 1310752 | tf_op jit(solution)/shard_map/all_to_all | solution.py:119
  54.6 1.3 convert_reduce_fusion.1
  56.5 0.9 fusion.108
  57.6 0.9 fusion.110
  58.5 0.9 fusion.106
  59.5 1.3 fusion.69
  60.8 3.6 %fusion.114 = (f32[16,8,128]{2,1,0:T(8,128)S(1)}, f32[16,8,128,128]{2,3,1,0:T(8,128)S(1)}) fusion(f32[16,8,128,128]{2,3,1,0:T(8,128)S(1)} %fusion.69, pred[8,128]{1,0:T(8,128)(4,1)S(1)} %iota_compare_fusion.19), kind=kOutput, calls=%fused_computation.178 | output fusion | flops 12583039 | bytes 16843776 | tf_op jit(solution)/shard_map/sub | solution.py:46
  64.4 1.2 fusion.52
  65.6 0.8 convert_reduce_fusion
  67.0 7.4 %fusion.33 = bf16[1024,512]{1,0:T(8,128)(2,1)} fusion(bf16[1024,512]{1,0:T(8,128)(2,1)S(1)} %get-tuple-element.22, bf16[2048,512]{1,0:T(8,128)(2,1)S(1)} %copy-done, bf16[512,2048]{1,0:T(8,128)(2,1)} %param.14, f32[1024]{0:T(1024)S(1)} %add_rsqrt_fusion.1, f32[1024]{0:T(1024)S(1)} %broadcast_multiply_fusion.1), kind=kOutput, calls=%fused_computation.46 | convolution fusion | flops 4317511680 | bytes 6299648 | tf_op jit(solution)/shard_map/dot_general | solution.py:64
  74.5 2.5 %copy.123 = bf16[8,16,8,512]{3,1,0,2:T(8,128)(2,1)} copy(bf16[8,16,8,512]{3,2,1,0:T(8,128)(2,1)} %bitcast.190) | data formatting | bytes 2097152 | tf_op jit(solution)/shard_map/reshape | solution.py:138
  77.0 4.3 %all-to-all-start.1 = ((bf16[8,16,8,512]{3,1,0,2:T(8,128)(2,1)}), bf16[8,16,8,512]{3,1,0,2:T(8,128)(2,1)S(1)}, u32[]{:S(2)}, u32[]{:S(2)}) async-start(bf16[8,16,8,512]{3,1,0,2:T(8,128)(2,1)} %copy.123), calls=%async_computation.1 | async-start | bytes 2097152 | tf_op jit(solution)/shard_map/all_to_all | solution.py:137
  81.3 2.6 %copy.127 = bf16[512,1536]{0,1:T(8,128)(2,1)} copy(bf16[512,1536]{1,0:T(8,128)(2,1)} %param.16) | data formatting | bytes 3145728 | tf_op args[7]
  84.3 2.3 %fusion.112 = (bf16[512,1,16,32]{0,3,2,1:T(8,128)(2,1)S(1)}, bf16[512,1,16,32]{0,3,2,1:T(8,128)(2,1)S(1)}, bf16[512,1,16,32]{0,3,2,1:T(8,128)(2,1)}) fusion(bf16[512,3,16,32]{0,3,2,1:T(8,128)(2,1)} %bitcast.179), kind=kLoop, calls=%fused_computation.176 | loop fusion | bytes 3145728 | tf_op jit(solution)/shard_map/slice | solution.py:37
  86.7 10.5 %all-to-all-done.1 = bf16[8,16,8,512]{3,1,0,2:T(8,128)(2,1)S(1)} async-done(((bf16[8,16,8,512]{3,1,0,2:T(8,128)(2,1)}), bf16[8,16,8,512]{3,1,0,2:T(8,128)(2,1)S(1)}, u32[]{:S(2)}, u32[]{:S(2)}) %all-to-all-start.1) | async-done | bytes 1048608 | tf_op jit(solution)/shard_map/all_to_all | solution.py:137
  99.1 0.7 fusion.117
  99.8 0.7 fusion.118
  100.6 1.3 fusion.62
  101.9 3.5 %fusion.115 = (f32[16,8,128]{2,1,0:T(8,128)S(1)}, f32[16,8,128,128]{2,3,1,0:T(8,128)S(1)}) fusion(f32[16,8,128,128]{2,3,1,0:T(8,128)S(1)} %fusion.62, pred[8,128]{1,0:T(8,128)(4,1)S(1)} %broadcast_compare_fusion), kind=kOutput, calls=%fused_computation.179 | output fusion | flops 12583039 | bytes 16843776 | tf_op jit(solution)/shard_map/sub | solution.py:46
  105.4 1.2 fusion.53
  106.7 0.9 copy-done.8
  107.7 0.7 fusion.34
  109.0 18.4 %all_to_all.41 = bf16[8,128,1,512]{3,0,2,1:T(8,128)(2,1)S(1)} all-to-all(bf16[8,128,1,512]{3,0,2,1:T(8,128)(2,1)S(1)} %copy.133), channel_id=1, replica_groups=mesh['win'=32,'grp'=8] {'grp'}, dimensions={1} | all-to-all | bytes 2097152 | tf_op jit(solution)/shard_map/all_to_all | solution.py:156
  128.3 1.3 fusion.47
  129.6 33.5 %all_to_all.42 = bf16[32,32,512]{2,1,0:T(8,128)(2,1)S(1)} all-to-all(bf16[32,32,512]{2,1,0:T(8,128)(2,1)S(1)} %bitcast.194), channel_id=1, replica_groups=mesh['win'=32,'grp'=8] {'win'}, dimensions={0} | all-to-all | bytes 2097152 | tf_op jit(solution)/shard_map/all_to_all | solution.py:160
  163.1 1.6 fusion.55
  (64 shorter events, 9.6 us)
Async XLA Ops:
  0.0 67.0 %copy-start = (bf16[2048,512]{1,0:T(8,128)(2,1)S(1)}, bf16[2048,512]{1,0:T(8,128)(2,1)}, u32[]{:S(2)}) copy-start(bf16[2048,512]{1,0:T(8,128)(2,1)} %param.15) | copy-start | bytes 6291460
  8.9 45.3 %all-to-all-start = ((bf16[32,32,640]{2,1,0:T(8,128)(2,1)}), bf16[32,32,640]{2,1,0:T(8,128)(2,1)S(1)}, u32[]{:S(2)}, u32[]{:S(2)}) async-start(bf16[32,32,640]{2,1,0:T(8,128)(2,1)} %bitcast.189), calls=%async_computation | async-start | bytes 2621440 | tf_op jit(solution)/shard_map/all_to_all | solution.py:119
  20.3 2.6 %copy-start.6 = (s32[8,32,8]{1,2,0:T(8,128)S(1)}, s32[8,32,8]{1,2,0:T(8,128)}, u32[]{:S(2)}) copy-start(s32[8,32,8]{1,2,0:T(8,128)} %param.11) | copy-start | bytes 24580
  54.6 1.9 %copy-start.5 = (bf16[512,1,16,32]{0,3,2,1:T(8,128)(2,1)S(1)}, bf16[512,1,16,32]{0,3,2,1:T(8,128)(2,1)}, u32[]{:S(2)}) copy-start(bf16[512,1,16,32]{0,3,2,1:T(8,128)(2,1)} %get-tuple-element.11) | copy-start | bytes 1572868
  56.5 1.0 copy-start.4
  57.5 1.1 copy-start.3
  64.4 1.2 copy-start.7
  77.0 20.2 %all-to-all-start.1 = ((bf16[8,16,8,512]{3,1,0,2:T(8,128)(2,1)}), bf16[8,16,8,512]{3,1,0,2:T(8,128)(2,1)S(1)}, u32[]{:S(2)}, u32[]{:S(2)}) async-start(bf16[8,16,8,512]{3,1,0,2:T(8,128)(2,1)} %copy.123), calls=%async_computation.1 | async-start | bytes 2097152 | tf_op jit(solution)/shard_map/all_to_all | solution.py:137
  97.2 1.2 copy-start.2
  106.6 1.1 copy-start.8
  129.6 35.1 %copy-start.1 = (bf16[2048,512]{1,0:T(8,128)(2,1)S(1)}, bf16[2048,512]{1,0:T(8,128)(2,1)}, u32[]{:S(2)}) copy-start(bf16[2048,512]{1,0:T(8,128)(2,1)} %param.15) | copy-start | bytes 6291460

commit v7 on v6

--- a/solution.py
+++ b/solution.py
@@ -1,7 +1,7 @@
 import jax
 import jax.numpy as jnp
 from jax import lax
-from jax.sharding import PartitionSpec as P
+from jax.sharding import Mesh, PartitionSpec as P
 
 HEAD_DIM = 32
 WINDOW_SLOTS = 128
@@ -9,6 +9,7 @@
 
 EPSILON = 1e-05
 MASKED = -1e30
+WIN_SLOW = 4
 SLOT_BASE = 32
 TAIL = 128
 
@@ -75,10 +76,17 @@
     ).astype(jnp.bfloat16)
 
 
+def exchange_win(rows, capacity):
+    slow, fast = lax.axis_size("win_slow"), lax.axis_size("win_fast")
+    blocks = rows.reshape(slow, fast, capacity, rows.shape[-1])
+    blocks = lax.all_to_all(blocks, "win_fast", split_axis=1, concat_axis=1, tiled=True)
+    return lax.all_to_all(blocks, "win_slow", split_axis=0, concat_axis=0, tiled=True)
+
+
 def on_device(points, rank, counts, w_qkv_one, w_out_one, w_up, w_down, w_qkv_two, w_out_two):
-    owner_count = lax.axis_size("win")
+    owner_count = lax.axis_size("win_slow") * lax.axis_size("win_fast")
     group_count = lax.axis_size("grp")
-    win_index = lax.axis_index("win")
+    win_index = lax.axis_index("win_slow") * lax.axis_size("win_fast") + lax.axis_index("win_fast")
     grp_index = lax.axis_index("grp")
     local_points = points.shape[2]
     model_dim = points.shape[3]
@@ -116,13 +124,7 @@
         jnp.where(tail_ids[None, :] == 1, (slot_code % SLOT_BASE)[:, None], 0),
     ).astype(jnp.bfloat16)
     outgoing = place(send_hot, jnp.concatenate([rows_x, code_cols], axis=1))
-    receiving = lax.all_to_all(
-        outgoing.reshape(owner_count, capacity, model_dim + TAIL),
-        "win",
-        split_axis=0,
-        concat_axis=0,
-        tiled=True,
-    ).reshape(buffer_rows, model_dim + TAIL)
+    receiving = exchange_win(outgoing, capacity).reshape(buffer_rows, model_dim + TAIL)
     arrived = receiving[:, :model_dim]
     code_back = receiving[:, model_dim:].astype(jnp.int32)
     arrived_slot = code_back[:, 0] * SLOT_BASE + code_back[:, 1] - 1
@@ -157,18 +159,25 @@
         slots_all, model_dim
     )
     returning = place_back(recv_hot, second_pad)
-    returned = lax.all_to_all(returning, "win", split_axis=0, concat_axis=0, tiled=True)
+    returned = exchange_win(returning, capacity).reshape(buffer_rows, model_dim)
     encoded = place_back(send_hot, returned)
     return encoded.reshape(1, 1, local_points, model_dim)
 
 
 def solution(mesh):
+    devices = mesh.devices
+    slow = WIN_SLOW
+    split_mesh = Mesh(
+        devices.reshape(slow, devices.shape[0] // slow, devices.shape[1]),
+        ("win_slow", "win_fast", "grp"),
+    )
+    win = ("win_slow", "win_fast")
     return jax.shard_map(
         on_device,
-        mesh=mesh,
+        mesh=split_mesh,
         in_specs=(
-            P("win", "grp", None, None),
-            P("win", "grp", None),
+            P(win, "grp", None, None),
+            P(win, "grp", None),
             P(),
             P(),
             P(),
@@ -177,6 +186,6 @@
             P(),
             P(),
         ),
-        out_specs=P("win", "grp", None, None),
+        out_specs=P(win, "grp", None, None),
         check_vma=False,
     )

time: 165 us -> 197 us (1.19)
  blocking collectives: 51.9 us -> 107 us
  waiting for transfers between devices: 39 us -> 20.7 us
  starting transfers between devices: 15.7 us -> 8.77 us
    all_to_all x1 -> x3, blocking collectives: 33.5 us -> 88.7 us  [the longest x2 73 us: exchange_win(): lax.all_to_all(blocks, 'win_fast', split_axis=1, concat_axis=1, tiled=True)]
    all_to_all x1, waiting for transfers between devices: 28.5 us -> 10.1 us  [exchange_win(): lax.all_to_all(blocks, 'win_slow', split_axis=0, concat_axis=0, tiled=True)]
    all_to_all x1, starting transfers between devices: 11.4 us -> 4.46 us  [exchange_win(): lax.all_to_all(blocks, 'win_slow', split_axis=0, concat_axis=0, tiled=True)]
  transfers between devices with their start and end apart: 2 -> 2, of which waited for: 2 -> 2; matrix products, arithmetic and copies ran while one was open for 7% -> 6% of each run, Pallas kernels for 0% -> 0%
where the time goes in v7:
time: 197 us; the launch traced here: 195 us
  blocking collectives  107 us (54%)
  matrix products  25.2 us (13%)
  waiting for transfers between devices  20.7 us (11%)
  local copies, waits for them, and re-layouts  18.7 us (9%)
  other arithmetic  14.3 us (7%)
  starting transfers between devices  8.77 us (4%)
    all_to_all x2, blocking collectives, exchange_win(): lax.all_to_all(blocks, 'win_fast', split_axis=1, concat_axis=1, tiled=True)  73 us
    all_to_all x1, blocking collectives, on_device(): lax.all_to_all(mixed_rows, 'grp', split_axis=1, concat_axis=2, tiled=True)  18.4 us
    all_to_all x1, blocking collectives, exchange_win(): lax.all_to_all(blocks, 'win_slow', split_axis=0, concat_axis=0, tiled=True)  15.7 us
    all_to_all x1, waiting for transfers between devices, on_device(): lax.all_to_all(first_pad.reshape(blocks, dilation_stride, group_count, mo...  10.5 us
    all_to_all x1, waiting for transfers between devices, exchange_win(): lax.all_to_all(blocks, 'win_slow', split_axis=0, concat_axis=0, tiled=True)  10.1 us
    dot_general x1, matrix products, feed_forward(): jnp.dot(hidden, w_down, preferred_element_type=jnp.float32)  7.41 us
    sub x2, other arithmetic, attention_block(): weights = jnp.exp(scores - row_max)  7.12 us
    unnamed x20, local copies, waits for them, and re-layouts  6.35 us
  transfers between devices with their start and end apart: 2, of which 2 were waited for; matrix products, arithmetic and copies ran while one was open for 6% of the time, Pallas kernels for 0%

profile of v7, /device:TPU:32, one launch (start us, length us, event | category | flops | bytes accessed | tf_op | source)
XLA Modules:
  0.0 195.1 jit_solution(11929214435559007029)
XLA Ops:
  0.0 0.8 dynamic-slice_bitcast_fusion
  3.0 1.2 reduce-window.6
  5.8 2.1 %fusion.45 = bf16[1024,640]{1,0:T(8,128)(2,1)S(1)} fusion(s32[512]{0:T(512)S(1)} %multiply_add_fusion, bf16[512,128]{1,0:T(8,128)(2,1)S(1)} %select_convert_fusion, bf16[512,512]{1,0:T(8,128)(2,1)} %bitcast.203), kind=kOutput, calls=%fused_computation.61 | convolution fusion | flops 673579008 | bytes 1968128 | tf_op jit(solution)/shard_map/dot_general | solution.py:70
  8.0 41.3 %all_to_all.44 = bf16[4,8,32,640]{3,2,0,1:T(8,128)(2,1)S(1)} all-to-all(bf16[4,8,32,640]{3,2,0,1:T(8,128)(2,1)S(1)} %copy.124), channel_id=1, replica_groups=mesh['win_slow'=4,'win_fast'=8,'grp'=8] {'win_fast'}, dimensions={1} | all-to-all | bytes 2621440 | tf_op jit(solution)/shard_map/all_to_all | solution.py:82
  49.3 1.2 copy.125
  50.5 4.5 %all-to-all-start.1 = ((bf16[4,8,32,640]{3,2,1,0:T(8,128)(2,1)}), bf16[4,8,32,640]{3,2,1,0:T(8,128)(2,1)S(1)}, u32[]{:S(2)}, u32[]{:S(2)}) async-start(bf16[4,8,32,640]{3,2,1,0:T(8,128)(2,1)} %copy.125), calls=%async_computation.1 | async-start | bytes 2621440 | tf_op jit(solution)/shard_map/all_to_all | solution.py:83
  54.9 2.6 %copy.126 = bf16[512,1536]{0,1:T(8,128)(2,1)} copy(bf16[512,1536]{1,0:T(8,128)(2,1)} %param.12) | data formatting | bytes 3145728 | tf_op args[3]
  57.8 2.6 %fusion.113 = (bf16[512,1,16,32]{0,3,2,1:T(8,128)(2,1)}, bf16[512,1,16,32]{0,3,2,1:T(8,128)(2,1)}, bf16[512,1,16,32]{0,3,2,1:T(8,128)(2,1)}) fusion(bf16[512,3,16,32]{0,3,2,1:T(8,128)(2,1)} %bitcast.178), kind=kLoop, calls=%fused_computation.177 | loop fusion | bytes 3145728 | tf_op jit(solution)/shard_map/slice | solution.py:38
  60.4 10.1 %all-to-all-done.1 = bf16[4,8,32,640]{3,2,1,0:T(8,128)(2,1)S(1)} async-done(((bf16[4,8,32,640]{3,2,1,0:T(8,128)(2,1)}), bf16[4,8,32,640]{3,2,1,0:T(8,128)(2,1)S(1)}, u32[]{:S(2)}, u32[]{:S(2)}) %all-to-all-start.1) | async-done | bytes 1310752 | tf_op jit(solution)/shard_map/all_to_all | solution.py:83
  70.9 1.3 convert_reduce_fusion.1
  72.9 0.9 fusion.110
  73.9 0.9 fusion.108
  74.8 0.9 fusion.106
  75.8 1.3 fusion.69
  77.1 3.6 %fusion.114 = (f32[16,8,128]{2,1,0:T(8,128)S(1)}, f32[16,8,128,128]{2,3,1,0:T(8,128)S(1)}) fusion(f32[16,8,128,128]{2,3,1,0:T(8,128)S(1)} %fusion.69, pred[8,128]{1,0:T(8,128)(4,1)S(1)} %iota_compare_fusion.19), kind=kOutput, calls=%fused_computation.178 | output fusion | flops 12583039 | bytes 16843776 | tf_op jit(solution)/shard_map/sub | solution.py:47
  80.7 1.2 fusion.52
  82.0 0.8 convert_reduce_fusion
  83.3 7.4 %fusion.33 = bf16[1024,512]{1,0:T(8,128)(2,1)} fusion(bf16[1024,512]{1,0:T(8,128)(2,1)S(1)} %get-tuple-element.22, bf16[2048,512]{1,0:T(8,128)(2,1)S(1)} %copy-done, bf16[512,2048]{1,0:T(8,128)(2,1)} %param.14, f32[1024]{0:T(1024)S(1)} %add_rsqrt_fusion.1, f32[1024]{0:T(1024)S(1)} %broadcast_multiply_fusion.1), kind=kOutput, calls=%fused_computation.46 | convolution fusion | flops 4317511680 | bytes 6299648 | tf_op jit(solution)/shard_map/dot_general | solution.py:65
  90.8 2.5 %copy.132 = bf16[8,16,8,512]{3,1,0,2:T(8,128)(2,1)} copy(bf16[8,16,8,512]{3,2,1,0:T(8,128)(2,1)} %bitcast.190) | data formatting | bytes 2097152 | tf_op jit(solution)/shard_map/reshape | solution.py:140
  93.3 4.3 %all-to-all-start.2 = ((bf16[8,16,8,512]{3,1,0,2:T(8,128)(2,1)}), bf16[8,16,8,512]{3,1,0,2:T(8,128)(2,1)S(1)}, u32[]{:S(2)}, u32[]{:S(2)}) async-start(bf16[8,16,8,512]{3,1,0,2:T(8,128)(2,1)} %copy.132), calls=%async_computation.2 | async-start | bytes 2097152 | tf_op jit(solution)/shard_map/all_to_all | solution.py:139
  97.6 2.6 %copy.136 = bf16[512,1536]{0,1:T(8,128)(2,1)} copy(bf16[512,1536]{1,0:T(8,128)(2,1)} %param.16) | data formatting | bytes 3145728 | tf_op args[7]
  100.6 2.3 %fusion.112 = (bf16[512,1,16,32]{0,3,2,1:T(8,128)(2,1)S(1)}, bf16[512,1,16,32]{0,3,2,1:T(8,128)(2,1)S(1)}, bf16[512,1,16,32]{0,3,2,1:T(8,128)(2,1)}) fusion(bf16[512,3,16,32]{0,3,2,1:T(8,128)(2,1)} %bitcast.179), kind=kLoop, calls=%fused_computation.176 | loop fusion | bytes 3145728 | tf_op jit(solution)/shard_map/slice | solution.py:38
  103.0 10.5 %all-to-all-done.2 = bf16[8,16,8,512]{3,1,0,2:T(8,128)(2,1)S(1)} async-done(((bf16[8,16,8,512]{3,1,0,2:T(8,128)(2,1)}), bf16[8,16,8,512]{3,1,0,2:T(8,128)(2,1)S(1)}, u32[]{:S(2)}, u32[]{:S(2)}) %all-to-all-start.2) | async-done | bytes 1048608 | tf_op jit(solution)/shard_map/all_to_all | solution.py:139
  116.9 1.3 fusion.62
  118.2 3.5 %fusion.115 = (f32[16,8,128]{2,1,0:T(8,128)S(1)}, f32[16,8,128,128]{2,3,1,0:T(8,128)S(1)}) fusion(f32[16,8,128,128]{2,3,1,0:T(8,128)S(1)} %fusion.62, pred[8,128]{1,0:T(8,128)(4,1)S(1)} %broadcast_compare_fusion), kind=kOutput, calls=%fused_computation.179 | output fusion | flops 12583039 | bytes 16843776 | tf_op jit(solution)/shard_map/sub | solution.py:47
  121.7 1.2 fusion.53
  123.0 0.9 copy-done.8
  125.3 18.4 %all_to_all.45 = bf16[8,128,1,512]{3,0,2,1:T(8,128)(2,1)S(1)} all-to-all(bf16[8,128,1,512]{3,0,2,1:T(8,128)(2,1)S(1)} %copy.142), channel_id=1, replica_groups=mesh['win_slow'=4,'win_fast'=8,'grp'=8] {'grp'}, dimensions={1} | all-to-all | bytes 2097152 | tf_op jit(solution)/shard_map/all_to_all | solution.py:158
  144.6 1.3 fusion.47
  146.0 31.7 %all_to_all.46 = bf16[4,8,32,512]{3,2,0,1:T(8,128)(2,1)S(1)} all-to-all(bf16[4,8,32,512]{3,2,0,1:T(8,128)(2,1)S(1)} %copy.145), channel_id=1, replica_groups=mesh['win_slow'=4,'win_fast'=8,'grp'=8] {'win_fast'}, dimensions={1} | all-to-all | bytes 2097152 | tf_op jit(solution)/shard_map/all_to_all | solution.py:82
  177.8 15.7 %all_to_all.47 = bf16[4,8,32,512]{3,2,1,0:T(8,128)(2,1)S(1)} all-to-all(bf16[4,8,32,512]{3,2,1,0:T(8,128)(2,1)S(1)} %copy.146), channel_id=1, replica_groups=mesh['win_slow'=4,'win_fast'=8,'grp'=8] {'win_slow'}, dimensions={0} | all-to-all | bytes 2097152 | tf_op jit(solution)/shard_map/all_to_all | solution.py:83
  193.5 1.6 fusion.55
  (70 shorter events, 12.1 us)
Async XLA Ops:
  0.0 83.3 %copy-start = (bf16[2048,512]{1,0:T(8,128)(2,1)S(1)}, bf16[2048,512]{1,0:T(8,128)(2,1)}, u32[]{:S(2)}) copy-start(bf16[2048,512]{1,0:T(8,128)(2,1)} %param.15) | copy-start | bytes 6291460
  50.5 20.0 %all-to-all-start.1 = ((bf16[4,8,32,640]{3,2,1,0:T(8,128)(2,1)}), bf16[4,8,32,640]{3,2,1,0:T(8,128)(2,1)S(1)}, u32[]{:S(2)}, u32[]{:S(2)}) async-start(bf16[4,8,32,640]{3,2,1,0:T(8,128)(2,1)} %copy.125), calls=%async_computation.1 | async-start | bytes 2621440 | tf_op jit(solution)/shard_map/all_to_all | solution.py:83
  54.9 2.6 %copy-start.6 = (s32[8,32,8]{1,2,0:T(8,128)S(1)}, s32[8,32,8]{1,2,0:T(8,128)}, u32[]{:S(2)}) copy-start(s32[8,32,8]{1,2,0:T(8,128)} %param.11) | copy-start | bytes 24580
  70.9 1.9 copy-start.5
  72.8 1.0 copy-start.4
  73.8 1.1 copy-start.3
  80.7 1.2 copy-start.7
  93.3 20.2 %all-to-all-start.2 = ((bf16[8,16,8,512]{3,1,0,2:T(8,128)(2,1)}), bf16[8,16,8,512]{3,1,0,2:T(8,128)(2,1)S(1)}, u32[]{:S(2)}, u32[]{:S(2)}) async-start(bf16[8,16,8,512]{3,1,0,2:T(8,128)(2,1)} %copy.132), calls=%async_computation.2 | async-start | bytes 2097152 | tf_op jit(solution)/shard_map/all_to_all | solution.py:139
  113.5 1.2 copy-start.2
  122.9 1.1 copy-start.8
  177.8 17.3 %copy-start.1 = (bf16[2048,512]{1,0:T(8,128)(2,1)S(1)}, bf16[2048,512]{1,0:T(8,128)(2,1)}, u32[]{:S(2)}) copy-start(bf16[2048,512]{1,0:T(8,128)(2,1)} %param.15) | copy-start | bytes 6291460

commit v8 on v6

--- a/solution.py
+++ b/solution.py
@@ -150,13 +150,22 @@
     flat_rows = dilated_rows.reshape(block_count * WINDOW_SLOTS, model_dim)
     mixed_rows = attention_block(
         flat_rows, valid_marks.reshape(block_count, WINDOW_SLOTS), w_qkv_two, w_out_two
-    ).reshape(
-        block_count, WINDOW_SLOTS, 1, model_dim
     )
-    second_pad = lax.all_to_all(mixed_rows, "grp", split_axis=1, concat_axis=2, tiled=True).reshape(
-        slots_all, model_dim
-    )
-    returning = place_back(recv_hot, second_pad)
+    mixed_rows = jnp.transpose(mixed_rows.reshape(block_count, WINDOW_SLOTS, model_dim), (1, 0, 2))
+    second_pad = lax.all_to_all(
+        mixed_rows.reshape(WINDOW_SLOTS, block_count, 1, model_dim),
+        "grp",
+        split_axis=0,
+        concat_axis=2,
+        tiled=True,
+    ).reshape(slots_all, model_dim)
+    row_ids = jnp.arange(slots_all, dtype=jnp.int32)
+    row_k = row_ids // (blocks * group_count)
+    row_b = (row_ids // group_count) % blocks
+    row_r = row_ids % group_count
+    row_slot = row_b * WINDOW_SLOTS + row_k * group_count + row_r
+    back_hot = (row_slot[:, None] == arrived_slot.reshape(1, buffer_rows)).astype(jnp.bfloat16)
+    returning = place_back(back_hot, second_pad)
     returned = lax.all_to_all(returning, "win", split_axis=0, concat_axis=0, tiled=True)
     encoded = place_back(send_hot, returned)
     return encoded.reshape(1, 1, local_points, model_dim)

time: 165 us -> 167 us (1.012)
  blocking collectives: 51.9 us -> 33.6 us
  waiting for transfers between devices: 39 us -> 54.8 us
  starting transfers between devices: 15.7 us -> 19.2 us
    all_to_all x1 -> x0, blocking collectives: 18.4 us -> none  [on_device(): lax.all_to_all(mixed_rows, 'grp', split_axis=1, concat_axis=2, tiled=True)]
    all_to_all x0 -> x1, waiting for transfers between devices: none -> 15.8 us  [on_device(): lax.all_to_all(mixed_rows.reshape(WINDOW_SLOTS, block_count, 1, model_dim...]
    all_to_all x0 -> x1, starting transfers between devices: none -> 3.56 us  [on_device(): lax.all_to_all(mixed_rows.reshape(WINDOW_SLOTS, block_count, 1, model_dim...]
  transfers between devices with their start and end apart: 2 -> 3, of which waited for: 2 -> 3; matrix products, arithmetic and copies ran while one was open for 7% -> 6% of each run, Pallas kernels for 0% -> 0%
where the time goes in v8:
time: 167 us
  waiting for transfers between devices  54.8 us (33%)
  blocking collectives  33.6 us (20%)
  matrix products  26.6 us (16%)
  starting transfers between devices  19.2 us (11%)
  local copies, waits for them, and re-layouts  17.8 us (11%)
  other arithmetic  14.4 us (9%)
    all_to_all x1, blocking collectives, on_device(): lax.all_to_all(returning, 'win', split_axis=0, concat_axis=0, tiled=True)  33.6 us
    all_to_all x1, waiting for transfers between devices, on_device(): lax.all_to_all(outgoing.reshape(owner_count, capacity, model_dim + TAIL),...  28.5 us
    all_to_all x1, waiting for transfers between devices, on_device(): lax.all_to_all(mixed_rows.reshape(WINDOW_SLOTS, block_count, 1, model_dim...  15.8 us
    all_to_all x1, starting transfers between devices, on_device(): lax.all_to_all(outgoing.reshape(owner_count, capacity, model_dim + TAIL),...  11.4 us
    all_to_all x1, waiting for transfers between devices, on_device(): lax.all_to_all(first_pad.reshape(blocks, dilation_stride, group_count, mo...  10.5 us
    dot_general x1, matrix products, feed_forward(): jnp.dot(hidden, w_down, preferred_element_type=jnp.float32)  7.41 us
    sub x2, other arithmetic, attention_block(): weights = jnp.exp(scores - row_max)  7.12 us
    unnamed x20, local copies, waits for them, and re-layouts  6.35 us
  transfers between devices with their start and end apart: 3, of which 3 were waited for; matrix products, arithmetic and copies ran while one was open for 6% of the time, Pallas kernels for 0%

profile of v8, /device:TPU:32, one launch (start us, length us, event | category | flops | bytes accessed | tf_op | source)
XLA Modules:
  0.0 166.7 jit_solution(1053117581643731860)
XLA Ops:
  0.0 0.8 dynamic-slice_bitcast_fusion
  4.0 1.2 reduce-window.6
  5.8 3.1 %fusion.47 = bf16[1024,640]{1,0:T(8,128)(2,1)} fusion(s32[512]{0:T(512)S(1)} %multiply_add_fusion, bf16[512,128]{1,0:T(8,128)(2,1)S(1)} %select_convert_fusion, bf16[512,512]{1,0:T(8,128)(2,1)} %bitcast.208), kind=kOutput, calls=%fused_computation.63 | convolution fusion | flops 673579008 | bytes 1968128 | tf_op jit(solution)/shard_map/dot_general | solution.py:69
  8.9 11.4 %all-to-all-start = ((bf16[32,32,640]{2,1,0:T(8,128)(2,1)}), bf16[32,32,640]{2,1,0:T(8,128)(2,1)S(1)}, u32[]{:S(2)}, u32[]{:S(2)}) async-start(bf16[32,32,640]{2,1,0:T(8,128)(2,1)} %bitcast.194), calls=%async_computation | async-start | bytes 2621440 | tf_op jit(solution)/shard_map/all_to_all | solution.py:119
  20.3 2.6 %copy.116 = bf16[512,1536]{0,1:T(8,128)(2,1)} copy(bf16[512,1536]{1,0:T(8,128)(2,1)} %param.12) | data formatting | bytes 3145728 | tf_op args[3]
  23.2 2.6 %fusion.131 = (bf16[512,1,16,32]{0,3,2,1:T(8,128)(2,1)}, bf16[512,1,16,32]{0,3,2,1:T(8,128)(2,1)}, bf16[512,1,16,32]{0,3,2,1:T(8,128)(2,1)}) fusion(bf16[512,3,16,32]{0,3,2,1:T(8,128)(2,1)} %bitcast.183), kind=kLoop, calls=%fused_computation.204 | loop fusion | bytes 3145728 | tf_op jit(solution)/shard_map/slice | solution.py:37
  25.7 28.5 %all-to-all-done = bf16[32,32,640]{2,1,0:T(8,128)(2,1)S(1)} async-done(((bf16[32,32,640]{2,1,0:T(8,128)(2,1)}), bf16[32,32,640]{2,1,0:T(8,128)(2,1)S(1)}, u32[]{:S(2)}, u32[]{:S(2)}) %all-to-all-start) | async-done | bytes 1310752 | tf_op jit(solution)/shard_map/all_to_all | solution.py:119
  54.6 1.3 convert_reduce_fusion.1
  56.5 0.9 fusion.126
  57.6 0.9 fusion.128
  58.5 0.9 fusion.124
  59.5 1.3 fusion.73
  60.8 3.6 %fusion.132 = (f32[16,8,128]{2,1,0:T(8,128)S(1)}, f32[16,8,128,128]{2,3,1,0:T(8,128)S(1)}) fusion(f32[16,8,128,128]{2,3,1,0:T(8,128)S(1)} %fusion.73, pred[8,128]{1,0:T(8,128)(4,1)S(1)} %iota_compare_fusion.16), kind=kOutput, calls=%fused_computation.205 | output fusion | flops 12583039 | bytes 16843776 | tf_op jit(solution)/shard_map/sub | solution.py:46
  64.4 1.2 fusion.56
  65.6 0.8 convert_reduce_fusion
  67.0 7.4 %fusion.34 = bf16[1024,512]{1,0:T(8,128)(2,1)} fusion(bf16[1024,512]{1,0:T(8,128)(2,1)S(1)} %get-tuple-element.22, bf16[2048,512]{1,0:T(8,128)(2,1)S(1)} %copy-done, bf16[512,2048]{1,0:T(8,128)(2,1)} %param.14, f32[1024]{0:T(1024)S(1)} %add_rsqrt_fusion.1, f32[1024]{0:T(1024)S(1)} %broadcast_multiply_fusion.1), kind=kOutput, calls=%fused_computation.47 | convolution fusion | flops 4317511680 | bytes 6299648 | tf_op jit(solution)/shard_map/dot_general | solution.py:64
  74.5 2.5 %copy.122 = bf16[8,16,8,512]{3,1,0,2:T(8,128)(2,1)} copy(bf16[8,16,8,512]{3,2,1,0:T(8,128)(2,1)} %bitcast.195) | data formatting | bytes 2097152 | tf_op jit(solution)/shard_map/reshape | solution.py:138
  77.0 4.3 %all-to-all-start.1 = ((bf16[8,16,8,512]{3,1,0,2:T(8,128)(2,1)}), bf16[8,16,8,512]{3,1,0,2:T(8,128)(2,1)S(1)}, u32[]{:S(2)}, u32[]{:S(2)}) async-start(bf16[8,16,8,512]{3,1,0,2:T(8,128)(2,1)} %copy.122), calls=%async_computation.1 | async-start | bytes 2097152 | tf_op jit(solution)/shard_map/all_to_all | solution.py:137
  81.3 2.6 %copy.126 = bf16[512,1536]{0,1:T(8,128)(2,1)} copy(bf16[512,1536]{1,0:T(8,128)(2,1)} %param.16) | data formatting | bytes 3145728 | tf_op args[7]
  84.3 2.3 %fusion.130 = (bf16[512,1,16,32]{0,3,2,1:T(8,128)(2,1)S(1)}, bf16[512,1,16,32]{0,3,2,1:T(8,128)(2,1)S(1)}, bf16[512,1,16,32]{0,3,2,1:T(8,128)(2,1)}) fusion(bf16[512,3,16,32]{0,3,2,1:T(8,128)(2,1)} %bitcast.184), kind=kLoop, calls=%fused_computation.203 | loop fusion | bytes 3145728 | tf_op jit(solution)/shard_map/slice | solution.py:37
  86.7 10.5 %all-to-all-done.1 = bf16[8,16,8,512]{3,1,0,2:T(8,128)(2,1)S(1)} async-done(((bf16[8,16,8,512]{3,1,0,2:T(8,128)(2,1)}), bf16[8,16,8,512]{3,1,0,2:T(8,128)(2,1)S(1)}, u32[]{:S(2)}, u32[]{:S(2)}) %all-to-all-start.1) | async-done | bytes 1048608 | tf_op jit(solution)/shard_map/all_to_all | solution.py:137
  99.1 0.7 fusion.135
  100.6 1.3 fusion.66
  101.9 3.5 %fusion.133 = (f32[16,8,128]{2,1,0:T(8,128)S(1)}, f32[16,8,128,128]{2,3,1,0:T(8,128)S(1)}) fusion(f32[16,8,128,128]{2,3,1,0:T(8,128)S(1)} %fusion.66, pred[8,128]{1,0:T(8,128)(4,1)S(1)} %broadcast_compare_fusion), kind=kOutput, calls=%fused_computation.206 | output fusion | flops 12583039 | bytes 16843776 | tf_op jit(solution)/shard_map/sub | solution.py:46
  105.4 1.2 fusion.57
  106.7 0.9 copy-done.8
  108.4 1.6 copy.187
  110.0 3.6 %all-to-all-start.2 = ((bf16[128,8,1,512]{3,1,2,0:T(8,128)(2,1)}), bf16[128,8,1,512]{3,1,2,0:T(8,128)(2,1)S(1)}, u32[]{:S(2)}, u32[]{:S(2)}) async-start(bf16[128,8,1,512]{3,1,2,0:T(8,128)(2,1)} %bitcast.176), calls=%async_computation.2 | async-start | bytes 2097152 | tf_op jit(solution)/shard_map/all_to_all | solution.py:155
  113.5 15.8 %all-to-all-done.2 = bf16[128,8,1,512]{3,1,2,0:T(8,128)(2,1)S(1)} async-done(((bf16[128,8,1,512]{3,1,2,0:T(8,128)(2,1)}), bf16[128,8,1,512]{3,1,2,0:T(8,128)(2,1)S(1)}, u32[]{:S(2)}, u32[]{:S(2)}) %all-to-all-start.2) | async-done | bytes 1048608 | tf_op jit(solution)/shard_map/all_to_all | solution.py:155
  130.0 1.6 fusion.48
  131.6 33.6 %all_to_all.41 = bf16[32,32,512]{2,1,0:T(8,128)(2,1)S(1)} all-to-all(bf16[32,32,512]{2,1,0:T(8,128)(2,1)S(1)} %bitcast.197), channel_id=1, replica_groups=mesh['win'=32,'grp'=8] {'win'}, dimensions={0} | all-to-all | bytes 2097152 | tf_op jit(solution)/shard_map/all_to_all | solution.py:169
  165.1 1.6 fusion.59
  (65 shorter events, 10.1 us)
Async XLA Ops:
  0.0 67.0 %copy-start = (bf16[2048,512]{1,0:T(8,128)(2,1)S(1)}, bf16[2048,512]{1,0:T(8,128)(2,1)}, u32[]{:S(2)}) copy-start(bf16[2048,512]{1,0:T(8,128)(2,1)} %param.15) | copy-start | bytes 6291460
  8.9 45.3 %all-to-all-start = ((bf16[32,32,640]{2,1,0:T(8,128)(2,1)}), bf16[32,32,640]{2,1,0:T(8,128)(2,1)S(1)}, u32[]{:S(2)}, u32[]{:S(2)}) async-start(bf16[32,32,640]{2,1,0:T(8,128)(2,1)} %bitcast.194), calls=%async_computation | async-start | bytes 2621440 | tf_op jit(solution)/shard_map/all_to_all | solution.py:119
  20.3 2.6 %copy-start.6 = (s32[8,32,8]{1,2,0:T(8,128)S(1)}, s32[8,32,8]{1,2,0:T(8,128)}, u32[]{:S(2)}) copy-start(s32[8,32,8]{1,2,0:T(8,128)} %param.11) | copy-start | bytes 24580
  54.6 1.9 %copy-start.5 = (bf16[512,1,16,32]{0,3,2,1:T(8,128)(2,1)S(1)}, bf16[512,1,16,32]{0,3,2,1:T(8,128)(2,1)}, u32[]{:S(2)}) copy-start(bf16[512,1,16,32]{0,3,2,1:T(8,128)(2,1)} %get-tuple-element.11) | copy-start | bytes 1572868
  56.5 1.0 copy-start.4
  57.5 1.1 copy-start.3
  64.4 1.2 copy-start.7
  77.0 20.2 %all-to-all-start.1 = ((bf16[8,16,8,512]{3,1,0,2:T(8,128)(2,1)}), bf16[8,16,8,512]{3,1,0,2:T(8,128)(2,1)S(1)}, u32[]{:S(2)}, u32[]{:S(2)}) async-start(bf16[8,16,8,512]{3,1,0,2:T(8,128)(2,1)} %copy.122), calls=%async_computation.1 | async-start | bytes 2097152 | tf_op jit(solution)/shard_map/all_to_all | solution.py:137
  97.2 1.2 copy-start.2
  106.6 1.1 copy-start.8
  110.0 19.4 %all-to-all-start.2 = ((bf16[128,8,1,512]{3,1,2,0:T(8,128)(2,1)}), bf16[128,8,1,512]{3,1,2,0:T(8,128)(2,1)S(1)}, u32[]{:S(2)}, u32[]{:S(2)}) async-start(bf16[128,8,1,512]{3,1,2,0:T(8,128)(2,1)} %bitcast.176), calls=%async_computation.2 | async-start | bytes 2097152 | tf_op jit(solution)/shard_map/all_to_all | solution.py:155
  131.6 35.1 %copy-start.1 = (bf16[2048,512]{1,0:T(8,128)(2,1)S(1)}, bf16[2048,512]{1,0:T(8,128)(2,1)}, u32[]{:S(2)}) copy-start(bf16[2048,512]{1,0:T(8,128)(2,1)} %param.15) | copy-start | bytes 6291460

commit v9 on v6

--- a/solution.py
+++ b/solution.py
@@ -133,20 +133,27 @@
 
     column = jnp.arange(WINDOW_SLOTS, dtype=jnp.int32)
     usable_mask = column[None, :] < own_counts[:, None]
-    first_pad = feed_forward(attention_block(padded_x, usable_mask, w_qkv_one, w_out_one), w_up, w_down)
+    first_mixed = attention_block(padded_x, usable_mask, w_qkv_one, w_out_one)
+    row_ids = jnp.arange(slots_all, dtype=jnp.int32)
+    row_r = row_ids // (blocks * dilation_stride)
+    row_b = (row_ids // dilation_stride) % blocks
+    row_k = row_ids % dilation_stride
+    source_row = row_b * WINDOW_SLOTS + row_k * group_count + row_r
+    order_hot = (source_row[:, None] == row_ids[None, :]).astype(jnp.bfloat16)
+    first_pad = feed_forward(place(order_hot, first_mixed), w_up, w_down)
     dilated_rows = lax.all_to_all(
-        first_pad.reshape(blocks, dilation_stride, group_count, model_dim),
+        first_pad.reshape(group_count, blocks, dilation_stride, model_dim),
         "grp",
-        split_axis=2,
-        concat_axis=1,
+        split_axis=0,
+        concat_axis=2,
         tiled=True,
     )
+    block_count = blocks
     owner_counts = lax.dynamic_index_in_dim(counts, win_index, 1, keepdims=False)
     k_ids = jnp.arange(dilation_stride, dtype=jnp.int32)
     valid_marks = (k_ids[None, None, :] * group_count + grp_index) < jnp.transpose(owner_counts)[
         :, :, None
     ]
-    block_count = dilated_rows.shape[0]
     flat_rows = dilated_rows.reshape(block_count * WINDOW_SLOTS, model_dim)
     mixed_rows = attention_block(
         flat_rows, valid_marks.reshape(block_count, WINDOW_SLOTS), w_qkv_two, w_out_two

time: 165 us -> 169 us (1.024)
  matrix products: 26.3 us -> 30.8 us
  local copies, waits for them, and re-layouts: 17.2 us -> 14.8 us
    dot_general x2 -> x3, matrix products: 4.47 us -> 8.68 us  [place(): jnp.dot(onehot, rows, preferred_element_type=jnp.float32)]
    reshape x1 -> x0, local copies, waits for them, and re-layouts: 2.5 us -> none  [on_device(): first_pad.reshape(blocks, dilation_stride, group_count, model_dim)]
    unnamed x20 -> x22, local copies, waits for them, and re-layouts: 6.35 us -> 6.17 us
  transfers between devices with their start and end apart: 2 -> 2, of which waited for: 2 -> 2; matrix products, arithmetic and copies ran while one was open for 7% -> 6% of each run, Pallas kernels for 0% -> 0%
where the time goes in v9:
time: 169 us; the launch traced here: 168 us
  blocking collectives  51.9 us (31%)
  waiting for transfers between devices  39 us (23%)
  matrix products  30.8 us (18%)
  starting transfers between devices  15.7 us (9%)
  other arithmetic  15.6 us (9%)
  local copies, waits for them, and re-layouts  14.8 us (9%)
    all_to_all x1, blocking collectives, on_device(): lax.all_to_all(returning, 'win', split_axis=0, concat_axis=0, tiled=True)  33.5 us
    all_to_all x1, waiting for transfers between devices, on_device(): lax.all_to_all(outgoing.reshape(owner_count, capacity, model_dim + TAIL),...  28.5 us
    all_to_all x1, blocking collectives, on_device(): lax.all_to_all(mixed_rows, 'grp', split_axis=1, concat_axis=2, tiled=True)  18.4 us
    all_to_all x1, starting transfers between devices, on_device(): lax.all_to_all(outgoing.reshape(owner_count, capacity, model_dim + TAIL),...  11.4 us
    all_to_all x1, waiting for transfers between devices, on_device(): lax.all_to_all(first_pad.reshape(group_count, blocks, dilation_stride, mo...  10.5 us
    dot_general x3, matrix products, place(): jnp.dot(onehot, rows, preferred_element_type=jnp.float32)  8.68 us
    dot_general x1, matrix products, feed_forward(): jnp.dot(hidden, w_down, preferred_element_type=jnp.float32)  7.96 us
    sub x2, other arithmetic, attention_block(): weights = jnp.exp(scores - row_max)  7.12 us
  transfers between devices with their start and end apart: 2, of which 2 were waited for; matrix products, arithmetic and copies ran while one was open for 6% of the time, Pallas kernels for 0%

profile of v9, /device:TPU:32, one launch (start us, length us, event | category | flops | bytes accessed | tf_op | source)
XLA Modules:
  0.0 168.0 jit_solution(520201520536059133)
XLA Ops:
  0.0 0.8 dynamic-slice_bitcast_fusion
  4.0 1.2 reduce-window.6
  5.8 3.1 %fusion.43 = bf16[1024,640]{1,0:T(8,128)(2,1)} fusion(s32[512]{0:T(512)S(1)} %multiply_add_fusion, bf16[512,128]{1,0:T(8,128)(2,1)S(1)} %select_convert_fusion, bf16[512,512]{1,0:T(8,128)(2,1)} %bitcast.202), kind=kOutput, calls=%fused_computation.61 | convolution fusion | flops 673579008 | bytes 1968128 | tf_op jit(solution)/shard_map/dot_general | solution.py:69
  8.9 11.4 %all-to-all-start = ((bf16[32,32,640]{2,1,0:T(8,128)(2,1)}), bf16[32,32,640]{2,1,0:T(8,128)(2,1)S(1)}, u32[]{:S(2)}, u32[]{:S(2)}) async-start(bf16[32,32,640]{2,1,0:T(8,128)(2,1)} %bitcast.190), calls=%async_computation | async-start | bytes 2621440 | tf_op jit(solution)/shard_map/all_to_all | solution.py:119
  20.3 2.6 %copy.108 = bf16[512,1536]{0,1:T(8,128)(2,1)} copy(bf16[512,1536]{1,0:T(8,128)(2,1)} %param.12) | data formatting | bytes 3145728 | tf_op args[3]
  23.2 2.6 %fusion.129 = (bf16[512,1,16,32]{0,3,2,1:T(8,128)(2,1)}, bf16[512,1,16,32]{0,3,2,1:T(8,128)(2,1)}, bf16[512,1,16,32]{0,3,2,1:T(8,128)(2,1)}) fusion(bf16[512,3,16,32]{0,3,2,1:T(8,128)(2,1)} %bitcast.179), kind=kLoop, calls=%fused_computation.202 | loop fusion | bytes 3145728 | tf_op jit(solution)/shard_map/slice | solution.py:37
  25.7 28.5 %all-to-all-done = bf16[32,32,640]{2,1,0:T(8,128)(2,1)S(1)} async-done(((bf16[32,32,640]{2,1,0:T(8,128)(2,1)}), bf16[32,32,640]{2,1,0:T(8,128)(2,1)S(1)}, u32[]{:S(2)}, u32[]{:S(2)}) %all-to-all-start) | async-done | bytes 1310752 | tf_op jit(solution)/shard_map/all_to_all | solution.py:119
  54.6 1.4 convert_reduce_fusion.1
  56.4 0.8 fusion.90
  57.4 0.7 fusion.88
  58.2 0.7 fusion.92
  59.0 1.3 fusion.69
  60.3 3.7 %fusion.130 = (f32[16,8,128]{2,1,0:T(8,128)S(1)}, f32[16,8,128,128]{2,3,1,0:T(8,128)S(1)}) fusion(f32[16,8,128,128]{2,3,1,0:T(8,128)S(1)} %fusion.69, pred[8,128]{1,0:T(8,128)(4,1)S(1)} %iota_compare_fusion.23), kind=kOutput, calls=%fused_computation.203 | output fusion | flops 12583039 | bytes 16843776 | tf_op jit(solution)/shard_map/sub | solution.py:46
  63.9 2.3 %fusion.52 = bf16[16,8,4,8,128]{4,3,2,1,0:T(8,128)(2,1)} fusion(f32[16,8,128,128]{2,3,1,0:T(8,128)S(1)} %get-tuple-element.20, f32[16,8,128]{2,1,0:T(8,128)S(1)} %get-tuple-element.19, f32[1024,16,32]{0,2,1:T(8,128)S(1)} %bitcast.205), kind=kOutput, calls=%fused_computation.68 | convolution fusion | flops 139460608 | bytes 11599872 | tf_op jit(solution)/shard_map/hbqk,hbke->hbqe/dot_general | solution.py:48
  66.2 4.2 %convert_reduce_fusion = (f32[1024]{0:T(1024)S(1)}, bf16[1024,512]{1,0:T(8,128)(2,1)}) fusion(bf16[1024,512]{0,1:T(8,128)(2,1)S(1)} %copy-done.4, bf16[16,32,512]{2,1,0:T(8,128)(2,1)} %bitcast.203, bf16[16,8,4,8,128]{4,3,2,1,0:T(8,128)(2,1)} %fusion.52, s32[1024]{0:T(1024)S(1)} %fusion.109), kind=kOutput, calls=%fused_computation.35 | convolution fusion | flops 1614806016 | bytes 3678208 | tf_op jit(solution)/shard_map/dot_general | solution.py:69
  70.4 1.7 %fusion.29 = f32[1024]{0:T(1024)S(1)} fusion(bf16[1024,512]{1,0:T(8,128)(2,1)} %get-tuple-element.22, f32[1024]{0:T(1024)S(1)} %broadcast_multiply_fusion.1), kind=kLoop, calls=%fused_computation.43 | loop fusion | flops 2096128 | bytes 1056768 | tf_op jit(solution)/shard_map/reduce_sum | solution.py:19
  72.1 8.0 %fusion.34 = bf16[1024,512]{1,0:T(8,128)(2,1)} fusion(bf16[1024,512]{1,0:T(8,128)(2,1)} %get-tuple-element.22, bf16[2048,512]{1,0:T(8,128)(2,1)S(1)} %copy-done, bf16[512,2048]{1,0:T(8,128)(2,1)} %param.14, f32[1024]{0:T(1024)S(1)} %add_rsqrt_fusion.1, f32[1024]{0:T(1024)S(1)} %broadcast_multiply_fusion.1), kind=kOutput, calls=%fused_computation.48 | convolution fusion | flops 4317511680 | bytes 6299648 | tf_op jit(solution)/shard_map/dot_general | solution.py:64
  80.1 4.3 %all-to-all-start.1 = ((bf16[8,8,16,512]{3,2,1,0:T(8,128)(2,1)}), bf16[8,8,16,512]{3,2,1,0:T(8,128)(2,1)S(1)}, u32[]{:S(2)}, u32[]{:S(2)}) async-start(bf16[8,8,16,512]{3,2,1,0:T(8,128)(2,1)} %bitcast.24), calls=%async_computation.1 | async-start | bytes 2097152 | tf_op jit(solution)/shard_map/all_to_all | solution.py:144
  84.4 2.6 %copy.122 = bf16[512,1536]{0,1:T(8,128)(2,1)} copy(bf16[512,1536]{1,0:T(8,128)(2,1)} %param.16) | data formatting | bytes 3145728 | tf_op args[7]
  87.5 2.3 %fusion.128 = (bf16[512,1,16,32]{0,3,2,1:T(8,128)(2,1)S(1)}, bf16[512,1,16,32]{0,3,2,1:T(8,128)(2,1)S(1)}, bf16[512,1,16,32]{0,3,2,1:T(8,128)(2,1)}) fusion(bf16[512,3,16,32]{0,3,2,1:T(8,128)(2,1)} %bitcast.180), kind=kLoop, calls=%fused_computation.201 | loop fusion | bytes 3145728 | tf_op jit(solution)/shard_map/slice | solution.py:37
  89.8 10.5 %all-to-all-done.1 = bf16[8,8,16,512]{3,2,1,0:T(8,128)(2,1)S(1)} async-done(((bf16[8,8,16,512]{3,2,1,0:T(8,128)(2,1)}), bf16[8,8,16,512]{3,2,1,0:T(8,128)(2,1)S(1)}, u32[]{:S(2)}, u32[]{:S(2)}) %all-to-all-start.1) | async-done | bytes 1048608 | tf_op jit(solution)/shard_map/all_to_all | solution.py:144
  102.2 0.7 fusion.134
  102.9 0.7 fusion.135
  103.6 0.7 fusion.136
  105.0 1.3 fusion.62
  106.3 3.5 %fusion.133 = (f32[16,8,128]{2,1,0:T(8,128)S(1)}, f32[16,8,128,128]{2,3,1,0:T(8,128)S(1)}) fusion(f32[16,8,128,128]{2,3,1,0:T(8,128)S(1)} %fusion.62, pred[8,128]{1,0:T(8,128)(4,1)S(1)} %broadcast_compare_fusion), kind=kOutput, calls=%fused_computation.204 | output fusion | flops 12583039 | bytes 16843776 | tf_op jit(solution)/shard_map/sub | solution.py:46
  109.8 1.2 fusion.53
  111.0 0.8 fusion.35
  112.3 18.4 %all_to_all.41 = bf16[8,128,1,512]{3,0,2,1:T(8,128)(2,1)S(1)} all-to-all(bf16[8,128,1,512]{3,0,2,1:T(8,128)(2,1)S(1)} %copy.128), channel_id=1, replica_groups=mesh['win'=32,'grp'=8] {'grp'}, dimensions={1} | all-to-all | bytes 2097152 | tf_op jit(solution)/shard_map/all_to_all | solution.py:163
  131.7 1.3 fusion.47
  133.0 33.5 %all_to_all.42 = bf16[32,32,512]{2,1,0:T(8,128)(2,1)S(1)} all-to-all(bf16[32,32,512]{2,1,0:T(8,128)(2,1)S(1)} %bitcast.193), channel_id=1, replica_groups=mesh['win'=32,'grp'=8] {'win'}, dimensions={0} | all-to-all | bytes 2097152 | tf_op jit(solution)/shard_map/all_to_all | solution.py:167
  166.5 1.6 fusion.55
  (68 shorter events, 9.4 us)
Async XLA Ops:
  0.0 72.1 %copy-start = (bf16[2048,512]{1,0:T(8,128)(2,1)S(1)}, bf16[2048,512]{1,0:T(8,128)(2,1)}, u32[]{:S(2)}) copy-start(bf16[2048,512]{1,0:T(8,128)(2,1)} %param.15) | copy-start | bytes 6291460
  8.9 45.3 %all-to-all-start = ((bf16[32,32,640]{2,1,0:T(8,128)(2,1)}), bf16[32,32,640]{2,1,0:T(8,128)(2,1)S(1)}, u32[]{:S(2)}, u32[]{:S(2)}) async-start(bf16[32,32,640]{2,1,0:T(8,128)(2,1)} %bitcast.190), calls=%async_computation | async-start | bytes 2621440 | tf_op jit(solution)/shard_map/all_to_all | solution.py:119
  20.3 2.6 %copy-start.8 = (s32[8,32,8]{1,2,0:T(8,128)S(1)}, s32[8,32,8]{1,2,0:T(8,128)}, u32[]{:S(2)}) copy-start(s32[8,32,8]{1,2,0:T(8,128)} %param.11) | copy-start | bytes 24580
  54.6 1.7 %copy-start.7 = (bf16[512,1,16,32]{0,3,2,1:T(8,128)(2,1)S(1)}, bf16[512,1,16,32]{0,3,2,1:T(8,128)(2,1)}, u32[]{:S(2)}) copy-start(bf16[512,1,16,32]{0,3,2,1:T(8,128)(2,1)} %get-tuple-element.11) | copy-start | bytes 1572868
  56.0 2.2 %copy-start.3 = (bf16[1024,512]{0,1:T(8,128)(2,1)}, bf16[1024,512]{0,1:T(8,128)(2,1)S(1)}, u32[]{:S(2)}) copy-start(bf16[1024,512]{0,1:T(8,128)(2,1)S(1)} %get-tuple-element.18) | copy-start | bytes 3145732
  56.3 1.1 copy-start.6
  57.1 1.1 copy-start.5
  63.9 2.3 %copy-start.4 = (bf16[1024,512]{0,1:T(8,128)(2,1)S(1)}, bf16[1024,512]{0,1:T(8,128)(2,1)}, u32[]{:S(2)}) copy-start(bf16[1024,512]{0,1:T(8,128)(2,1)} %copy-done.3) | copy-start | bytes 3145732
  80.1 20.2 %all-to-all-start.1 = ((bf16[8,8,16,512]{3,2,1,0:T(8,128)(2,1)}), bf16[8,8,16,512]{3,2,1,0:T(8,128)(2,1)S(1)}, u32[]{:S(2)}, u32[]{:S(2)}) async-start(bf16[8,8,16,512]{3,2,1,0:T(8,128)(2,1)} %bitcast.24), calls=%async_computation.1 | async-start | bytes 2097152 | tf_op jit(solution)/shard_map/all_to_all | solution.py:144
  101.1 1.0 copy-start.2
  109.8 1.2 copy-start.9
  133.0 35.0 %copy-start.1 = (bf16[2048,512]{1,0:T(8,128)(2,1)S(1)}, bf16[2048,512]{1,0:T(8,128)(2,1)}, u32[]{:S(2)}) copy-start(bf16[2048,512]{1,0:T(8,128)(2,1)} %param.15) | copy-start | bytes 6291460

commit v10 on v6

--- a/solution.py
+++ b/solution.py
@@ -94,7 +94,10 @@
     owner_dev = point_rank // local_points
     owner_ids = jnp.arange(owner_count, dtype=jnp.int32)
     choose = (owner_dev[:, None] == owner_ids[None, :]).astype(jnp.int32)
-    peer_order = jnp.sum(choose * (jnp.cumsum(choose, axis=0) - 1), axis=1)
+    point_ids = jnp.arange(local_points, dtype=jnp.int32)
+    lower = (point_ids[None, :] <= point_ids[:, None]).astype(jnp.bfloat16)
+    running = jnp.dot(lower, choose.astype(jnp.bfloat16), preferred_element_type=jnp.float32)
+    peer_order = jnp.sum(choose * (running.astype(jnp.int32) - 1), axis=1)
     send_place = owner_dev * capacity + peer_order
     buffer_ids = jnp.arange(buffer_rows, dtype=jnp.int32)
     send_hot = (buffer_ids[:, None] == send_place[None, :]).astype(jnp.bfloat16)
@@ -102,8 +105,13 @@
     window_ends = jnp.cumsum(column_counts, axis=1)
     starts = window_ends - column_counts
     offset = point_rank % local_points
-    owner_ends = jnp.sum(choose[:, :, None] * window_ends[None], axis=1)
-    owner_starts = jnp.sum(choose[:, :, None] * starts[None], axis=1)
+    table = jnp.concatenate(
+        [window_ends // SLOT_BASE, window_ends % SLOT_BASE, starts // SLOT_BASE, starts % SLOT_BASE], axis=1
+    ).astype(jnp.bfloat16)
+    picked = jnp.dot(choose.astype(jnp.bfloat16), table, preferred_element_type=jnp.float32)
+    picked = picked.astype(jnp.int32)
+    owner_ends = picked[:, :blocks] * SLOT_BASE + picked[:, blocks : 2 * blocks]
+    owner_starts = picked[:, 2 * blocks : 3 * blocks] * SLOT_BASE + picked[:, 3 * blocks :]
     window = jnp.sum((owner_ends <= offset[:, None]).astype(jnp.int32), axis=1)
     block_ids = jnp.arange(blocks, dtype=jnp.int32)
     block_pick = (window[:, None] == block_ids[None, :]).astype(jnp.int32)

time: 165 us -> 163 us (0.988)
  other arithmetic: 14.3 us -> 12.2 us
where the time goes in v10:
time: 163 us
  blocking collectives  51.9 us (32%)
  waiting for transfers between devices  39 us (24%)
  matrix products  26.7 us (16%)
  local copies, waits for them, and re-layouts  16.8 us (10%)
  starting transfers between devices  15.7 us (10%)
  other arithmetic  12.2 us (7%)
    all_to_all x1, blocking collectives, on_device(): lax.all_to_all(returning, 'win', split_axis=0, concat_axis=0, tiled=True)  33.5 us
    all_to_all x1, waiting for transfers between devices, on_device(): lax.all_to_all(outgoing.reshape(owner_count, capacity, model_dim + TAIL),...  28.5 us
    all_to_all x1, blocking collectives, on_device(): lax.all_to_all(mixed_rows, 'grp', split_axis=1, concat_axis=2, tiled=True)  18.4 us
    all_to_all x1, starting transfers between devices, on_device(): lax.all_to_all(outgoing.reshape(owner_count, capacity, model_dim + TAIL),...  11.4 us
    all_to_all x1, waiting for transfers between devices, on_device(): lax.all_to_all(first_pad.reshape(blocks, dilation_stride, group_count, mo...  10.5 us
    dot_general x1, matrix products, feed_forward(): jnp.dot(hidden, w_down, preferred_element_type=jnp.float32)  7.41 us
    sub x2, other arithmetic, attention_block(): weights = jnp.exp(scores - row_max)  7.12 us
    unnamed x20, local copies, waits for them, and re-layouts  6.35 us
  transfers between devices with their start and end apart: 2, of which 2 were waited for; matrix products, arithmetic and copies ran while one was open for 7% of the time, Pallas kernels for 0%

profile of v10, /device:TPU:32, one launch (start us, length us, event | category | flops | bytes accessed | tf_op | source)
XLA Modules:
  0.0 162.6 jit_solution(14790241169722998200)
XLA Ops:
  0.0 0.8 dynamic-slice_bitcast_fusion
  3.7 3.1 %fusion.45 = bf16[1024,640]{1,0:T(8,128)(2,1)} fusion(s32[512]{0:T(512)S(1)} %multiply_add_fusion, bf16[512,128]{1,0:T(8,128)(2,1)S(1)} %select_convert_fusion, bf16[512,512]{1,0:T(8,128)(2,1)} %bitcast.182), kind=kOutput, calls=%fused_computation.61 | convolution fusion | flops 673579008 | bytes 1968128 | tf_op jit(solution)/shard_map/dot_general | solution.py:69
  6.8 11.4 %all-to-all-start = ((bf16[32,32,640]{2,1,0:T(8,128)(2,1)}), bf16[32,32,640]{2,1,0:T(8,128)(2,1)S(1)}, u32[]{:S(2)}, u32[]{:S(2)}) async-start(bf16[32,32,640]{2,1,0:T(8,128)(2,1)} %bitcast.169), calls=%async_computation | async-start | bytes 2621440 | tf_op jit(solution)/shard_map/all_to_all | solution.py:127
  18.2 2.6 %copy.77 = bf16[512,1536]{0,1:T(8,128)(2,1)} copy(bf16[512,1536]{1,0:T(8,128)(2,1)} %param.12) | data formatting | bytes 3145728 | tf_op args[3]
  21.1 2.6 %fusion.130 = (bf16[512,1,16,32]{0,3,2,1:T(8,128)(2,1)}, bf16[512,1,16,32]{0,3,2,1:T(8,128)(2,1)}, bf16[512,1,16,32]{0,3,2,1:T(8,128)(2,1)}) fusion(bf16[512,3,16,32]{0,3,2,1:T(8,128)(2,1)} %bitcast.158), kind=kLoop, calls=%fused_computation.201 | loop fusion | bytes 3145728 | tf_op jit(solution)/shard_map/slice | solution.py:37
  23.6 28.5 %all-to-all-done = bf16[32,32,640]{2,1,0:T(8,128)(2,1)S(1)} async-done(((bf16[32,32,640]{2,1,0:T(8,128)(2,1)}), bf16[32,32,640]{2,1,0:T(8,128)(2,1)S(1)}, u32[]{:S(2)}, u32[]{:S(2)}) %all-to-all-start) | async-done | bytes 1310752 | tf_op jit(solution)/shard_map/all_to_all | solution.py:127
  52.5 1.3 convert_reduce_fusion.1
  54.4 0.9 fusion.125
  55.4 0.9 fusion.127
  56.4 0.9 fusion.123
  57.3 1.3 fusion.72
  58.7 3.6 %fusion.131 = (f32[16,8,128]{2,1,0:T(8,128)S(1)}, f32[16,8,128,128]{2,3,1,0:T(8,128)S(1)}) fusion(f32[16,8,128,128]{2,3,1,0:T(8,128)S(1)} %fusion.72, pred[8,128]{1,0:T(8,128)(4,1)S(1)} %iota_compare_fusion.20), kind=kOutput, calls=%fused_computation.202 | output fusion | flops 12583039 | bytes 16843776 | tf_op jit(solution)/shard_map/sub | solution.py:46
  62.3 1.2 fusion.52
  63.5 0.8 convert_reduce_fusion
  64.9 7.4 %fusion.33 = bf16[1024,512]{1,0:T(8,128)(2,1)} fusion(bf16[1024,512]{1,0:T(8,128)(2,1)S(1)} %get-tuple-element.24, bf16[2048,512]{1,0:T(8,128)(2,1)S(1)} %copy-done, bf16[512,2048]{1,0:T(8,128)(2,1)} %param.14, f32[1024]{0:T(1024)S(1)} %add_rsqrt_fusion.1, f32[1024]{0:T(1024)S(1)} %broadcast_multiply_fusion.1), kind=kOutput, calls=%fused_computation.46 | convolution fusion | flops 4317511680 | bytes 6299648 | tf_op jit(solution)/shard_map/dot_general | solution.py:64
  72.3 2.5 %copy.83 = bf16[8,16,8,512]{3,1,0,2:T(8,128)(2,1)} copy(bf16[8,16,8,512]{3,2,1,0:T(8,128)(2,1)} %bitcast.170) | data formatting | bytes 2097152 | tf_op jit(solution)/shard_map/reshape | solution.py:146
  74.8 4.3 %all-to-all-start.1 = ((bf16[8,16,8,512]{3,1,0,2:T(8,128)(2,1)}), bf16[8,16,8,512]{3,1,0,2:T(8,128)(2,1)S(1)}, u32[]{:S(2)}, u32[]{:S(2)}) async-start(bf16[8,16,8,512]{3,1,0,2:T(8,128)(2,1)} %copy.83), calls=%async_computation.1 | async-start | bytes 2097152 | tf_op jit(solution)/shard_map/all_to_all | solution.py:145
  79.1 2.6 %copy.87 = bf16[512,1536]{0,1:T(8,128)(2,1)} copy(bf16[512,1536]{1,0:T(8,128)(2,1)} %param.16) | data formatting | bytes 3145728 | tf_op args[7]
  82.2 2.3 %fusion.129 = (bf16[512,1,16,32]{0,3,2,1:T(8,128)(2,1)S(1)}, bf16[512,1,16,32]{0,3,2,1:T(8,128)(2,1)S(1)}, bf16[512,1,16,32]{0,3,2,1:T(8,128)(2,1)}) fusion(bf16[512,3,16,32]{0,3,2,1:T(8,128)(2,1)} %bitcast.159), kind=kLoop, calls=%fused_computation.200 | loop fusion | bytes 3145728 | tf_op jit(solution)/shard_map/slice | solution.py:37
  84.6 10.5 %all-to-all-done.1 = bf16[8,16,8,512]{3,1,0,2:T(8,128)(2,1)S(1)} async-done(((bf16[8,16,8,512]{3,1,0,2:T(8,128)(2,1)}), bf16[8,16,8,512]{3,1,0,2:T(8,128)(2,1)S(1)}, u32[]{:S(2)}, u32[]{:S(2)}) %all-to-all-start.1) | async-done | bytes 1048608 | tf_op jit(solution)/shard_map/all_to_all | solution.py:145
  96.2 0.7 fusion.133
  97.0 0.7 fusion.134
  97.7 0.7 fusion.135
  98.5 1.3 fusion.65
  99.8 3.5 %fusion.132 = (f32[16,8,128]{2,1,0:T(8,128)S(1)}, f32[16,8,128,128]{2,3,1,0:T(8,128)S(1)}) fusion(f32[16,8,128,128]{2,3,1,0:T(8,128)S(1)} %fusion.65, pred[8,128]{1,0:T(8,128)(4,1)S(1)} %broadcast_compare_fusion), kind=kOutput, calls=%fused_computation.203 | output fusion | flops 12583039 | bytes 16843776 | tf_op jit(solution)/shard_map/sub | solution.py:46
  103.3 1.2 fusion.53
  104.6 0.9 copy-done.8
  105.5 0.7 fusion.34
  106.9 18.4 %all_to_all.41 = bf16[8,128,1,512]{3,0,2,1:T(8,128)(2,1)S(1)} all-to-all(bf16[8,128,1,512]{3,0,2,1:T(8,128)(2,1)S(1)} %copy.93), channel_id=1, replica_groups=mesh['win'=32,'grp'=8] {'grp'}, dimensions={1} | all-to-all | bytes 2097152 | tf_op jit(solution)/shard_map/all_to_all | solution.py:164
  126.2 1.3 fusion.47
  127.5 33.5 %all_to_all.42 = bf16[32,32,512]{2,1,0:T(8,128)(2,1)S(1)} all-to-all(bf16[32,32,512]{2,1,0:T(8,128)(2,1)S(1)} %bitcast.174), channel_id=1, replica_groups=mesh['win'=32,'grp'=8] {'win'}, dimensions={0} | all-to-all | bytes 2097152 | tf_op jit(solution)/shard_map/all_to_all | solution.py:168
  161.0 1.6 fusion.55
  (55 shorter events, 7.9 us)
Async XLA Ops:
  0.0 64.9 %copy-start = (bf16[2048,512]{1,0:T(8,128)(2,1)S(1)}, bf16[2048,512]{1,0:T(8,128)(2,1)}, u32[]{:S(2)}) copy-start(bf16[2048,512]{1,0:T(8,128)(2,1)} %param.15) | copy-start | bytes 6291460
  6.8 45.3 %all-to-all-start = ((bf16[32,32,640]{2,1,0:T(8,128)(2,1)}), bf16[32,32,640]{2,1,0:T(8,128)(2,1)S(1)}, u32[]{:S(2)}, u32[]{:S(2)}) async-start(bf16[32,32,640]{2,1,0:T(8,128)(2,1)} %bitcast.169), calls=%async_computation | async-start | bytes 2621440 | tf_op jit(solution)/shard_map/all_to_all | solution.py:127
  18.2 2.6 %copy-start.6 = (s32[8,32,8]{1,2,0:T(8,128)S(1)}, s32[8,32,8]{1,2,0:T(8,128)}, u32[]{:S(2)}) copy-start(s32[8,32,8]{1,2,0:T(8,128)} %param.11) | copy-start | bytes 24580
  52.5 1.9 %copy-start.5 = (bf16[512,1,16,32]{0,3,2,1:T(8,128)(2,1)S(1)}, bf16[512,1,16,32]{0,3,2,1:T(8,128)(2,1)}, u32[]{:S(2)}) copy-start(bf16[512,1,16,32]{0,3,2,1:T(8,128)(2,1)} %get-tuple-element.9) | copy-start | bytes 1572868
  54.4 1.0 copy-start.4
  55.4 1.1 copy-start.3
  62.3 1.2 copy-start.7
  74.8 20.2 %all-to-all-start.1 = ((bf16[8,16,8,512]{3,1,0,2:T(8,128)(2,1)}), bf16[8,16,8,512]{3,1,0,2:T(8,128)(2,1)S(1)}, u32[]{:S(2)}, u32[]{:S(2)}) async-start(bf16[8,16,8,512]{3,1,0,2:T(8,128)(2,1)} %copy.83), calls=%async_computation.1 | async-start | bytes 2097152 | tf_op jit(solution)/shard_map/all_to_all | solution.py:145
  95.1 1.2 copy-start.2
  104.5 1.1 copy-start.8
  127.5 35.1 %copy-start.1 = (bf16[2048,512]{1,0:T(8,128)(2,1)S(1)}, bf16[2048,512]{1,0:T(8,128)(2,1)}, u32[]{:S(2)}) copy-start(bf16[2048,512]{1,0:T(8,128)(2,1)} %param.15) | copy-start | bytes 6291460

commit v11 on v10

--- a/solution.py
+++ b/solution.py
@@ -91,7 +91,7 @@
     point_rank = rank.reshape(local_points)
     column_counts = lax.dynamic_index_in_dim(counts, grp_index, 0, keepdims=False)
 
-    owner_dev = point_rank // local_points
+    owner_dev = lax.div(point_rank, local_points)
     owner_ids = jnp.arange(owner_count, dtype=jnp.int32)
     choose = (owner_dev[:, None] == owner_ids[None, :]).astype(jnp.int32)
     point_ids = jnp.arange(local_points, dtype=jnp.int32)
@@ -104,9 +104,9 @@
 
     window_ends = jnp.cumsum(column_counts, axis=1)
     starts = window_ends - column_counts
-    offset = point_rank % local_points
+    offset = lax.rem(point_rank, local_points)
     table = jnp.concatenate(
-        [window_ends // SLOT_BASE, window_ends % SLOT_BASE, starts // SLOT_BASE, starts % SLOT_BASE], axis=1
+        [lax.div(window_ends, SLOT_BASE), lax.rem(window_ends, SLOT_BASE), lax.div(starts, SLOT_BASE), lax.rem(starts, SLOT_BASE)], axis=1
     ).astype(jnp.bfloat16)
     picked = jnp.dot(choose.astype(jnp.bfloat16), table, preferred_element_type=jnp.float32)
     picked = picked.astype(jnp.int32)
@@ -120,8 +120,8 @@
     tail_ids = jnp.arange(TAIL, dtype=jnp.int32)
     code_cols = jnp.where(
         tail_ids[None, :] == 0,
-        (slot_code // SLOT_BASE)[:, None],
-        jnp.where(tail_ids[None, :] == 1, (slot_code % SLOT_BASE)[:, None], 0),
+        lax.div(slot_code, SLOT_BASE)[:, None],
+        jnp.where(tail_ids[None, :] == 1, lax.rem(slot_code, SLOT_BASE)[:, None], 0),
     ).astype(jnp.bfloat16)
     outgoing = place(send_hot, jnp.concatenate([rows_x, code_cols], axis=1))
     receiving = lax.all_to_all(

time: 163 us -> 163 us (level)
  no operation moved by 1% of the time
where the time goes in v11:
time: 163 us
  blocking collectives  51.9 us (32%)
  waiting for transfers between devices  39 us (24%)
  matrix products  26.7 us (16%)
  local copies, waits for them, and re-layouts  16.8 us (10%)
  starting transfers between devices  15.7 us (10%)
  other arithmetic  12.2 us (7%)
    all_to_all x1, blocking collectives, on_device(): lax.all_to_all(returning, 'win', split_axis=0, concat_axis=0, tiled=True)  33.5 us
    all_to_all x1, waiting for transfers between devices, on_device(): lax.all_to_all(outgoing.reshape(owner_count, capacity, model_dim + TAIL),...  28.5 us
    all_to_all x1, blocking collectives, on_device(): lax.all_to_all(mixed_rows, 'grp', split_axis=1, concat_axis=2, tiled=True)  18.4 us
    all_to_all x1, starting transfers between devices, on_device(): lax.all_to_all(outgoing.reshape(owner_count, capacity, model_dim + TAIL),...  11.4 us
    all_to_all x1, waiting for transfers between devices, on_device(): lax.all_to_all(first_pad.reshape(blocks, dilation_stride, group_count, mo...  10.5 us
    dot_general x1, matrix products, feed_forward(): jnp.dot(hidden, w_down, preferred_element_type=jnp.float32)  7.42 us
    sub x2, other arithmetic, attention_block(): weights = jnp.exp(scores - row_max)  7.12 us
    unnamed x20, local copies, waits for them, and re-layouts  6.35 us
  transfers between devices with their start and end apart: 2, of which 2 were waited for; matrix products, arithmetic and copies ran while one was open for 7% of the time, Pallas kernels for 0%

profile of v11, /device:TPU:32, one launch (start us, length us, event | category | flops | bytes accessed | tf_op | source)
XLA Modules:
  0.0 162.5 jit_solution(15884425211801808277)
XLA Ops:
  0.0 0.8 dynamic-slice_bitcast_fusion
  3.6 3.1 %fusion.45 = bf16[1024,640]{1,0:T(8,128)(2,1)} fusion(s32[512]{0:T(512)S(1)} %get-tuple-element.17, bf16[512,128]{1,0:T(8,128)(2,1)S(1)} %select_convert_fusion, bf16[512,512]{1,0:T(8,128)(2,1)} %bitcast.182), kind=kOutput, calls=%fused_computation.61 | convolution fusion | flops 673579008 | bytes 1968128 | tf_op jit(solution)/shard_map/dot_general | solution.py:69
  6.8 11.4 %all-to-all-start = ((bf16[32,32,640]{2,1,0:T(8,128)(2,1)}), bf16[32,32,640]{2,1,0:T(8,128)(2,1)S(1)}, u32[]{:S(2)}, u32[]{:S(2)}) async-start(bf16[32,32,640]{2,1,0:T(8,128)(2,1)} %bitcast.169), calls=%async_computation | async-start | bytes 2621440 | tf_op jit(solution)/shard_map/all_to_all | solution.py:127
  18.1 2.6 %copy.77 = bf16[512,1536]{0,1:T(8,128)(2,1)} copy(bf16[512,1536]{1,0:T(8,128)(2,1)} %param.12) | data formatting | bytes 3145728 | tf_op args[3]
  21.0 2.6 %fusion.124 = (bf16[512,1,16,32]{0,3,2,1:T(8,128)(2,1)}, bf16[512,1,16,32]{0,3,2,1:T(8,128)(2,1)}, bf16[512,1,16,32]{0,3,2,1:T(8,128)(2,1)}) fusion(bf16[512,3,16,32]{0,3,2,1:T(8,128)(2,1)} %bitcast.158), kind=kLoop, calls=%fused_computation.181 | loop fusion | bytes 3145728 | tf_op jit(solution)/shard_map/slice | solution.py:37
  23.6 28.5 %all-to-all-done = bf16[32,32,640]{2,1,0:T(8,128)(2,1)S(1)} async-done(((bf16[32,32,640]{2,1,0:T(8,128)(2,1)}), bf16[32,32,640]{2,1,0:T(8,128)(2,1)S(1)}, u32[]{:S(2)}, u32[]{:S(2)}) %all-to-all-start) | async-done | bytes 1310752 | tf_op jit(solution)/shard_map/all_to_all | solution.py:127
  52.5 1.3 convert_reduce_fusion.1
  54.4 0.9 fusion.119
  55.4 0.9 fusion.121
  56.4 0.9 fusion.117
  57.3 1.3 fusion.72
  58.6 3.6 %fusion.125 = (f32[16,8,128]{2,1,0:T(8,128)S(1)}, f32[16,8,128,128]{2,3,1,0:T(8,128)S(1)}) fusion(f32[16,8,128,128]{2,3,1,0:T(8,128)S(1)} %fusion.72, pred[8,128]{1,0:T(8,128)(4,1)S(1)} %iota_compare_fusion.20), kind=kOutput, calls=%fused_computation.182 | output fusion | flops 12583039 | bytes 16843776 | tf_op jit(solution)/shard_map/sub | solution.py:46
  62.3 1.2 fusion.52
  63.5 0.8 convert_reduce_fusion
  64.9 7.4 %fusion.33 = bf16[1024,512]{1,0:T(8,128)(2,1)} fusion(bf16[1024,512]{1,0:T(8,128)(2,1)S(1)} %get-tuple-element.25, bf16[2048,512]{1,0:T(8,128)(2,1)S(1)} %copy-done, bf16[512,2048]{1,0:T(8,128)(2,1)} %param.14, f32[1024]{0:T(1024)S(1)} %add_rsqrt_fusion.1, f32[1024]{0:T(1024)S(1)} %broadcast_multiply_fusion.1), kind=kOutput, calls=%fused_computation.46 | convolution fusion | flops 4317511680 | bytes 6299648 | tf_op jit(solution)/shard_map/dot_general | solution.py:64
  72.3 2.5 %copy.83 = bf16[8,16,8,512]{3,1,0,2:T(8,128)(2,1)} copy(bf16[8,16,8,512]{3,2,1,0:T(8,128)(2,1)} %bitcast.170) | data formatting | bytes 2097152 | tf_op jit(solution)/shard_map/reshape | solution.py:146
  74.8 4.3 %all-to-all-start.1 = ((bf16[8,16,8,512]{3,1,0,2:T(8,128)(2,1)}), bf16[8,16,8,512]{3,1,0,2:T(8,128)(2,1)S(1)}, u32[]{:S(2)}, u32[]{:S(2)}) async-start(bf16[8,16,8,512]{3,1,0,2:T(8,128)(2,1)} %copy.83), calls=%async_computation.1 | async-start | bytes 2097152 | tf_op jit(solution)/shard_map/all_to_all | solution.py:145
  79.1 2.6 %copy.87 = bf16[512,1536]{0,1:T(8,128)(2,1)} copy(bf16[512,1536]{1,0:T(8,128)(2,1)} %param.16) | data formatting | bytes 3145728 | tf_op args[7]
  82.2 2.3 %fusion.123 = (bf16[512,1,16,32]{0,3,2,1:T(8,128)(2,1)S(1)}, bf16[512,1,16,32]{0,3,2,1:T(8,128)(2,1)S(1)}, bf16[512,1,16,32]{0,3,2,1:T(8,128)(2,1)}) fusion(bf16[512,3,16,32]{0,3,2,1:T(8,128)(2,1)} %bitcast.159), kind=kLoop, calls=%fused_computation.180 | loop fusion | bytes 3145728 | tf_op jit(solution)/shard_map/slice | solution.py:37
  84.5 10.5 %all-to-all-done.1 = bf16[8,16,8,512]{3,1,0,2:T(8,128)(2,1)S(1)} async-done(((bf16[8,16,8,512]{3,1,0,2:T(8,128)(2,1)}), bf16[8,16,8,512]{3,1,0,2:T(8,128)(2,1)S(1)}, u32[]{:S(2)}, u32[]{:S(2)}) %all-to-all-start.1) | async-done | bytes 1048608 | tf_op jit(solution)/shard_map/all_to_all | solution.py:145
  96.2 0.7 fusion.127
  96.9 0.7 fusion.128
  97.7 0.7 fusion.129
  98.4 1.3 fusion.65
  99.8 3.5 %fusion.126 = (f32[16,8,128]{2,1,0:T(8,128)S(1)}, f32[16,8,128,128]{2,3,1,0:T(8,128)S(1)}) fusion(f32[16,8,128,128]{2,3,1,0:T(8,128)S(1)} %fusion.65, pred[8,128]{1,0:T(8,128)(4,1)S(1)} %broadcast_compare_fusion), kind=kOutput, calls=%fused_computation.183 | output fusion | flops 12583039 | bytes 16843776 | tf_op jit(solution)/shard_map/sub | solution.py:46
  103.2 1.2 fusion.53
  104.6 0.9 copy-done.8
  105.5 0.7 fusion.34
  106.8 18.4 %all_to_all.41 = bf16[8,128,1,512]{3,0,2,1:T(8,128)(2,1)S(1)} all-to-all(bf16[8,128,1,512]{3,0,2,1:T(8,128)(2,1)S(1)} %copy.93), channel_id=1, replica_groups=mesh['win'=32,'grp'=8] {'grp'}, dimensions={1} | all-to-all | bytes 2097152 | tf_op jit(solution)/shard_map/all_to_all | solution.py:164
  126.2 1.3 fusion.47
  127.5 33.5 %all_to_all.42 = bf16[32,32,512]{2,1,0:T(8,128)(2,1)S(1)} all-to-all(bf16[32,32,512]{2,1,0:T(8,128)(2,1)S(1)} %bitcast.174), channel_id=1, replica_groups=mesh['win'=32,'grp'=8] {'win'}, dimensions={0} | all-to-all | bytes 2097152 | tf_op jit(solution)/shard_map/all_to_all | solution.py:168
  161.0 1.6 fusion.55
  (54 shorter events, 7.9 us)
Async XLA Ops:
  0.0 64.9 %copy-start = (bf16[2048,512]{1,0:T(8,128)(2,1)S(1)}, bf16[2048,512]{1,0:T(8,128)(2,1)}, u32[]{:S(2)}) copy-start(bf16[2048,512]{1,0:T(8,128)(2,1)} %param.15) | copy-start | bytes 6291460
  6.8 45.3 %all-to-all-start = ((bf16[32,32,640]{2,1,0:T(8,128)(2,1)}), bf16[32,32,640]{2,1,0:T(8,128)(2,1)S(1)}, u32[]{:S(2)}, u32[]{:S(2)}) async-start(bf16[32,32,640]{2,1,0:T(8,128)(2,1)} %bitcast.169), calls=%async_computation | async-start | bytes 2621440 | tf_op jit(solution)/shard_map/all_to_all | solution.py:127
  18.1 2.6 %copy-start.6 = (s32[8,32,8]{1,2,0:T(8,128)S(1)}, s32[8,32,8]{1,2,0:T(8,128)}, u32[]{:S(2)}) copy-start(s32[8,32,8]{1,2,0:T(8,128)} %param.11) | copy-start | bytes 24580
  52.5 1.9 %copy-start.5 = (bf16[512,1,16,32]{0,3,2,1:T(8,128)(2,1)S(1)}, bf16[512,1,16,32]{0,3,2,1:T(8,128)(2,1)}, u32[]{:S(2)}) copy-start(bf16[512,1,16,32]{0,3,2,1:T(8,128)(2,1)} %get-tuple-element.9) | copy-start | bytes 1572868
  54.4 1.0 copy-start.4
  55.3 1.1 copy-start.3
  62.3 1.2 copy-start.7
  74.8 20.2 %all-to-all-start.1 = ((bf16[8,16,8,512]{3,1,0,2:T(8,128)(2,1)}), bf16[8,16,8,512]{3,1,0,2:T(8,128)(2,1)S(1)}, u32[]{:S(2)}, u32[]{:S(2)}) async-start(bf16[8,16,8,512]{3,1,0,2:T(8,128)(2,1)} %copy.83), calls=%async_computation.1 | async-start | bytes 2097152 | tf_op jit(solution)/shard_map/all_to_all | solution.py:145
  95.0 1.2 copy-start.2
  104.4 1.1 copy-start.8
  127.5 35.1 %copy-start.1 = (bf16[2048,512]{1,0:T(8,128)(2,1)S(1)}, bf16[2048,512]{1,0:T(8,128)(2,1)}, u32[]{:S(2)}) copy-start(bf16[2048,512]{1,0:T(8,128)(2,1)} %param.15) | copy-start | bytes 6291460

commit v12 on v10

--- a/solution.py
+++ b/solution.py
@@ -100,7 +100,7 @@
     peer_order = jnp.sum(choose * (running.astype(jnp.int32) - 1), axis=1)
     send_place = owner_dev * capacity + peer_order
     buffer_ids = jnp.arange(buffer_rows, dtype=jnp.int32)
-    send_hot = (buffer_ids[:, None] == send_place[None, :]).astype(jnp.bfloat16)
+    send_hot = (send_place[:, None] == buffer_ids[None, :]).astype(jnp.bfloat16)
 
     window_ends = jnp.cumsum(column_counts, axis=1)
     starts = window_ends - column_counts
@@ -123,7 +123,7 @@
         (slot_code // SLOT_BASE)[:, None],
         jnp.where(tail_ids[None, :] == 1, (slot_code % SLOT_BASE)[:, None], 0),
     ).astype(jnp.bfloat16)
-    outgoing = place(send_hot, jnp.concatenate([rows_x, code_cols], axis=1))
+    outgoing = place_back(send_hot, jnp.concatenate([rows_x, code_cols], axis=1))
     receiving = lax.all_to_all(
         outgoing.reshape(owner_count, capacity, model_dim + TAIL),
         "win",
@@ -166,7 +166,7 @@
     )
     returning = place_back(recv_hot, second_pad)
     returned = lax.all_to_all(returning, "win", split_axis=0, concat_axis=0, tiled=True)
-    encoded = place_back(send_hot, returned)
+    encoded = place(send_hot, returned)
     return encoded.reshape(1, 1, local_points, model_dim)
 
 

time: 163 us -> 163 us (level)
    dot_general x2, matrix products: 2.85 us -> 4.53 us  [place_back(): lax.dot_general(onehot, rows, (((0,), (0,)), ((), ())), preferred_element...]
where the time goes in v12:
time: 163 us
  blocking collectives  51.9 us (32%)
  waiting for transfers between devices  39 us (24%)
  matrix products  26.8 us (16%)
  local copies, waits for them, and re-layouts  16.8 us (10%)
  starting transfers between devices  15.7 us (10%)
  other arithmetic  12.2 us (7%)
    all_to_all x1, blocking collectives, on_device(): lax.all_to_all(returning, 'win', split_axis=0, concat_axis=0, tiled=True)  33.5 us
    all_to_all x1, waiting for transfers between devices, on_device(): lax.all_to_all(outgoing.reshape(owner_count, capacity, model_dim + TAIL),...  28.5 us
    all_to_all x1, blocking collectives, on_device(): lax.all_to_all(mixed_rows, 'grp', split_axis=1, concat_axis=2, tiled=True)  18.4 us
    all_to_all x1, starting transfers between devices, on_device(): lax.all_to_all(outgoing.reshape(owner_count, capacity, model_dim + TAIL),...  11.4 us
    all_to_all x1, waiting for transfers between devices, on_device(): lax.all_to_all(first_pad.reshape(blocks, dilation_stride, group_count, mo...  10.5 us
    dot_general x1, matrix products, feed_forward(): jnp.dot(hidden, w_down, preferred_element_type=jnp.float32)  7.41 us
    sub x2, other arithmetic, attention_block(): weights = jnp.exp(scores - row_max)  7.12 us
    unnamed x20, local copies, waits for them, and re-layouts  6.35 us
  transfers between devices with their start and end apart: 2, of which 2 were waited for; matrix products, arithmetic and copies ran while one was open for 7% of the time, Pallas kernels for 0%

profile of v12, /device:TPU:32, one launch (start us, length us, event | category | flops | bytes accessed | tf_op | source)
XLA Modules:
  0.0 162.6 jit_solution(13285460866174162938)
XLA Ops:
  0.0 0.8 dynamic-slice_bitcast_fusion
  3.7 3.2 %fusion.45 = bf16[1024,640]{1,0:T(8,128)(2,1)} fusion(s32[512]{0:T(512)S(1)} %multiply_add_fusion, bf16[512,128]{1,0:T(8,128)(2,1)S(1)} %select_convert_fusion, bf16[512,512]{1,0:T(8,128)(2,1)} %bitcast.182), kind=kOutput, calls=%fused_computation.61 | convolution fusion | flops 673579008 | bytes 1968128 | tf_op jit(solution)/shard_map/dot_general | solution.py:73
  6.9 11.4 %all-to-all-start = ((bf16[32,32,640]{2,1,0:T(8,128)(2,1)}), bf16[32,32,640]{2,1,0:T(8,128)(2,1)S(1)}, u32[]{:S(2)}, u32[]{:S(2)}) async-start(bf16[32,32,640]{2,1,0:T(8,128)(2,1)} %bitcast.169), calls=%async_computation | async-start | bytes 2621440 | tf_op jit(solution)/shard_map/all_to_all | solution.py:127
  18.3 2.6 %copy.77 = bf16[512,1536]{0,1:T(8,128)(2,1)} copy(bf16[512,1536]{1,0:T(8,128)(2,1)} %param.12) | data formatting | bytes 3145728 | tf_op args[3]
  21.1 2.6 %fusion.130 = (bf16[512,1,16,32]{0,3,2,1:T(8,128)(2,1)}, bf16[512,1,16,32]{0,3,2,1:T(8,128)(2,1)}, bf16[512,1,16,32]{0,3,2,1:T(8,128)(2,1)}) fusion(bf16[512,3,16,32]{0,3,2,1:T(8,128)(2,1)} %bitcast.158), kind=kLoop, calls=%fused_computation.201 | loop fusion | bytes 3145728 | tf_op jit(solution)/shard_map/slice | solution.py:37
  23.7 28.5 %all-to-all-done = bf16[32,32,640]{2,1,0:T(8,128)(2,1)S(1)} async-done(((bf16[32,32,640]{2,1,0:T(8,128)(2,1)}), bf16[32,32,640]{2,1,0:T(8,128)(2,1)S(1)}, u32[]{:S(2)}, u32[]{:S(2)}) %all-to-all-start) | async-done | bytes 1310752 | tf_op jit(solution)/shard_map/all_to_all | solution.py:127
  52.6 1.3 convert_reduce_fusion.1
  54.5 0.9 fusion.125
  55.5 0.9 fusion.127
  56.5 0.9 fusion.123
  57.4 1.3 fusion.72
  58.7 3.6 %fusion.131 = (f32[16,8,128]{2,1,0:T(8,128)S(1)}, f32[16,8,128,128]{2,3,1,0:T(8,128)S(1)}) fusion(f32[16,8,128,128]{2,3,1,0:T(8,128)S(1)} %fusion.72, pred[8,128]{1,0:T(8,128)(4,1)S(1)} %iota_compare_fusion.20), kind=kOutput, calls=%fused_computation.202 | output fusion | flops 12583039 | bytes 16843776 | tf_op jit(solution)/shard_map/sub | solution.py:46
  62.4 1.2 fusion.52
  63.6 0.8 convert_reduce_fusion
  65.0 7.4 %fusion.33 = bf16[1024,512]{1,0:T(8,128)(2,1)} fusion(bf16[1024,512]{1,0:T(8,128)(2,1)S(1)} %get-tuple-element.24, bf16[2048,512]{1,0:T(8,128)(2,1)S(1)} %copy-done, bf16[512,2048]{1,0:T(8,128)(2,1)} %param.14, f32[1024]{0:T(1024)S(1)} %add_rsqrt_fusion.1, f32[1024]{0:T(1024)S(1)} %broadcast_multiply_fusion.1), kind=kOutput, calls=%fused_computation.46 | convolution fusion | flops 4317511680 | bytes 6299648 | tf_op jit(solution)/shard_map/dot_general | solution.py:64
  72.4 2.5 %copy.83 = bf16[8,16,8,512]{3,1,0,2:T(8,128)(2,1)} copy(bf16[8,16,8,512]{3,2,1,0:T(8,128)(2,1)} %bitcast.170) | data formatting | bytes 2097152 | tf_op jit(solution)/shard_map/reshape | solution.py:146
  74.9 4.3 %all-to-all-start.1 = ((bf16[8,16,8,512]{3,1,0,2:T(8,128)(2,1)}), bf16[8,16,8,512]{3,1,0,2:T(8,128)(2,1)S(1)}, u32[]{:S(2)}, u32[]{:S(2)}) async-start(bf16[8,16,8,512]{3,1,0,2:T(8,128)(2,1)} %copy.83), calls=%async_computation.1 | async-start | bytes 2097152 | tf_op jit(solution)/shard_map/all_to_all | solution.py:145
  79.2 2.6 %copy.87 = bf16[512,1536]{0,1:T(8,128)(2,1)} copy(bf16[512,1536]{1,0:T(8,128)(2,1)} %param.16) | data formatting | bytes 3145728 | tf_op args[7]
  82.3 2.3 %fusion.129 = (bf16[512,1,16,32]{0,3,2,1:T(8,128)(2,1)S(1)}, bf16[512,1,16,32]{0,3,2,1:T(8,128)(2,1)S(1)}, bf16[512,1,16,32]{0,3,2,1:T(8,128)(2,1)}) fusion(bf16[512,3,16,32]{0,3,2,1:T(8,128)(2,1)} %bitcast.159), kind=kLoop, calls=%fused_computation.200 | loop fusion | bytes 3145728 | tf_op jit(solution)/shard_map/slice | solution.py:37
  84.6 10.5 %all-to-all-done.1 = bf16[8,16,8,512]{3,1,0,2:T(8,128)(2,1)S(1)} async-done(((bf16[8,16,8,512]{3,1,0,2:T(8,128)(2,1)}), bf16[8,16,8,512]{3,1,0,2:T(8,128)(2,1)S(1)}, u32[]{:S(2)}, u32[]{:S(2)}) %all-to-all-start.1) | async-done | bytes 1048608 | tf_op jit(solution)/shard_map/all_to_all | solution.py:145
  96.3 0.7 fusion.133
  97.1 0.7 fusion.134
  97.8 0.7 fusion.135
  98.6 1.3 fusion.65
  99.9 3.5 %fusion.132 = (f32[16,8,128]{2,1,0:T(8,128)S(1)}, f32[16,8,128,128]{2,3,1,0:T(8,128)S(1)}) fusion(f32[16,8,128,128]{2,3,1,0:T(8,128)S(1)} %fusion.65, pred[8,128]{1,0:T(8,128)(4,1)S(1)} %broadcast_compare_fusion), kind=kOutput, calls=%fused_computation.203 | output fusion | flops 12583039 | bytes 16843776 | tf_op jit(solution)/shard_map/sub | solution.py:46
  103.3 1.2 fusion.53
  104.7 0.9 copy-done.8
  105.6 0.7 fusion.34
  107.0 18.4 %all_to_all.41 = bf16[8,128,1,512]{3,0,2,1:T(8,128)(2,1)S(1)} all-to-all(bf16[8,128,1,512]{3,0,2,1:T(8,128)(2,1)S(1)} %copy.93), channel_id=1, replica_groups=mesh['win'=32,'grp'=8] {'grp'}, dimensions={1} | all-to-all | bytes 2097152 | tf_op jit(solution)/shard_map/all_to_all | solution.py:164
  126.3 1.3 fusion.47
  127.6 33.5 %all_to_all.42 = bf16[32,32,512]{2,1,0:T(8,128)(2,1)S(1)} all-to-all(bf16[32,32,512]{2,1,0:T(8,128)(2,1)S(1)} %bitcast.174), channel_id=1, replica_groups=mesh['win'=32,'grp'=8] {'win'}, dimensions={0} | all-to-all | bytes 2097152 | tf_op jit(solution)/shard_map/all_to_all | solution.py:168
  161.1 1.5 fusion.55
  (55 shorter events, 7.9 us)
Async XLA Ops:
  0.0 65.0 %copy-start = (bf16[2048,512]{1,0:T(8,128)(2,1)S(1)}, bf16[2048,512]{1,0:T(8,128)(2,1)}, u32[]{:S(2)}) copy-start(bf16[2048,512]{1,0:T(8,128)(2,1)} %param.15) | copy-start | bytes 6291460
  6.9 45.3 %all-to-all-start = ((bf16[32,32,640]{2,1,0:T(8,128)(2,1)}), bf16[32,32,640]{2,1,0:T(8,128)(2,1)S(1)}, u32[]{:S(2)}, u32[]{:S(2)}) async-start(bf16[32,32,640]{2,1,0:T(8,128)(2,1)} %bitcast.169), calls=%async_computation | async-start | bytes 2621440 | tf_op jit(solution)/shard_map/all_to_all | solution.py:127
  18.2 2.6 %copy-start.6 = (s32[8,32,8]{1,2,0:T(8,128)S(1)}, s32[8,32,8]{1,2,0:T(8,128)}, u32[]{:S(2)}) copy-start(s32[8,32,8]{1,2,0:T(8,128)} %param.11) | copy-start | bytes 24580
  52.6 1.9 %copy-start.5 = (bf16[512,1,16,32]{0,3,2,1:T(8,128)(2,1)S(1)}, bf16[512,1,16,32]{0,3,2,1:T(8,128)(2,1)}, u32[]{:S(2)}) copy-start(bf16[512,1,16,32]{0,3,2,1:T(8,128)(2,1)} %get-tuple-element.9) | copy-start | bytes 1572868
  54.5 1.0 copy-start.4
  55.4 1.1 copy-start.3
  62.4 1.2 copy-start.7
  74.9 20.2 %all-to-all-start.1 = ((bf16[8,16,8,512]{3,1,0,2:T(8,128)(2,1)}), bf16[8,16,8,512]{3,1,0,2:T(8,128)(2,1)S(1)}, u32[]{:S(2)}, u32[]{:S(2)}) async-start(bf16[8,16,8,512]{3,1,0,2:T(8,128)(2,1)} %copy.83), calls=%async_computation.1 | async-start | bytes 2097152 | tf_op jit(solution)/shard_map/all_to_all | solution.py:145
  95.2 1.2 copy-start.2
  104.6 1.1 copy-start.8
  127.6 35.1 %copy-start.1 = (bf16[2048,512]{1,0:T(8,128)(2,1)S(1)}, bf16[2048,512]{1,0:T(8,128)(2,1)}, u32[]{:S(2)}) copy-start(bf16[2048,512]{1,0:T(8,128)(2,1)} %param.15) | copy-start | bytes 6291460
